TPU v7x, 32 devices: a whole 2x2x4 slice. The times are simulated.
32 devices in a mesh: row: 4 (over y, core), col: 8 (over z, x).
Axes of the slice: x: 2, y: 2, z: 4, core: 2. Of those that a mesh axis runs over, the one named last changes fastest.
Arguments:
- doc_embed: bfloat16 [4096, 768], P(('row', 'col')), may hold values from -6 to 6
- pair_doc: int32 [32768], P(('row', 'col')), may hold values from 0 to 127
- pair_owner: int32 [32768, 1], P(('row', 'col')), may hold values from 0 to 31; in each aligned block of 1024 rows (0 to 1023, 1024 to 2047, ...) at most 64 rows name the same one
- pair_slot: int32 [32768], P(('row', 'col')), may hold values from 0 to 95
- label_cluster: int32 [3072], P(('row', 'col')), may hold values from 0 to 255, as said below
Outputs:
- label_vectors: bfloat16 [3072, 768], P(('row', 'col'))
- centroids: bfloat16 [256, 768], replicated
- distances: float32 [3072, 256], P(('row', 'col'))
Inputs may be any that keep to these rules, and one draw needn't show every extreme that they name: `pair_owner`: among the pairs of one device, at most 64 have one owner, and some owner has exactly 64. `label_cluster`: every cluster holds exactly 12 labels.
All inputs are finite; a program needn't handle non-finite values.
Results may differ from a plain program's by a relative error of at most 0.0049.
Values may be sent and summed in bfloat16 or wider, within the bound.
No kernel may reach another device: no remote copies, remote signals or barrier semaphores. Data moves between devices by JAX's collectives and lax.ppermute only.
A program may use at most 64 MiB of HBM per device.

v0:
```python
import jax
import jax.numpy as jnp
from jax import lax
from jax.sharding import PartitionSpec as P

CLUSTERS = 256


def rms_scale(values):
    return values * lax.rsqrt(jnp.mean(values * values, axis=-1, keepdims=True) + 1e-06)


def local(doc_embed, pair_doc, pair_owner, pair_slot, label_cluster):
    devices = lax.axis_size(("row", "col"))
    pairs = pair_doc.shape[0]
    width = doc_embed.shape[1]
    owned = label_cluster.shape[0]
    capacity = 2 * pairs // devices
    owner = pair_owner[:, 0]
    owner_hits = (owner[:, None] == jnp.arange(devices, dtype=jnp.int32)[None, :]).astype(jnp.int32)
    before = jnp.cumsum(owner_hits, axis=0) - owner_hits
    rank = jnp.sum(before * owner_hits, axis=1)
    position = owner * capacity + rank
    send_rows = (
        jnp.zeros((devices * capacity, width), jnp.bfloat16).at[position].set(doc_embed[pair_doc])
    )
    send_slot = jnp.full((devices * capacity,), owned, jnp.int32).at[position].set(pair_slot)
    got_rows, got_slot = (
        lax.all_to_all(
            send_rows.reshape(devices, capacity, width),
            ("row", "col"),
            split_axis=0,
            concat_axis=0,
            tiled=True,
        ),
        lax.all_to_all(
            send_slot.reshape(devices, capacity),
            ("row", "col"),
            split_axis=0,
            concat_axis=0,
            tiled=True,
        ),
    )
    groups = 8
    block_rows = got_rows.reshape(groups, -1, width)
    block_slot = got_slot.reshape(groups, -1)
    label_ids = jnp.arange(owned, dtype=jnp.int32)

    def add_group(total, inputs):
        rows_now, slot_now = inputs
        onehot = (label_ids[:, None] == slot_now[None, :]).astype(jnp.bfloat16)
        return (total + jnp.dot(onehot, rows_now, preferred_element_type=jnp.float32), None)

    label_sums, _ = lax.scan(
        add_group, jnp.zeros((owned, width), jnp.float32), (block_rows, block_slot)
    )
    label_vectors = rms_scale(label_sums).astype(jnp.bfloat16)
    members = (jnp.arange(CLUSTERS, dtype=jnp.int32)[:, None] == label_cluster[None, :]).astype(
        jnp.bfloat16
    )
    partial_sums = jnp.dot(members, label_vectors, preferred_element_type=jnp.float32)
    cluster_sums = lax.psum(partial_sums, ("row", "col"))
    centroids = rms_scale(cluster_sums).astype(jnp.bfloat16)
    inner = lax.dot_general(
        label_vectors, centroids, (((1,), (1,)), ((), ())), preferred_element_type=jnp.float32
    )
    distances = 1.0 - inner / float(width)
    return (label_vectors, centroids, distances)


def solution(mesh):
    placed = (
        P(("row", "col"), None),
        P(("row", "col")),
        P(("row", "col"), None),
        P(("row", "col")),
        P(("row", "col")),
    )
    return jax.shard_map(
        local,
        mesh=mesh,
        in_specs=placed,
        out_specs=(P(("row", "col"), None), P(), P(("row", "col"), None)),
        check_vma=False,
    )
```

profile of v0, /device:TPU:0, one launch (start us, length us, event | category | flops | bytes accessed | tf_op | source)
XLA Modules:
  0.0 274.0 jit_solution(7812681545642322157)
XLA Ops:
  7.2 0.0 copy-start
  7.2 0.7 fusion.13
  7.9 9.0 %reduce-window.6 = s32[32,8,128]{2,1,0:T(8,128)S(1)} reduce-window(s32[32,8,128]{2,1,0:T(8,128)S(1)} %fusion.13, s32[]{:T(128)} %constant.8.clone.1), window={size=1x1x128 pad=0_0x0_0x127_0}, to_apply=%region_0.0 | reduce-window | flops 4161536 | bytes 262148 | tf_op jit(solution)/shard_map/reduce-window
  16.9 0.1 slice.10
  17.0 0.1 copy.10
  17.2 0.1 copy.11
  17.3 0.1 broadcast_add_fusion
  17.4 0.7 fusion.12
  18.1 0.7 compare_select_fusion
  18.8 4.5 %scatter_custom_fusion = s32[2048]{0:T(1024)S(1)} fusion(s32[1024]{0:T(1024)S(1)} %bitcast.41, s32[1024]{0:T(1024)} %param.10, s32[]{:T(128)} %constant.14.clone.1), kind=kCustom, calls=%fused_computation.34 | custom fusion | bytes 8704 | tf_op jit(solution)/shard_map/scatter | solution.py:27
  23.3 0.7 all_to_all.9
  24.0 7.3 %all-to-all-start = ((s32[32,1,64]{2,1,0:T(1,128)}), s32[32,1,64]{2,1,0:T(1,128)S(1)}, u32[]{:S(2)}, u32[]{:S(2)}) async-start(s32[32,1,64]{2,1,0:T(1,128)} %all_to_all.9), calls=%async_computation | async-start | bytes 32768 | tf_op jit(solution)/shard_map/all_to_all | solution.py:36
  31.3 0.7 fusion.16
  32.0 0.0 copy-done
  32.0 13.5 %scatter_custom_fusion.1 = bf16[2048,768]{1,0:T(8,128)(2,1)} fusion(s32[1024]{0:T(1024)S(1)} %bitcast.42, bf16[128,768]{1,0:T(8,128)(2,1)S(1)} %copy-done, s32[1024]{0:T(1024)S(1)} %fusion.16, bf16[]{:T(256)} %constant.18.clone.1), kind=kCustom, calls=%fused_computation.11 | custom fusion | bytes 3145730 | tf_op jit(solution)/shard_map/scatter | solution.py:25
  45.6 0.0 all-to-all-done
  45.6 5.9 %all-to-all-start.1 = ((bf16[32,64,768]{2,1,0:T(8,128)(2,1)}), bf16[32,64,768]{2,1,0:T(8,128)(2,1)}, u32[]{:S(2)}, u32[]{:S(2)}) async-start(bf16[32,64,768]{2,1,0:T(8,128)(2,1)} %bitcast.6), calls=%async_computation.1 | async-start | bytes 6291456 | tf_op jit(solution)/shard_map/all_to_all | solution.py:29
  51.5 0.0 copy-start.3
  51.5 0.0 all-reduce.2.cloned.1.call-start
  51.6 0.5 broadcast.73
  52.1 0.7 reduce.3
  52.8 0.1 reshape.56
  52.9 71.2 %all-to-all-done.1 = bf16[32,64,768]{2,1,0:T(8,128)(2,1)} async-done(((bf16[32,64,768]{2,1,0:T(8,128)(2,1)}), bf16[32,64,768]{2,1,0:T(8,128)(2,1)}, u32[]{:S(2)}, u32[]{:S(2)}) %all-to-all-start.1) | async-done | bytes 3145760 | tf_op jit(solution)/shard_map/all_to_all | solution.py:29
  124.0 10.1 %while.11 = (s32[]{:T(128)}, f32[96,768]{1,0:T(8,128)S(1)}, s32[8,256]{1,0:T(8,128)S(1)}, bf16[8,256,768]{2,1,0:T(8,128)(2,1)}, s32[]{:T(128)}, /*index=5*/s32[]{:T(128)}) while((s32[]{:T(128)}, f32[96,768]{1,0:T(8,128)S(1)}, s32[8,256]{1,0:T(8,128)S(1)}, bf16[8,256,768]{2,1,0:T(8,128)(2,1)}, s32[]{:T(128)}, ...), condition=%wide.region_6.7_spmd.clone, body=%wide.region_5.6_spmd.clone.sunk | while | flops 37920768 | bytes 986707 | solution.py:54
  124.1 1.2 convolution_add_fusion.2
  125.3 1.2 convolution_add_fusion.2
  126.6 1.2 convolution_add_fusion.2
  127.8 1.2 convolution_add_fusion.2
  129.1 1.2 convolution_add_fusion.2
  130.4 1.2 convolution_add_fusion.2
  131.6 1.2 convolution_add_fusion.2
  132.9 1.2 convolution_add_fusion.2
  134.1 0.1 multiply_reduce_fusion.1
  134.2 0.1 multiply_convert_fusion.1
  134.3 0.0 copy-done.3
  134.4 0.0 copy-start.2
  134.4 1.1 fusion.14
  135.5 0.0 all-reduce.2.cloned.1.call-update
  135.5 128.1 %all-reduce.2.cloned.1.call-done = f32[256,768]{1,0:T(8,128)} async-done(((f32[256,768]{1,0:T(8,128)}), f32[256,768]{1,0:T(8,128)}) %all-reduce.2.cloned.1.call-update) | async-done | bytes 786448 | tf_op jit(solution)/shard_map/psum | solution.py:62
  263.7 1.3 multiply_reduce_fusion
  264.9 1.2 multiply_convert_fusion
  266.2 0.0 copy-start.1
  266.2 0.9 fusion.9
  267.1 0.0 copy-done.2
  267.1 0.0 copy-done.1
  (13 shorter events, 0.1 us)
Async XLA Ops:
  7.2 24.9 %copy-start = (bf16[128,768]{1,0:T(8,128)(2,1)S(1)}, bf16[128,768]{1,0:T(8,128)(2,1)}, u32[]{:S(2)}) copy-start(bf16[128,768]{1,0:T(8,128)(2,1)} %param.7) | copy-start | bytes 589828
  24.0 21.6 %all-to-all-start = ((s32[32,1,64]{2,1,0:T(1,128)}), s32[32,1,64]{2,1,0:T(1,128)S(1)}, u32[]{:S(2)}, u32[]{:S(2)}) async-start(s32[32,1,64]{2,1,0:T(1,128)} %all_to_all.9), calls=%async_computation | async-start | bytes 32768 | tf_op jit(solution)/shard_map/all_to_all | solution.py:36
  45.6 78.5 %all-to-all-start.1 = ((bf16[32,64,768]{2,1,0:T(8,128)(2,1)}), bf16[32,64,768]{2,1,0:T(8,128)(2,1)}, u32[]{:S(2)}, u32[]{:S(2)}) async-start(bf16[32,64,768]{2,1,0:T(8,128)(2,1)} %bitcast.6), calls=%async_computation.1 | async-start | bytes 6291456 | tf_op jit(solution)/shard_map/all_to_all | solution.py:29
  51.5 82.8 %copy-start.3 = (s32[96]{0:T(128)S(1)}, s32[96]{0:T(128)}, u32[]{:S(2)}) copy-start(s32[96]{0:T(128)} %param.11) | copy-start | bytes 1156
  51.5 212.1 %all-reduce.2.cloned.1.call-start = ((), (), s32[]{:S(2)}) async-start(), calls=%async_computation.2 | async-start | bytes 1572864 | tf_op jit(solution)/shard_map/psum | solution.py:62
  134.4 132.7 %copy-start.2 = (bf16[96,768]{1,0:T(8,128)(2,1)}, bf16[96,768]{1,0:T(8,128)(2,1)S(1)}, u32[]{:S(2)}) copy-start(bf16[96,768]{1,0:T(8,128)(2,1)S(1)} %multiply_convert_fusion.1) | copy-start | bytes 442372
  266.2 0.9 copy-start.1
Sparse Core Ops, SparseCore 0:
  135.7 127.9 all-reduce.1
where the time goes:
time: 275 us; the launch traced here: 274 us
  waiting for transfers between devices  199 us (72%)
  local copies, waits for them, and re-layouts  19.7 us (7%)
  other arithmetic  15.4 us (6%)
  between operations  14.2 us (5%)
  starting transfers between devices  13.3 us (5%)
  matrix products  11.8 us (4%)
    psum x1, waiting for transfers between devices, local(): cluster_sums = lax.psum(partial_sums, ('row', 'col'))  128 us
    all_to_all x1, waiting for transfers between devices, local(): lax.all_to_all(send_rows.reshape(devices, capacity, width), ('row', 'col'...  71.2 us
    scatter x1, local copies, waits for them, and re-layouts, local(): jnp.zeros((devices * capacity, width), jnp.bfloat16).at[position]  13.5 us
    dot_general x8, matrix products, add_group(): jnp.dot(onehot, rows_now, preferred_element_type=jnp.float32)  9.76 us
    another operation x3, other arithmetic  9.15 us
    all_to_all x1, starting transfers between devices, local(): lax.all_to_all(send_slot.reshape(devices, capacity), ('row', 'col'), spli...  7.33 us
    all_to_all x1, starting transfers between devices, local(): lax.all_to_all(send_rows.reshape(devices, capacity, width), ('row', 'col'...  5.95 us
  transfers between devices with their start and end apart: 3, of which 2 were waited for; matrix products, arithmetic and copies ran while one was open for 6% of the time, Pallas kernels for 0%

commit v1 on v0

v1 whole, which is shorter than its diff:
```python
import jax
import jax.numpy as jnp
from jax import lax
from jax.sharding import PartitionSpec as P

CLUSTERS = 256


def rms_scale(values):
    return values * lax.rsqrt(jnp.mean(values * values, axis=-1, keepdims=True) + 1e-06)


def local(doc_embed, pair_doc, pair_owner, pair_slot, label_cluster):
    axes = ("row", "col")
    devices = lax.axis_size(axes)
    pairs = pair_doc.shape[0]
    docs, width = doc_embed.shape
    owned = label_cluster.shape[0]
    capacity = 2 * pairs // devices
    owner = pair_owner[:, 0]
    f32, bf16 = jnp.float32, jnp.bfloat16

    owner_hits = (owner[:, None] == jnp.arange(devices, dtype=jnp.int32)[None, :]).astype(bf16)
    pid = jnp.arange(pairs, dtype=jnp.int32)
    earlier = (pid[None, :] < pid[:, None]).astype(bf16)
    before = jnp.dot(earlier, owner_hits, preferred_element_type=f32)
    rank = jnp.sum(before * owner_hits.astype(f32), axis=1).astype(jnp.int32)
    position = owner * capacity + rank

    place = (jnp.arange(devices * capacity, dtype=jnp.int32)[:, None] == position[None, :]).astype(bf16)
    doc_hits = (pair_doc[:, None] == jnp.arange(docs, dtype=jnp.int32)[None, :]).astype(bf16)
    pick = jnp.dot(place, doc_hits, preferred_element_type=f32).astype(bf16)
    send_rows = jnp.dot(pick, doc_embed, preferred_element_type=f32).astype(bf16)
    slot_plus = (pair_slot + 1).astype(bf16)[:, None]
    send_slot = jnp.dot(place, slot_plus, preferred_element_type=f32)[:, 0].astype(jnp.int32) - 1

    got_rows = lax.all_to_all(
        send_rows.reshape(devices, capacity, width), axes, split_axis=0, concat_axis=0, tiled=True
    ).reshape(devices * capacity, width)
    got_slot = lax.all_to_all(
        send_slot.reshape(devices, 1, capacity), axes, split_axis=0, concat_axis=0, tiled=True
    ).reshape(devices * capacity)

    label_ids = jnp.arange(owned, dtype=jnp.int32)
    onehot = (label_ids[:, None] == got_slot[None, :]).astype(bf16)
    label_sums = jnp.dot(onehot, got_rows, preferred_element_type=f32)
    label_vectors = rms_scale(label_sums).astype(bf16)
    members = (jnp.arange(CLUSTERS, dtype=jnp.int32)[:, None] == label_cluster[None, :]).astype(bf16)
    partial_sums = jnp.dot(members, label_vectors, preferred_element_type=f32)

    if CLUSTERS % devices == 0:
        share = CLUSTERS // devices
        parts = lax.all_to_all(
            partial_sums.reshape(devices, share, width), axes, split_axis=0, concat_axis=0, tiled=True
        )
        own = rms_scale(jnp.sum(parts, axis=0)).astype(bf16)
        centroids = lax.all_to_all(
            jnp.broadcast_to(own[None], (devices, share, width)),
            axes,
            split_axis=0,
            concat_axis=0,
            tiled=True,
        ).reshape(CLUSTERS, width)
    else:
        centroids = rms_scale(lax.psum(partial_sums, axes)).astype(bf16)
    inner = lax.dot_general(
        label_vectors, centroids, (((1,), (1,)), ((), ())), preferred_element_type=f32
    )
    distances = 1.0 - inner / float(width)
    return (label_vectors, centroids, distances)


def solution(mesh):
    placed = (
        P(("row", "col"), None),
        P(("row", "col")),
        P(("row", "col"), None),
        P(("row", "col")),
        P(("row", "col")),
    )
    return jax.shard_map(
        local,
        mesh=mesh,
        in_specs=placed,
        out_specs=(P(("row", "col"), None), P(), P(("row", "col"), None)),
        check_vma=False,
    )
```

time: 275 us -> 140 us (0.51)
  waiting for transfers between devices: 199 us -> 73.3 us
  blocking collectives: 0 us -> 39.9 us
  local copies, waits for them, and re-layouts: 19.7 us -> 2.09 us
  between operations: 14.2 us -> 0.75 us
  other arithmetic: 15.4 us -> 2.45 us
    psum x1 -> x0, waiting for transfers between devices: 128 us -> none  [local(): cluster_sums = lax.psum(partial_sums, ('row', 'col'))]
    all_to_all x0 -> x2, blocking collectives: none -> 39.9 us  [the longest x1 24.3 us: local(): lax.all_to_all(partial_sums.reshape(devices, share, width), axes, split_a...]
    scatter x2 -> x0, local copies, waits for them, and re-layouts: 18 us -> none  [the longest x1 13.5 us: local(): jnp.zeros((devices * capacity, width), jnp.bfloat16).at[position]]
    another operation x3 -> x0, other arithmetic: 9.15 us -> none
    dot_general x9 -> x5, matrix products: 10.9 us -> 8.76 us  [the longest x1 5.03 us: local(): jnp.dot(pick, doc_embed, preferred_element_type=f32).astype(bf16)]
  transfers between devices with their start and end apart: 3 -> 2, of which waited for: 2 -> 2; matrix products, arithmetic and copies ran while one was open for 6% -> 5% of each run, Pallas kernels for 0% -> 0%
where the time goes in v1:
time: 140 us; the launch traced here: 139 us
  waiting for transfers between devices  73.3 us (52%)
  blocking collectives  39.9 us (28%)
  starting transfers between devices  11.1 us (8%)
  matrix products  9.67 us (7%)
  other arithmetic  2.45 us (2%)
  local copies, waits for them, and re-layouts  2.09 us (1%)
    all_to_all x1, waiting for transfers between devices, local(): lax.all_to_all(send_rows.reshape(devices, capacity, width), axes, split_a...  71.2 us
    all_to_all x1, blocking collectives, local(): lax.all_to_all(partial_sums.reshape(devices, share, width), axes, split_a...  24.3 us
    all_to_all x1, blocking collectives, local(): lax.all_to_all(jnp.broadcast_to(own[None], (devices, share, width)), axes...  15.6 us
    all_to_all x1, starting transfers between devices, local(): lax.all_to_all(send_slot.reshape(devices, 1, capacity), axes, split_axis=...  7.32 us
    dot_general x1, matrix products, local(): jnp.dot(pick, doc_embed, preferred_element_type=f32).astype(bf16)  5.03 us
    all_to_all x1, starting transfers between devices, local(): lax.all_to_all(send_rows.reshape(devices, capacity, width), axes, split_a...  3.82 us
  transfers between devices with their start and end apart: 2, of which 2 were waited for; matrix products, arithmetic and copies ran while one was open for 5% of the time, Pallas kernels for 0%

profile of v1, /device:TPU:0, one launch (start us, length us, event | category | flops | bytes accessed | tf_op | source)
XLA Modules:
  0.0 139.3 jit_solution(16460837160433416571)
XLA Ops:
  0.6 0.0 copy-start
  0.6 0.0 copy-start.3
  0.7 1.3 fusion.8
  2.0 0.7 convert_add_fusion.1
  2.7 0.7 add_convert_fusion
  3.4 1.5 %fusion.1 = f32[1,2048]{1,0:T(1,128)S(1)} fusion(bf16[1024,1]{0,1:T(2,128)(2,1)S(1)} %reshape.87, s32[1024]{0:T(1024)S(1)} %convert_add_fusion.1), kind=kOutput, calls=%fused_computation.2 | convolution fusion | flops 6291456 | bytes 14336 | tf_op jit(solution)/shard_map/dot_general | solution.py:35
  4.8 0.7 sub.13
  5.5 7.3 %all-to-all-start = ((s32[32,1,64]{2,1,0:T(1,128)}), s32[32,1,64]{2,1,0:T(1,128)S(1)}, u32[]{:S(2)}, u32[]{:S(2)}) async-start(s32[32,1,64]{2,1,0:T(1,128)} %sub.13), calls=%async_computation | async-start | bytes 32768 | tf_op jit(solution)/shard_map/all_to_all | solution.py:40
  12.8 0.0 copy-done
  12.9 0.0 copy-done.3
  12.9 5.0 %convolution_convert_fusion = bf16[2048,768]{1,0:T(8,128)(2,1)} fusion(bf16[128,768]{1,0:T(8,128)(2,1)S(1)} %copy-done, s32[1024]{0:T(1024)S(1)} %convert_add_fusion.1, s32[1024]{0:T(1024)S(1)} %copy-done.3), kind=kOutput, calls=%fused_computation.7 | convolution fusion | flops 943587328 | bytes 3350528 | tf_op jit(solution)/shard_map/dot_general | solution.py:33
  17.9 2.0 %all-to-all-done = s32[32,1,64]{2,1,0:T(1,128)S(1)} async-done(((s32[32,1,64]{2,1,0:T(1,128)}), s32[32,1,64]{2,1,0:T(1,128)S(1)}, u32[]{:S(2)}, u32[]{:S(2)}) %all-to-all-start) | async-done | bytes 8224 | tf_op jit(solution)/shard_map/all_to_all | solution.py:40
  19.9 3.8 %all-to-all-start.1 = ((bf16[32,64,768]{2,1,0:T(8,128)(2,1)}), bf16[32,64,768]{2,1,0:T(8,128)(2,1)S(1)}, u32[]{:S(2)}, u32[]{:S(2)}) async-start(bf16[32,64,768]{2,1,0:T(8,128)(2,1)} %bitcast.16), calls=%async_computation.1 | async-start | bytes 6291456 | tf_op jit(solution)/shard_map/all_to_all | solution.py:37
  23.7 0.0 copy-start.2
  23.8 0.5 broadcast.63
  24.3 0.7 reduce.3
  25.0 0.1 eq.74
  25.0 71.2 %all-to-all-done.1 = bf16[32,64,768]{2,1,0:T(8,128)(2,1)S(1)} async-done(((bf16[32,64,768]{2,1,0:T(8,128)(2,1)}), bf16[32,64,768]{2,1,0:T(8,128)(2,1)S(1)}, u32[]{:S(2)}, u32[]{:S(2)}) %all-to-all-start.1) | async-done | bytes 3145760 | tf_op jit(solution)/shard_map/all_to_all | solution.py:37
  96.3 0.7 multiply_reduce_fusion
  97.0 0.1 multiply_convert_fusion
  97.1 0.0 copy-done.2
  97.1 0.0 copy-start.1
  97.1 0.2 convolution_bitcast_fusion
  97.4 24.3 %all_to_all.20 = f32[32,8,768]{2,1,0:T(8,128)S(1)} all-to-all(f32[32,8,768]{2,1,0:T(8,128)S(1)} %convolution_bitcast_fusion), channel_id=1, replica_groups=mesh['row'=4,'col'=8] {'row','col'}, dimensions={0} | all-to-all | bytes 1572864 | tf_op jit(solution)/shard_map/all_to_all | solution.py:53
  121.7 0.1 reduce_sum.38
  121.8 0.1 multiply_reduce_fusion.1
  121.9 0.1 multiply_convert_fusion.1
  122.0 15.6 %all_to_all.21 = bf16[32,8,768]{2,1,0:T(8,128)(2,1)S(1)} all-to-all(bf16[32,8,768]{2,1,0:T(8,128)(2,1)S(1)} %broadcast_in_dim.2), channel_id=1, replica_groups=mesh['row'=4,'col'=8] {'row','col'}, dimensions={0} | all-to-all | bytes 786432 | tf_op jit(solution)/shard_map/all_to_all | solution.py:57
  137.6 0.9 fusion.7
  138.5 0.7 copy.9
  139.3 0.0 copy-done.1
  (5 shorter events, 0.1 us)
Async XLA Ops:
  0.6 12.2 %copy-start = (bf16[128,768]{1,0:T(8,128)(2,1)S(1)}, bf16[128,768]{1,0:T(8,128)(2,1)}, u32[]{:S(2)}) copy-start(bf16[128,768]{1,0:T(8,128)(2,1)} %param.5) | copy-start | bytes 589828
  0.6 12.2 %copy-start.3 = (s32[1024]{0:T(1024)S(1)}, s32[1024]{0:T(1024)}, u32[]{:S(2)}) copy-start(s32[1024]{0:T(1024)} %param.6) | copy-start | bytes 12292
  5.5 14.4 %all-to-all-start = ((s32[32,1,64]{2,1,0:T(1,128)}), s32[32,1,64]{2,1,0:T(1,128)S(1)}, u32[]{:S(2)}, u32[]{:S(2)}) async-start(s32[32,1,64]{2,1,0:T(1,128)} %sub.13), calls=%async_computation | async-start | bytes 32768 | tf_op jit(solution)/shard_map/all_to_all | solution.py:40
  19.9 76.4 %all-to-all-start.1 = ((bf16[32,64,768]{2,1,0:T(8,128)(2,1)}), bf16[32,64,768]{2,1,0:T(8,128)(2,1)S(1)}, u32[]{:S(2)}, u32[]{:S(2)}) async-start(bf16[32,64,768]{2,1,0:T(8,128)(2,1)} %bitcast.16), calls=%async_computation.1 | async-start | bytes 6291456 | tf_op jit(solution)/shard_map/all_to_all | solution.py:37
  23.7 73.4 %copy-start.2 = (s32[96]{0:T(128)S(1)}, s32[96]{0:T(128)}, u32[]{:S(2)}) copy-start(s32[96]{0:T(128)} %param.9) | copy-start | bytes 1156
  97.1 42.2 %copy-start.1 = (bf16[96,768]{1,0:T(8,128)(2,1)}, bf16[96,768]{1,0:T(8,128)(2,1)S(1)}, u32[]{:S(2)}) copy-start(bf16[96,768]{1,0:T(8,128)(2,1)S(1)} %multiply_convert_fusion) | copy-start | bytes 442372

commit v2 on v1

--- a/solution.py
+++ b/solution.py
@@ -1,7 +1,7 @@
 import jax
 import jax.numpy as jnp
 from jax import lax
-from jax.sharding import PartitionSpec as P
+from jax.sharding import Mesh, PartitionSpec as P
 
 CLUSTERS = 256
 
@@ -11,7 +11,7 @@
 
 
 def local(doc_embed, pair_doc, pair_owner, pair_slot, label_cluster):
-    axes = ("row", "col")
+    axes = ("y", "core", "col")
     devices = lax.axis_size(axes)
     pairs = pair_doc.shape[0]
     docs, width = doc_embed.shape
@@ -28,11 +28,11 @@
     position = owner * capacity + rank
 
     place = (jnp.arange(devices * capacity, dtype=jnp.int32)[:, None] == position[None, :]).astype(bf16)
-    doc_hits = (pair_doc[:, None] == jnp.arange(docs, dtype=jnp.int32)[None, :]).astype(bf16)
-    pick = jnp.dot(place, doc_hits, preferred_element_type=f32).astype(bf16)
+    tags = jnp.stack([pair_doc + 1, pair_slot + 1], axis=1).astype(bf16)
+    picked = jnp.dot(place, tags, preferred_element_type=f32).astype(jnp.int32) - 1
+    send_doc, send_slot = picked[:, 0], picked[:, 1]
+    pick = (send_doc[:, None] == jnp.arange(docs, dtype=jnp.int32)[None, :]).astype(bf16)
     send_rows = jnp.dot(pick, doc_embed, preferred_element_type=f32).astype(bf16)
-    slot_plus = (pair_slot + 1).astype(bf16)[:, None]
-    send_slot = jnp.dot(place, slot_plus, preferred_element_type=f32)[:, 0].astype(jnp.int32) - 1
 
     got_rows = lax.all_to_all(
         send_rows.reshape(devices, capacity, width), axes, split_axis=0, concat_axis=0, tiled=True
@@ -50,13 +50,25 @@
 
     if CLUSTERS % devices == 0:
         share = CLUSTERS // devices
+        pair = lax.all_to_all(
+            partial_sums.reshape(2, CLUSTERS // 2, width), "core", split_axis=0, concat_axis=0, tiled=True
+        )
+        half = jnp.sum(pair, axis=0)
+        chips = ("y", "col")
         parts = lax.all_to_all(
-            partial_sums.reshape(devices, share, width), axes, split_axis=0, concat_axis=0, tiled=True
+            half.reshape(devices // 2, share, width), chips, split_axis=0, concat_axis=0, tiled=True
         )
         own = rms_scale(jnp.sum(parts, axis=0)).astype(bf16)
+        half_c = lax.all_to_all(
+            jnp.broadcast_to(own[None], (devices // 2, share, width)),
+            chips,
+            split_axis=0,
+            concat_axis=0,
+            tiled=True,
+        ).reshape(CLUSTERS // 2, width)
         centroids = lax.all_to_all(
-            jnp.broadcast_to(own[None], (devices, share, width)),
-            axes,
+            jnp.broadcast_to(half_c[None], (2, CLUSTERS // 2, width)),
+            "core",
             split_axis=0,
             concat_axis=0,
             tiled=True,
@@ -71,17 +83,14 @@
 
 
 def solution(mesh):
-    placed = (
-        P(("row", "col"), None),
-        P(("row", "col")),
-        P(("row", "col"), None),
-        P(("row", "col")),
-        P(("row", "col")),
-    )
+    rows, cols = mesh.shape["row"], mesh.shape["col"]
+    split = Mesh(mesh.devices.reshape(rows // 2, 2, cols), ("y", "core", "col"))
+    spread = ("y", "core", "col")
+    placed = (P(spread, None), P(spread), P(spread, None), P(spread), P(spread))
     return jax.shard_map(
         local,
-        mesh=mesh,
+        mesh=split,
         in_specs=placed,
-        out_specs=(P(("row", "col"), None), P(), P(("row", "col"), None)),
+        out_specs=(P(spread, None), P(), P(spread, None)),
         check_vma=False,
     )

time: 140 us -> 136 us (0.971)
  blocking collectives: 39.9 us -> 36.2 us
  waiting for transfers between devices: 73.3 us -> 75.9 us
  matrix products: 9.67 us -> 7.09 us
    all_to_all x2 -> x4, blocking collectives: 39.9 us -> 36.2 us  [the longest x1 16.5 us: local(): lax.all_to_all(half.reshape(devices // 2, share, width), chips, split_axi...]
    all_to_all x1, waiting for transfers between devices: 2.02 us -> 4.63 us  [local(): lax.all_to_all(send_slot.reshape(devices, 1, capacity), axes, split_axis=...]
    dot_general x1, matrix products: 5.03 us -> 2.43 us  [local(): jnp.dot(pick, doc_embed, preferred_element_type=f32).astype(bf16)]
    another operation x0 -> x2, other arithmetic: none -> 1.42 us
  transfers between devices with their start and end apart: 2 -> 2, of which waited for: 2 -> 2; matrix products, arithmetic and copies ran while one was open for 5% -> 3% of each run, Pallas kernels for 0% -> 0%
where the time goes in v2:
time: 136 us; the launch traced here: 135 us
  waiting for transfers between devices  75.9 us (56%)
  blocking collectives  36.2 us (27%)
  starting transfers between devices  10.1 us (7%)
  matrix products  7.09 us (5%)
  other arithmetic  3.19 us (2%)
  local copies, waits for them, and re-layouts  2.12 us (2%)
    all_to_all x1, waiting for transfers between devices, local(): lax.all_to_all(send_rows.reshape(devices, capacity, width), axes, split_a...  71.2 us
    all_to_all x1, blocking collectives, local(): lax.all_to_all(half.reshape(devices // 2, share, width), chips, split_axi...  16.5 us
    all_to_all x1, blocking collectives, local(): lax.all_to_all(jnp.broadcast_to(own[None], (devices // 2, share, width)),...  11.2 us
    all_to_all x1, starting transfers between devices, local(): lax.all_to_all(send_slot.reshape(devices, 1, capacity), axes, split_axis=...  7.32 us
    all_to_all x1, waiting for transfers between devices, local(): lax.all_to_all(send_slot.reshape(devices, 1, capacity), axes, split_axis=...  4.63 us
    all_to_all x1, blocking collectives, local(): lax.all_to_all(partial_sums.reshape(2, CLUSTERS // 2, width), 'core', spl...  4.37 us
    all_to_all x1, blocking collectives, local(): lax.all_to_all(jnp.broadcast_to(half_c[None], (2, CLUSTERS // 2, width)),...  4.05 us
    all_to_all x1, starting transfers between devices, local(): lax.all_to_all(send_rows.reshape(devices, capacity, width), axes, split_a...  2.78 us
  transfers between devices with their start and end apart: 2, of which 2 were waited for; matrix products, arithmetic and copies ran while one was open for 3% of the time, Pallas kernels for 0%

profile of v2, /device:TPU:0, one launch (start us, length us, event | category | flops | bytes accessed | tf_op | source)
XLA Modules:
  0.0 135.3 jit_solution(4349709021862722131)
XLA Ops:
  0.6 0.0 copy-start
  0.6 0.7 add_convert_fusion.1
  1.4 0.7 add_convert_fusion
  2.1 1.3 fusion.7
  3.4 0.7 convert_add_fusion
  4.1 1.5 %fusion.4 = s32[2048,2]{0,1:T(2,128)S(1)} fusion(s32[1024]{0:T(1024)S(1)} %convert_add_fusion, bf16[1024,1]{0,1:T(2,128)(2,1)S(1)} %stack.13, bf16[1024,1]{0,1:T(2,128)(2,1)S(1)} %stack.12), kind=kOutput, calls=%fused_computation.7 | convolution fusion | flops 10502144 | bytes 24576 | tf_op jit(solution)/shard_map/dot_general | solution.py:32
  5.6 0.7 reshape_squeeze.3
  6.3 7.3 %all-to-all-start = ((s32[32,1,64]{2,1,0:T(1,128)}), s32[32,1,64]{2,1,0:T(1,128)S(1)}, u32[]{:S(2)}, u32[]{:S(2)}) async-start(s32[32,1,64]{2,1,0:T(1,128)} %bitcast.1), calls=%async_computation | async-start | bytes 32768 | tf_op jit(solution)/shard_map/all_to_all | solution.py:40
  13.6 0.0 copy-done
  13.6 2.4 %convolution_convert_fusion = bf16[2048,768]{1,0:T(8,128)(2,1)} fusion(bf16[128,768]{1,0:T(8,128)(2,1)S(1)} %copy-done, s32[2048]{0:T(1024)S(1)} %bitcast.20), kind=kOutput, calls=%fused_computation.5 | convolution fusion | flops 404488192 | bytes 3350528 | tf_op jit(solution)/shard_map/dot_general | solution.py:35
  16.0 4.6 %all-to-all-done = s32[32,1,64]{2,1,0:T(1,128)S(1)} async-done(((s32[32,1,64]{2,1,0:T(1,128)}), s32[32,1,64]{2,1,0:T(1,128)S(1)}, u32[]{:S(2)}, u32[]{:S(2)}) %all-to-all-start) | async-done | bytes 8224 | tf_op jit(solution)/shard_map/all_to_all | solution.py:40
  20.7 2.8 %all-to-all-start.1 = ((bf16[32,64,768]{2,1,0:T(8,128)(2,1)}), bf16[32,64,768]{2,1,0:T(8,128)(2,1)S(1)}, u32[]{:S(2)}, u32[]{:S(2)}) async-start(bf16[32,64,768]{2,1,0:T(8,128)(2,1)} %bitcast.3), calls=%async_computation.1 | async-start | bytes 6291456 | tf_op jit(solution)/shard_map/all_to_all | solution.py:37
  23.5 0.0 copy-start.2
  23.5 0.5 broadcast.62
  24.0 0.7 reduce.7
  24.7 0.1 eq.76
  24.8 71.2 %all-to-all-done.1 = bf16[32,64,768]{2,1,0:T(8,128)(2,1)S(1)} async-done(((bf16[32,64,768]{2,1,0:T(8,128)(2,1)}), bf16[32,64,768]{2,1,0:T(8,128)(2,1)S(1)}, u32[]{:S(2)}, u32[]{:S(2)}) %all-to-all-start.1) | async-done | bytes 3145760 | tf_op jit(solution)/shard_map/all_to_all | solution.py:37
  96.0 0.7 multiply_reduce_fusion
  96.7 0.1 multiply_convert_fusion
  96.8 0.0 copy-done.2
  96.8 0.0 copy-start.1
  96.9 0.2 fusion.12
  97.1 4.4 %all_to_all.30 = f32[2,128,768]{2,1,0:T(8,128)S(1)} all-to-all(f32[2,128,768]{2,1,0:T(8,128)S(1)} %bitcast.17), channel_id=1, replica_groups=mesh['y'=2,'core'=2,'col'=8] {'core'}, dimensions={0} | all-to-all | bytes 1572864 | tf_op jit(solution)/shard_map/all_to_all | solution.py:53
  101.5 0.1 reduce_sum.47
  101.5 16.5 %all_to_all.31 = f32[16,8,768]{2,1,0:T(8,128)S(1)} all-to-all(f32[16,8,768]{2,1,0:T(8,128)S(1)} %bitcast.18), channel_id=1, replica_groups=mesh['y'=2,'core'=2,'col'=8] {'y','col'}, dimensions={0} | all-to-all | bytes 786432 | tf_op jit(solution)/shard_map/all_to_all | solution.py:58
  118.0 0.1 multiply_reduce_fusion.1
  118.2 0.1 multiply_convert_fusion.1
  118.3 11.2 %all_to_all.32 = bf16[16,8,768]{2,1,0:T(8,128)(2,1)S(1)} all-to-all(bf16[16,8,768]{2,1,0:T(8,128)(2,1)S(1)} %broadcast_in_dim.6), channel_id=1, replica_groups=mesh['y'=2,'core'=2,'col'=8] {'y','col'}, dimensions={0} | all-to-all | bytes 393216 | tf_op jit(solution)/shard_map/all_to_all | solution.py:62
  129.6 4.0 %all_to_all.33 = bf16[2,128,768]{2,1,0:T(8,128)(2,1)S(1)} all-to-all(bf16[2,128,768]{2,1,0:T(8,128)(2,1)S(1)} %broadcast_in_dim.8), channel_id=1, replica_groups=mesh['y'=2,'core'=2,'col'=8] {'core'}, dimensions={0} | all-to-all | bytes 786432 | tf_op jit(solution)/shard_map/all_to_all | solution.py:69
  133.6 0.0 copy-done.1
  133.6 0.9 fusion.6
  134.5 0.7 copy.11
  (8 shorter events, 0.1 us)
Async XLA Ops:
  0.6 13.0 %copy-start = (bf16[128,768]{1,0:T(8,128)(2,1)S(1)}, bf16[128,768]{1,0:T(8,128)(2,1)}, u32[]{:S(2)}) copy-start(bf16[128,768]{1,0:T(8,128)(2,1)} %param.5) | copy-start | bytes 589828
  6.3 14.4 %all-to-all-start = ((s32[32,1,64]{2,1,0:T(1,128)}), s32[32,1,64]{2,1,0:T(1,128)S(1)}, u32[]{:S(2)}, u32[]{:S(2)}) async-start(s32[32,1,64]{2,1,0:T(1,128)} %bitcast.1), calls=%async_computation | async-start | bytes 32768 | tf_op jit(solution)/shard_map/all_to_all | solution.py:40
  20.7 75.3 %all-to-all-start.1 = ((bf16[32,64,768]{2,1,0:T(8,128)(2,1)}), bf16[32,64,768]{2,1,0:T(8,128)(2,1)S(1)}, u32[]{:S(2)}, u32[]{:S(2)}) async-start(bf16[32,64,768]{2,1,0:T(8,128)(2,1)} %bitcast.3), calls=%async_computation.1 | async-start | bytes 6291456 | tf_op jit(solution)/shard_map/all_to_all | solution.py:37
  23.5 73.4 %copy-start.2 = (s32[96]{0:T(128)S(1)}, s32[96]{0:T(128)}, u32[]{:S(2)}) copy-start(s32[96]{0:T(128)} %param.9) | copy-start | bytes 1156
  96.8 36.8 %copy-start.1 = (bf16[96,768]{1,0:T(8,128)(2,1)}, bf16[96,768]{1,0:T(8,128)(2,1)S(1)}, u32[]{:S(2)}) copy-start(bf16[96,768]{1,0:T(8,128)(2,1)S(1)} %multiply_convert_fusion) | copy-start | bytes 442372

commit v3 on v2

--- a/solution.py
+++ b/solution.py
@@ -11,8 +11,11 @@
 
 
 def local(doc_embed, pair_doc, pair_owner, pair_slot, label_cluster):
-    axes = ("y", "core", "col")
+    axes = ("y", "core", "zh", "zr")
+    near = ("y", "core", "zr")
     devices = lax.axis_size(axes)
+    halves = lax.axis_size("zr")
+    group = devices // 2
     pairs = pair_doc.shape[0]
     docs, width = doc_embed.shape
     owned = label_cluster.shape[0]
@@ -25,7 +28,11 @@
     earlier = (pid[None, :] < pid[:, None]).astype(bf16)
     before = jnp.dot(earlier, owner_hits, preferred_element_type=f32)
     rank = jnp.sum(before * owner_hits.astype(f32), axis=1).astype(jnp.int32)
-    position = owner * capacity + rank
+    cols = 2 * halves
+    o_row, o_col = owner // cols, owner % cols
+    o_zh, o_zr = o_col // halves, o_col % halves
+    proxy = o_row * halves + o_zr
+    position = proxy * (2 * capacity) + o_zh * capacity + rank
 
     place = (jnp.arange(devices * capacity, dtype=jnp.int32)[:, None] == position[None, :]).astype(bf16)
     tags = jnp.stack([pair_doc + 1, pair_slot + 1], axis=1).astype(bf16)
@@ -35,15 +42,23 @@
     send_rows = jnp.dot(pick, doc_embed, preferred_element_type=f32).astype(bf16)
 
     got_rows = lax.all_to_all(
-        send_rows.reshape(devices, capacity, width), axes, split_axis=0, concat_axis=0, tiled=True
+        send_rows.reshape(group, 2 * capacity, width), near, split_axis=0, concat_axis=0, tiled=True
     ).reshape(devices * capacity, width)
     got_slot = lax.all_to_all(
-        send_slot.reshape(devices, 1, capacity), axes, split_axis=0, concat_axis=0, tiled=True
+        send_slot.reshape(group, 1, 2 * capacity), near, split_axis=0, concat_axis=0, tiled=True
     ).reshape(devices * capacity)
 
+    me = lax.axis_index("zh")
+    block = (jnp.arange(devices * capacity, dtype=jnp.int32) // capacity) % 2
+    wanted = jnp.stack([1 - me, me])
     label_ids = jnp.arange(owned, dtype=jnp.int32)
-    onehot = (label_ids[:, None] == got_slot[None, :]).astype(bf16)
-    label_sums = jnp.dot(onehot, got_rows, preferred_element_type=f32)
+    onehot = (
+        (label_ids[None, :, None] == got_slot[None, None, :])
+        & (block[None, None, :] == wanted[:, None, None])
+    ).astype(bf16).reshape(2 * owned, devices * capacity)
+    partial = jnp.dot(onehot, got_rows, preferred_element_type=f32)
+    mirrored = lax.ppermute(partial[:owned], "zh", [(0, 1), (1, 0)])
+    label_sums = partial[owned:] + mirrored
     label_vectors = rms_scale(label_sums).astype(bf16)
     members = (jnp.arange(CLUSTERS, dtype=jnp.int32)[:, None] == label_cluster[None, :]).astype(bf16)
     partial_sums = jnp.dot(members, label_vectors, preferred_element_type=f32)
@@ -54,7 +69,7 @@
             partial_sums.reshape(2, CLUSTERS // 2, width), "core", split_axis=0, concat_axis=0, tiled=True
         )
         half = jnp.sum(pair, axis=0)
-        chips = ("y", "col")
+        chips = ("y", "zh", "zr")
         parts = lax.all_to_all(
             half.reshape(devices // 2, share, width), chips, split_axis=0, concat_axis=0, tiled=True
         )
@@ -84,8 +99,8 @@
 
 def solution(mesh):
     rows, cols = mesh.shape["row"], mesh.shape["col"]
-    split = Mesh(mesh.devices.reshape(rows // 2, 2, cols), ("y", "core", "col"))
-    spread = ("y", "core", "col")
+    split = Mesh(mesh.devices.reshape(rows // 2, 2, 2, cols // 2), ("y", "core", "zh", "zr"))
+    spread = ("y", "core", "zh", "zr")
     placed = (P(spread, None), P(spread), P(spread, None), P(spread), P(spread))
     return jax.shard_map(
         local,

time: 136 us -> 120 us (0.88)
  waiting for transfers between devices: 75.9 us -> 54.7 us
  starting transfers between devices: 10.1 us -> 12.7 us
  blocking collectives: 36.2 us -> 37.7 us
    all_to_all x2, waiting for transfers between devices: 75.9 us -> 41.6 us  [the longest x1 38.6 us: local(): lax.all_to_all(send_rows.reshape(group, 2 * capacity, width), near, split...]
    ppermute x0 -> x1, waiting for transfers between devices: none -> 13.1 us  [local(): mirrored = lax.ppermute(partial[:owned], 'zh', [(0, 1), (1, 0)])]
    ppermute x0 -> x1, starting transfers between devices: none -> 2.65 us  [local(): mirrored = lax.ppermute(partial[:owned], 'zh', [(0, 1), (1, 0)])]
    all_to_all x1, blocking collectives: 16.5 us -> 18.1 us  [local(): lax.all_to_all(half.reshape(devices // 2, share, width), chips, split_axi...]
  transfers between devices with their start and end apart: 2 -> 3, of which waited for: 2 -> 3; matrix products, arithmetic and copies ran while one was open for 3% -> 3% of each run, Pallas kernels for 0% -> 0%
where the time goes in v3:
time: 120 us; the launch traced here: 119 us
  waiting for transfers between devices  54.7 us (46%)
  blocking collectives  37.7 us (31%)
  starting transfers between devices  12.7 us (11%)
  matrix products  8.14 us (7%)
  other arithmetic  3.85 us (3%)
  local copies, waits for them, and re-layouts  1.46 us (1%)
    all_to_all x1, waiting for transfers between devices, local(): lax.all_to_all(send_rows.reshape(group, 2 * capacity, width), near, split...  38.6 us
    all_to_all x1, blocking collectives, local(): lax.all_to_all(half.reshape(devices // 2, share, width), chips, split_axi...  18.1 us
    ppermute x1, waiting for transfers between devices, local(): mirrored = lax.ppermute(partial[:owned], 'zh', [(0, 1), (1, 0)])  13.1 us
    all_to_all x1, blocking collectives, local(): lax.all_to_all(jnp.broadcast_to(own[None], (devices // 2, share, width)),...  11.2 us
    all_to_all x1, starting transfers between devices, local(): lax.all_to_all(send_slot.reshape(group, 1, 2 * capacity), near, split_axi...  6.32 us
    all_to_all x1, blocking collectives, local(): lax.all_to_all(partial_sums.reshape(2, CLUSTERS // 2, width), 'core', spl...  4.37 us
    all_to_all x1, blocking collectives, local(): lax.all_to_all(jnp.broadcast_to(half_c[None], (2, CLUSTERS // 2, width)),...  4.05 us
    all_to_all x1, starting transfers between devices, local(): lax.all_to_all(send_rows.reshape(group, 2 * capacity, width), near, split...  3.74 us
  transfers between devices with their start and end apart: 3, of which 3 were waited for; matrix products, arithmetic and copies ran while one was open for 3% of the time, Pallas kernels for 0%

profile of v3, /device:TPU:0, one launch (start us, length us, event | category | flops | bytes accessed | tf_op | source)
XLA Modules:
  0.0 119.4 jit_solution(9637240400981913143)
XLA Ops:
  0.6 0.0 copy-start
  0.6 0.7 add_convert_fusion.1
  1.4 0.7 add_convert_fusion
  2.1 1.3 %fusion.7 = f32[1024]{0:T(1024)S(1)} fusion(s32[1024]{0:T(1024)} %bitcast.31), kind=kOutput, calls=%fused_computation.11 | convolution fusion | flops 68353024 | bytes 8192 | tf_op jit(solution)/shard_map/dot_general | solution.py:29
  3.4 0.7 fusion.21
  4.1 1.5 %fusion.4 = s32[2048,2]{0,1:T(2,128)S(1)} fusion(s32[1024]{0:T(1024)S(1)} %fusion.21, bf16[1024,1]{0,1:T(2,128)(2,1)S(1)} %stack.22, bf16[1024,1]{0,1:T(2,128)(2,1)S(1)} %stack.21), kind=kOutput, calls=%fused_computation.7 | convolution fusion | flops 10502144 | bytes 24576 | tf_op jit(solution)/shard_map/dot_general | solution.py:39
  5.6 0.6 fusion.33
  6.2 6.3 %all-to-all-start = ((s32[16,1,128]{2,1,0:T(1,128)}), s32[16,1,128]{2,1,0:T(1,128)S(1)}, u32[]{:S(2)}, u32[]{:S(2)}) async-start(s32[16,1,128]{2,1,0:T(1,128)} %get-tuple-element.4), calls=%async_computation | async-start | bytes 16384 | tf_op jit(solution)/shard_map/all_to_all | solution.py:47
  12.5 0.0 copy-done
  12.5 2.4 %convolution_convert_fusion = bf16[2048,768]{1,0:T(8,128)(2,1)} fusion(bf16[128,768]{1,0:T(8,128)(2,1)S(1)} %copy-done, s32[2048]{0:T(1024)S(1)} %bitcast.29), kind=kOutput, calls=%fused_computation.5 | convolution fusion | flops 404488192 | bytes 3350528 | tf_op jit(solution)/shard_map/dot_general | solution.py:42
  15.0 3.0 %all-to-all-done = s32[16,1,128]{2,1,0:T(1,128)S(1)} async-done(((s32[16,1,128]{2,1,0:T(1,128)}), s32[16,1,128]{2,1,0:T(1,128)S(1)}, u32[]{:S(2)}, u32[]{:S(2)}) %all-to-all-start) | async-done | bytes 8224 | tf_op jit(solution)/shard_map/all_to_all | solution.py:47
  17.9 3.7 %all-to-all-start.1 = ((bf16[16,128,768]{2,1,0:T(8,128)(2,1)}), bf16[16,128,768]{2,1,0:T(8,128)(2,1)S(1)}, u32[]{:S(2)}, u32[]{:S(2)}) async-start(bf16[16,128,768]{2,1,0:T(8,128)(2,1)} %bitcast.8), calls=%async_computation.1 | async-start | bytes 6291456 | tf_op jit(solution)/shard_map/all_to_all | solution.py:44
  21.7 0.1 pad_add_fusion
  21.8 0.1 broadcast_compare_fusion
  21.9 0.1 iota_compare_fusion.14
  22.0 0.9 broadcast_and_fusion
  22.9 0.0 copy-start.2
  22.9 38.6 %all-to-all-done.1 = bf16[16,128,768]{2,1,0:T(8,128)(2,1)S(1)} async-done(((bf16[16,128,768]{2,1,0:T(8,128)(2,1)}), bf16[16,128,768]{2,1,0:T(8,128)(2,1)S(1)}, u32[]{:S(2)}, u32[]{:S(2)}) %all-to-all-start.1) | async-done | bytes 3145760 | tf_op jit(solution)/shard_map/all_to_all | solution.py:44
  61.5 1.8 %fusion.34 = f32[192,768]{1,0:T(8,128)S(1)} fusion(pred[192,2048]{1,0:T(32,128)(4,1)} %bitcast.28, bf16[2048,768]{1,0:T(8,128)(2,1)S(1)} %bitcast.24), kind=kOutput, calls=%fused_computation.74 | convolution fusion | flops 603979776 | bytes 4128768 | tf_op jit(solution)/shard_map/dot_general | solution.py:59
  63.4 2.6 %collective-permute-start = (f32[96,768]{1,0:T(8,128)S(1)}, f32[96,768]{1,0:T(8,128)S(1)}, u32[]{:S(2)}, u32[]{:S(2)}) collective-permute-start(f32[96,768]{1,0:T(8,128)S(1)} %slice.19), channel_id=1, source_target_pairs={{0,4},{4,0},{1,5},{5,1},{2,6},{6,2},{3,7},{7,3},{8,12},{12,8},{9,1... | collective-permute-start | bytes 884744 | tf_op jit(solution)/shard_map/ppermute | solution.py:60
  66.0 13.1 %collective-permute-done = f32[96,768]{1,0:T(8,128)S(1)} collective-permute-done((f32[96,768]{1,0:T(8,128)S(1)}, f32[96,768]{1,0:T(8,128)S(1)}, u32[]{:S(2)}, u32[]{:S(2)}) %collective-permute-start) | collective-permute-done | bytes 294944 | tf_op jit(solution)/shard_map/ppermute | solution.py:60
  79.1 0.1 multiply_reduce_fusion
  79.2 0.1 multiply_convert_fusion
  79.3 0.0 copy-done.2
  79.4 0.0 copy-start.1
  79.4 0.2 fusion.10
  79.6 4.4 %all_to_all.30 = f32[2,128,768]{2,1,0:T(8,128)S(1)} all-to-all(f32[2,128,768]{2,1,0:T(8,128)S(1)} %bitcast.25), channel_id=1, replica_groups=mesh['y'=2,'core'=2,'zh'=2,'zr'=4] {'core'}, dimensions={0} | all-to-all | bytes 1572864 | tf_op jit(solution)/shard_map/all_to_all | solution.py:68
  84.0 0.1 reduce_sum.47
  84.0 18.1 %all_to_all.31 = f32[16,8,768]{2,1,0:T(8,128)S(1)} all-to-all(f32[16,8,768]{2,1,0:T(8,128)S(1)} %bitcast.26), channel_id=1, replica_groups=mesh['y'=2,'core'=2,'zh'=2,'zr'=4] {'y','zh','zr'}, dimensions={0} | all-to-all | bytes 786432 | tf_op jit(solution)/shard_map/all_to_all | solution.py:73
  102.1 0.1 multiply_reduce_fusion.1
  102.3 0.1 multiply_convert_fusion.1
  102.4 11.2 %all_to_all.32 = bf16[16,8,768]{2,1,0:T(8,128)(2,1)S(1)} all-to-all(bf16[16,8,768]{2,1,0:T(8,128)(2,1)S(1)} %broadcast_in_dim.6), channel_id=1, replica_groups=mesh['y'=2,'core'=2,'zh'=2,'zr'=4] {'y','zh','zr'}, dimensions={0} | all-to-all | bytes 393216 | tf_op jit(solution)/shard_map/all_to_all | solution.py:77
  113.7 4.0 %all_to_all.33 = bf16[2,128,768]{2,1,0:T(8,128)(2,1)S(1)} all-to-all(bf16[2,128,768]{2,1,0:T(8,128)(2,1)S(1)} %broadcast_in_dim.8), channel_id=1, replica_groups=mesh['y'=2,'core'=2,'zh'=2,'zr'=4] {'core'}, dimensions={0} | all-to-all | bytes 786432 | tf_op jit(solution)/shard_map/all_to_all | solution.py:84
  117.7 0.0 copy-done.1
  117.7 0.9 fusion.6
  118.6 0.7 copy.13
  (9 shorter events, 0.1 us)
Async XLA Ops:
  0.6 11.9 %copy-start = (bf16[128,768]{1,0:T(8,128)(2,1)S(1)}, bf16[128,768]{1,0:T(8,128)(2,1)}, u32[]{:S(2)}) copy-start(bf16[128,768]{1,0:T(8,128)(2,1)} %param.5) | copy-start | bytes 589828
  6.2 11.7 %all-to-all-start = ((s32[16,1,128]{2,1,0:T(1,128)}), s32[16,1,128]{2,1,0:T(1,128)S(1)}, u32[]{:S(2)}, u32[]{:S(2)}) async-start(s32[16,1,128]{2,1,0:T(1,128)} %get-tuple-element.4), calls=%async_computation | async-start | bytes 16384 | tf_op jit(solution)/shard_map/all_to_all | solution.py:47
  17.9 43.6 %all-to-all-start.1 = ((bf16[16,128,768]{2,1,0:T(8,128)(2,1)}), bf16[16,128,768]{2,1,0:T(8,128)(2,1)S(1)}, u32[]{:S(2)}, u32[]{:S(2)}) async-start(bf16[16,128,768]{2,1,0:T(8,128)(2,1)} %bitcast.8), calls=%async_computation.1 | async-start | bytes 6291456 | tf_op jit(solution)/shard_map/all_to_all | solution.py:44
  22.9 56.4 %copy-start.2 = (s32[96]{0:T(128)S(1)}, s32[96]{0:T(128)}, u32[]{:S(2)}) copy-start(s32[96]{0:T(128)} %param.9) | copy-start | bytes 1156
  63.4 15.8 %collective-permute-start = (f32[96,768]{1,0:T(8,128)S(1)}, f32[96,768]{1,0:T(8,128)S(1)}, u32[]{:S(2)}, u32[]{:S(2)}) collective-permute-start(f32[96,768]{1,0:T(8,128)S(1)} %slice.19), channel_id=1, source_target_pairs={{0,4},{4,0},{1,5},{5,1},{2,6},{6,2},{3,7},{7,3},{8,12},{12,8},{9,1... | collective-permute-start | bytes 884744 | tf_op jit(solution)/shard_map/ppermute | solution.py:60
  79.4 38.3 %copy-start.1 = (bf16[96,768]{1,0:T(8,128)(2,1)}, bf16[96,768]{1,0:T(8,128)(2,1)S(1)}, u32[]{:S(2)}) copy-start(bf16[96,768]{1,0:T(8,128)(2,1)S(1)} %multiply_convert_fusion) | copy-start | bytes 442372

commit v4 on v3

--- a/solution.py
+++ b/solution.py
@@ -63,27 +63,17 @@
     members = (jnp.arange(CLUSTERS, dtype=jnp.int32)[:, None] == label_cluster[None, :]).astype(bf16)
     partial_sums = jnp.dot(members, label_vectors, preferred_element_type=f32)
 
-    if CLUSTERS % devices == 0:
-        share = CLUSTERS // devices
-        pair = lax.all_to_all(
-            partial_sums.reshape(2, CLUSTERS // 2, width), "core", split_axis=0, concat_axis=0, tiled=True
+    if CLUSTERS % group == 0:
+        share = CLUSTERS // group
+        parts = lax.all_to_all(
+            partial_sums.reshape(group, share, width), near, split_axis=0, concat_axis=0, tiled=True
         )
-        half = jnp.sum(pair, axis=0)
-        chips = ("y", "zh", "zr")
-        parts = lax.all_to_all(
-            half.reshape(devices // 2, share, width), chips, split_axis=0, concat_axis=0, tiled=True
-        )
-        own = rms_scale(jnp.sum(parts, axis=0)).astype(bf16)
-        half_c = lax.all_to_all(
-            jnp.broadcast_to(own[None], (devices // 2, share, width)),
-            chips,
-            split_axis=0,
-            concat_axis=0,
-            tiled=True,
-        ).reshape(CLUSTERS // 2, width)
+        half_sums = jnp.sum(parts, axis=0)
+        sums = half_sums + lax.ppermute(half_sums, "zh", [(0, 1), (1, 0)])
+        own = rms_scale(sums).astype(bf16)
         centroids = lax.all_to_all(
-            jnp.broadcast_to(half_c[None], (2, CLUSTERS // 2, width)),
-            "core",
+            jnp.broadcast_to(own[None], (group, share, width)),
+            near,
             split_axis=0,
             concat_axis=0,
             tiled=True,

time: 120 us -> 114 us (0.950)
  blocking collectives: 37.7 us -> 26.2 us
  starting transfers between devices: 12.7 us -> 15.8 us
  waiting for transfers between devices: 54.7 us -> 57.8 us
    all_to_all x4 -> x2, blocking collectives: 37.7 us -> 26.2 us  [the longest x1 15.5 us: local(): lax.all_to_all(partial_sums.reshape(group, share, width), near, split_axi...]
    ppermute x0 -> x1, starting transfers between devices: none -> 3.11 us  [local(): sums = half_sums + lax.ppermute(half_sums, 'zh', [(0, 1), (1, 0)])]
    ppermute x0 -> x1, waiting for transfers between devices: none -> 3.07 us  [local(): sums = half_sums + lax.ppermute(half_sums, 'zh', [(0, 1), (1, 0)])]
  transfers between devices with their start and end apart: 3 -> 4, of which waited for: 3 -> 4; matrix products, arithmetic and copies ran while one was open for 3% -> 3% of each run, Pallas kernels for 0% -> 0%
where the time goes in v4:
time: 114 us
  waiting for transfers between devices  57.8 us (51%)
  blocking collectives  26.2 us (23%)
  starting transfers between devices  15.8 us (14%)
  matrix products  8.14 us (7%)
  other arithmetic  3.81 us (3%)
  local copies, waits for them, and re-layouts  1.45 us (1%)
    all_to_all x1, waiting for transfers between devices, local(): lax.all_to_all(send_rows.reshape(group, 2 * capacity, width), near, split...  38.6 us
    all_to_all x1, blocking collectives, local(): lax.all_to_all(partial_sums.reshape(group, share, width), near, split_axi...  15.5 us
    ppermute x1, waiting for transfers between devices, local(): mirrored = lax.ppermute(partial[:owned], 'zh', [(0, 1), (1, 0)])  13.1 us
    all_to_all x1, blocking collectives, local(): lax.all_to_all(jnp.broadcast_to(own[None], (group, share, width)), near,...  10.7 us
    all_to_all x1, starting transfers between devices, local(): lax.all_to_all(send_slot.reshape(group, 1, 2 * capacity), near, split_axi...  6.32 us
    all_to_all x1, starting transfers between devices, local(): lax.all_to_all(send_rows.reshape(group, 2 * capacity, width), near, split...  3.74 us
    ppermute x1, starting transfers between devices, local(): sums = half_sums + lax.ppermute(half_sums, 'zh', [(0, 1), (1, 0)])  3.11 us
    ppermute x1, waiting for transfers between devices, local(): sums = half_sums + lax.ppermute(half_sums, 'zh', [(0, 1), (1, 0)])  3.07 us
  transfers between devices with their start and end apart: 4, of which 4 were waited for; matrix products, arithmetic and copies ran while one was open for 3% of the time, Pallas kernels for 0%

profile of v4, /device:TPU:0, one launch (start us, length us, event | category | flops | bytes accessed | tf_op | source)
XLA Modules:
  0.0 114.0 jit_solution(4044239189230847004)
XLA Ops:
  0.6 0.0 copy-start
  0.6 0.7 add_convert_fusion.1
  1.4 0.7 add_convert_fusion
  2.1 1.3 %fusion.7 = f32[1024]{0:T(1024)S(1)} fusion(s32[1024]{0:T(1024)} %bitcast.27), kind=kOutput, calls=%fused_computation.11 | convolution fusion | flops 68353024 | bytes 8192 | tf_op jit(solution)/shard_map/dot_general | solution.py:29
  3.4 0.7 fusion.21
  4.1 1.5 %fusion.4 = s32[2048,2]{0,1:T(2,128)S(1)} fusion(s32[1024]{0:T(1024)S(1)} %fusion.21, bf16[1024,1]{0,1:T(2,128)(2,1)S(1)} %stack.22, bf16[1024,1]{0,1:T(2,128)(2,1)S(1)} %stack.21), kind=kOutput, calls=%fused_computation.7 | convolution fusion | flops 10502144 | bytes 24576 | tf_op jit(solution)/shard_map/dot_general | solution.py:39
  5.6 0.6 fusion.33
  6.2 6.3 %all-to-all-start = ((s32[16,1,128]{2,1,0:T(1,128)}), s32[16,1,128]{2,1,0:T(1,128)S(1)}, u32[]{:S(2)}, u32[]{:S(2)}) async-start(s32[16,1,128]{2,1,0:T(1,128)} %get-tuple-element.6), calls=%async_computation | async-start | bytes 16384 | tf_op jit(solution)/shard_map/all_to_all | solution.py:47
  12.5 0.0 copy-done
  12.5 2.4 %convolution_convert_fusion = bf16[2048,768]{1,0:T(8,128)(2,1)} fusion(bf16[128,768]{1,0:T(8,128)(2,1)S(1)} %copy-done, s32[2048]{0:T(1024)S(1)} %bitcast.25), kind=kOutput, calls=%fused_computation.5 | convolution fusion | flops 404488192 | bytes 3350528 | tf_op jit(solution)/shard_map/dot_general | solution.py:42
  15.0 3.0 %all-to-all-done = s32[16,1,128]{2,1,0:T(1,128)S(1)} async-done(((s32[16,1,128]{2,1,0:T(1,128)}), s32[16,1,128]{2,1,0:T(1,128)S(1)}, u32[]{:S(2)}, u32[]{:S(2)}) %all-to-all-start) | async-done | bytes 8224 | tf_op jit(solution)/shard_map/all_to_all | solution.py:47
  17.9 3.7 %all-to-all-start.1 = ((bf16[16,128,768]{2,1,0:T(8,128)(2,1)}), bf16[16,128,768]{2,1,0:T(8,128)(2,1)S(1)}, u32[]{:S(2)}, u32[]{:S(2)}) async-start(bf16[16,128,768]{2,1,0:T(8,128)(2,1)} %bitcast.8), calls=%async_computation.1 | async-start | bytes 6291456 | tf_op jit(solution)/shard_map/all_to_all | solution.py:44
  21.7 0.1 pad_add_fusion
  21.8 0.1 broadcast_compare_fusion
  21.9 0.1 iota_compare_fusion.14
  22.0 0.9 broadcast_and_fusion
  22.9 0.0 copy-start.2
  22.9 38.6 %all-to-all-done.1 = bf16[16,128,768]{2,1,0:T(8,128)(2,1)S(1)} async-done(((bf16[16,128,768]{2,1,0:T(8,128)(2,1)}), bf16[16,128,768]{2,1,0:T(8,128)(2,1)S(1)}, u32[]{:S(2)}, u32[]{:S(2)}) %all-to-all-start.1) | async-done | bytes 3145760 | tf_op jit(solution)/shard_map/all_to_all | solution.py:44
  61.5 1.8 %fusion.34 = f32[192,768]{1,0:T(8,128)S(1)} fusion(pred[192,2048]{1,0:T(32,128)(4,1)} %bitcast.24, bf16[2048,768]{1,0:T(8,128)(2,1)S(1)} %bitcast.22), kind=kOutput, calls=%fused_computation.74 | convolution fusion | flops 603979776 | bytes 4128768 | tf_op jit(solution)/shard_map/dot_general | solution.py:59
  63.4 2.6 %collective-permute-start = (f32[96,768]{1,0:T(8,128)S(1)}, f32[96,768]{1,0:T(8,128)S(1)}, u32[]{:S(2)}, u32[]{:S(2)}) collective-permute-start(f32[96,768]{1,0:T(8,128)S(1)} %slice.19), channel_id=1, source_target_pairs={{0,4},{4,0},{1,5},{5,1},{2,6},{6,2},{3,7},{7,3},{8,12},{12,8},{9,1... | collective-permute-start | bytes 884744 | tf_op jit(solution)/shard_map/ppermute | solution.py:60
  66.0 13.1 %collective-permute-done = f32[96,768]{1,0:T(8,128)S(1)} collective-permute-done((f32[96,768]{1,0:T(8,128)S(1)}, f32[96,768]{1,0:T(8,128)S(1)}, u32[]{:S(2)}, u32[]{:S(2)}) %collective-permute-start) | collective-permute-done | bytes 294944 | tf_op jit(solution)/shard_map/ppermute | solution.py:60
  79.1 0.1 multiply_reduce_fusion
  79.2 0.1 multiply_convert_fusion
  79.3 0.0 copy-done.2
  79.4 0.0 copy-start.1
  79.4 0.2 fusion.10
  79.6 15.5 %all_to_all.20 = f32[16,16,768]{2,1,0:T(8,128)S(1)} all-to-all(f32[16,16,768]{2,1,0:T(8,128)S(1)} %bitcast.23), channel_id=1, replica_groups=mesh['y'=2,'core'=2,'zh'=2,'zr'=4] {'y','core','zr'}, dimensions={0} | all-to-all | bytes 1572864 | tf_op jit(solution)/shard_map/all_to_all | solution.py:68
  95.2 3.1 %collective-permute-start.1 = (f32[16,768]{1,0:T(8,128)S(1)}, f32[16,768]{1,0:T(8,128)S(1)}, u32[]{:S(2)}, u32[]{:S(2)}) collective-permute-start(f32[16,768]{1,0:T(8,128)S(1)} %reduce_sum.38), channel_id=1, source_target_pairs={{0,4},{4,0},{1,5},{5,1},{2,6},{6,2},{3,7},{7,3},{8,12},{12,8},{9,1... | collective-permute-start | bytes 147464 | tf_op jit(solution)/shard_map/ppermute | solution.py:72
  98.3 3.1 %collective-permute-done.1 = f32[16,768]{1,0:T(8,128)S(1)} collective-permute-done((f32[16,768]{1,0:T(8,128)S(1)}, f32[16,768]{1,0:T(8,128)S(1)}, u32[]{:S(2)}, u32[]{:S(2)}) %collective-permute-start.1) | collective-permute-done | bytes 49184 | tf_op jit(solution)/shard_map/ppermute | solution.py:72
  101.4 0.1 multiply_reduce_fusion.1
  101.5 0.1 multiply_convert_fusion.1
  101.6 10.7 %all_to_all.21 = bf16[16,16,768]{2,1,0:T(8,128)(2,1)S(1)} all-to-all(bf16[16,16,768]{2,1,0:T(8,128)(2,1)S(1)} %broadcast_in_dim.2), channel_id=1, replica_groups=mesh['y'=2,'core'=2,'zh'=2,'zr'=4] {'y','core','zr'}, dimensions={0} | all-to-all | bytes 786432 | tf_op jit(solution)/shard_map/all_to_all | solution.py:74
  112.3 0.9 fusion.6
  113.2 0.7 copy.12
  114.0 0.0 copy-done.1
  (8 shorter events, 0.1 us)
Async XLA Ops:
  0.6 11.9 %copy-start = (bf16[128,768]{1,0:T(8,128)(2,1)S(1)}, bf16[128,768]{1,0:T(8,128)(2,1)}, u32[]{:S(2)}) copy-start(bf16[128,768]{1,0:T(8,128)(2,1)} %param.5) | copy-start | bytes 589828
  6.2 11.7 %all-to-all-start = ((s32[16,1,128]{2,1,0:T(1,128)}), s32[16,1,128]{2,1,0:T(1,128)S(1)}, u32[]{:S(2)}, u32[]{:S(2)}) async-start(s32[16,1,128]{2,1,0:T(1,128)} %get-tuple-element.6), calls=%async_computation | async-start | bytes 16384 | tf_op jit(solution)/shard_map/all_to_all | solution.py:47
  17.9 43.6 %all-to-all-start.1 = ((bf16[16,128,768]{2,1,0:T(8,128)(2,1)}), bf16[16,128,768]{2,1,0:T(8,128)(2,1)S(1)}, u32[]{:S(2)}, u32[]{:S(2)}) async-start(bf16[16,128,768]{2,1,0:T(8,128)(2,1)} %bitcast.8), calls=%async_computation.1 | async-start | bytes 6291456 | tf_op jit(solution)/shard_map/all_to_all | solution.py:44
  22.9 56.4 %copy-start.2 = (s32[96]{0:T(128)S(1)}, s32[96]{0:T(128)}, u32[]{:S(2)}) copy-start(s32[96]{0:T(128)} %param.9) | copy-start | bytes 1156
  63.4 15.8 %collective-permute-start = (f32[96,768]{1,0:T(8,128)S(1)}, f32[96,768]{1,0:T(8,128)S(1)}, u32[]{:S(2)}, u32[]{:S(2)}) collective-permute-start(f32[96,768]{1,0:T(8,128)S(1)} %slice.19), channel_id=1, source_target_pairs={{0,4},{4,0},{1,5},{5,1},{2,6},{6,2},{3,7},{7,3},{8,12},{12,8},{9,1... | collective-permute-start | bytes 884744 | tf_op jit(solution)/shard_map/ppermute | solution.py:60
  79.4 34.6 %copy-start.1 = (bf16[96,768]{1,0:T(8,128)(2,1)}, bf16[96,768]{1,0:T(8,128)(2,1)S(1)}, u32[]{:S(2)}) copy-start(bf16[96,768]{1,0:T(8,128)(2,1)S(1)} %multiply_convert_fusion) | copy-start | bytes 442372
  95.2 6.2 %collective-permute-start.1 = (f32[16,768]{1,0:T(8,128)S(1)}, f32[16,768]{1,0:T(8,128)S(1)}, u32[]{:S(2)}, u32[]{:S(2)}) collective-permute-start(f32[16,768]{1,0:T(8,128)S(1)} %reduce_sum.38), channel_id=1, source_target_pairs={{0,4},{4,0},{1,5},{5,1},{2,6},{6,2},{3,7},{7,3},{8,12},{12,8},{9,1... | collective-permute-start | bytes 147464 | tf_op jit(solution)/shard_map/ppermute | solution.py:72

commit v5 on v4

--- a/solution.py
+++ b/solution.py
@@ -36,17 +36,28 @@
 
     place = (jnp.arange(devices * capacity, dtype=jnp.int32)[:, None] == position[None, :]).astype(bf16)
     tags = jnp.stack([pair_doc + 1, pair_slot + 1], axis=1).astype(bf16)
-    picked = jnp.dot(place, tags, preferred_element_type=f32).astype(jnp.int32) - 1
-    send_doc, send_slot = picked[:, 0], picked[:, 1]
-    pick = (send_doc[:, None] == jnp.arange(docs, dtype=jnp.int32)[None, :]).astype(bf16)
-    send_rows = jnp.dot(pick, doc_embed, preferred_element_type=f32).astype(bf16)
+    picked = jnp.dot(place, tags, preferred_element_type=f32).astype(jnp.int32)
+    send_doc, slot_plus = picked[:, 0] - 1, picked[:, 1]
 
-    got_rows = lax.all_to_all(
-        send_rows.reshape(group, 2 * capacity, width), near, split_axis=0, concat_axis=0, tiled=True
-    ).reshape(devices * capacity, width)
-    got_slot = lax.all_to_all(
-        send_slot.reshape(group, 1, 2 * capacity), near, split_axis=0, concat_axis=0, tiled=True
-    ).reshape(devices * capacity)
+    span, extra = 2 * capacity, 16
+    doc_part = (send_doc[:, None] == jnp.arange(docs, dtype=jnp.int32)[None, :]).astype(bf16)
+    doc_part = jnp.concatenate(
+        [doc_part.reshape(group, span, docs), jnp.zeros((group, extra, docs), bf16)], axis=1
+    )
+    slot_row = slot_plus.astype(bf16).reshape(group, 1, span)
+    slot_part = jnp.concatenate(
+        [jnp.zeros((group, span, span), bf16), slot_row, jnp.zeros((group, extra - 1, span), bf16)],
+        axis=1,
+    )
+    chooser = jnp.concatenate([doc_part, slot_part], axis=2).reshape(group * (span + extra), docs + span)
+    table = jnp.concatenate([doc_embed, jnp.eye(span, width, dtype=bf16)], axis=0)
+    send = jnp.dot(chooser, table, preferred_element_type=f32).astype(bf16)
+
+    got = lax.all_to_all(
+        send.reshape(group, span + extra, width), near, split_axis=0, concat_axis=0, tiled=True
+    )
+    got_slot = got[:, span, :span].astype(jnp.int32).reshape(devices * capacity) - 1
+    got_rows = got.reshape(group * (span + extra), width)
 
     me = lax.axis_index("zh")
     block = (jnp.arange(devices * capacity, dtype=jnp.int32) // capacity) % 2
@@ -55,7 +66,9 @@
     onehot = (
         (label_ids[None, :, None] == got_slot[None, None, :])
         & (block[None, None, :] == wanted[:, None, None])
-    ).astype(bf16).reshape(2 * owned, devices * capacity)
+    ).astype(bf16).reshape(2 * owned, group, span)
+    onehot = jnp.concatenate([onehot, jnp.zeros((2 * owned, group, extra), bf16)], axis=2)
+    onehot = onehot.reshape(2 * owned, group * (span + extra))
     partial = jnp.dot(onehot, got_rows, preferred_element_type=f32)
     mirrored = lax.ppermute(partial[:owned], "zh", [(0, 1), (1, 0)])
     label_sums = partial[owned:] + mirrored

time: 114 us -> 117 us (1.026)
  starting transfers between devices: 15.8 us -> 12.1 us
  local copies, waits for them, and re-layouts: 1.45 us -> 4.41 us
  waiting for transfers between devices: 57.8 us -> 60.6 us
    all_to_all x2 -> x1, starting transfers between devices: 10.1 us -> 6.32 us  [local(): lax.all_to_all(send.reshape(group, span + extra, width), near, split_axis...]
    all_to_all x2 -> x1, waiting for transfers between devices: 41.6 us -> 44.5 us  [local(): lax.all_to_all(send.reshape(group, span + extra, width), near, split_axis...]
    convert_element_type x0 -> x1, local copies, waits for them, and re-layouts: none -> 2.4 us  [local(): onehot = ((label_ids[None, :, None] == got_slot[None, None, :]) & (block[...]
  transfers between devices with their start and end apart: 4 -> 3, of which waited for: 4 -> 3; matrix products, arithmetic and copies ran while one was open for 3% -> 0% of each run, Pallas kernels for 0% -> 0%
where the time goes in v5:
time: 117 us
  waiting for transfers between devices  60.6 us (52%)
  blocking collectives  26.2 us (22%)
  starting transfers between devices  12.1 us (10%)
  matrix products  8.81 us (8%)
  local copies, waits for them, and re-layouts  4.41 us (4%)
  other arithmetic  3.76 us (3%)
    all_to_all x1, waiting for transfers between devices, local(): lax.all_to_all(send.reshape(group, span + extra, width), near, split_axis...  44.5 us
    all_to_all x1, blocking collectives, local(): lax.all_to_all(partial_sums.reshape(group, share, width), near, split_axi...  15.5 us
    ppermute x1, waiting for transfers between devices, local(): mirrored = lax.ppermute(partial[:owned], 'zh', [(0, 1), (1, 0)])  13.1 us
    all_to_all x1, blocking collectives, local(): lax.all_to_all(jnp.broadcast_to(own[None], (group, share, width)), near,...  10.7 us
    all_to_all x1, starting transfers between devices, local(): lax.all_to_all(send.reshape(group, span + extra, width), near, split_axis...  6.32 us
    ppermute x1, starting transfers between devices, local(): sums = half_sums + lax.ppermute(half_sums, 'zh', [(0, 1), (1, 0)])  3.18 us
    ppermute x1, waiting for transfers between devices, local(): sums = half_sums + lax.ppermute(half_sums, 'zh', [(0, 1), (1, 0)])  3.07 us
    dot_general x1, matrix products, local(): send = jnp.dot(chooser, table, preferred_element_type=f32).astype(bf16)  2.84 us
  transfers between devices with their start and end apart: 3, of which 3 were waited for; matrix products, arithmetic and copies ran while one was open for 0% of the time, Pallas kernels for 0%

profile of v5, /device:TPU:0, one launch (start us, length us, event | category | flops | bytes accessed | tf_op | source)
XLA Modules:
  0.0 116.8 jit_solution(9270562663167064071)
XLA Ops:
  0.7 1.3 %fusion.11 = f32[1024]{0:T(1024)S(1)} fusion(s32[1024]{0:T(1024)} %bitcast.29), kind=kOutput, calls=%fused_computation.15 | convolution fusion | flops 68353024 | bytes 8192 | tf_op jit(solution)/shard_map/dot_general | solution.py:29
  2.0 0.7 fusion.30
  2.7 0.7 add_convert_fusion.1
  3.4 0.7 add_convert_fusion
  4.1 1.5 %fusion.5 = s32[2048,2]{0,1:T(2,128)S(1)} fusion(s32[1024]{0:T(1024)S(1)} %fusion.30, bf16[1024,1]{0,1:T(2,128)(2,1)S(1)} %stack.22, bf16[1024,1]{0,1:T(2,128)(2,1)S(1)} %stack.21), kind=kOutput, calls=%fused_computation.8 | convolution fusion | flops 10498048 | bytes 24576 | tf_op jit(solution)/shard_map/dot_general | solution.py:39
  5.5 0.0 copy-start.1
  5.6 0.3 iota_compare_fusion.10
  5.9 0.1 pad_convert_fusion
  6.1 0.2 maximum_maximum_fusion
  6.3 0.2 copy-done.1
  6.5 2.8 %convolution_convert_fusion = bf16[2304,768]{1,0:T(8,128)(2,1)} fusion(bf16[2304,256]{1,0:T(8,128)(2,1)S(1)} %bitcast.21, bf16[128,768]{1,0:T(8,128)(2,1)S(1)} %fusion.15, bf16[128,768]{1,0:T(8,128)(2,1)S(1)} %copy-done.1), kind=kOutput, calls=%fused_computation.2 | convolution fusion | flops 908525568 | bytes 5111808 | tf_op jit(solution)/shard_map/dot_general | solution.py:54
  9.3 6.3 %all-to-all-start = ((bf16[16,144,768]{2,1,0:T(8,128)(2,1)}), bf16[16,144,768]{2,1,0:T(8,128)(2,1)S(1)}, u32[]{:S(2)}, u32[]{:S(2)}) async-start(bf16[16,144,768]{2,1,0:T(8,128)(2,1)} %bitcast.4), calls=%async_computation | async-start | bytes 7077888 | tf_op jit(solution)/shard_map/all_to_all | solution.py:56
  15.6 0.1 pad_add_fusion
  15.7 0.1 broadcast_compare_fusion
  15.8 44.5 %all-to-all-done = bf16[16,144,768]{2,1,0:T(8,128)(2,1)S(1)} async-done(((bf16[16,144,768]{2,1,0:T(8,128)(2,1)}), bf16[16,144,768]{2,1,0:T(8,128)(2,1)S(1)}, u32[]{:S(2)}, u32[]{:S(2)}) %all-to-all-start) | async-done | bytes 3538976 | tf_op jit(solution)/shard_map/all_to_all | solution.py:56
  60.3 0.1 iota_compare_fusion.11
  60.4 0.2 broadcast_and_fusion
  60.7 1.0 copy.13
  61.6 2.4 %copy.12 = pred[192,16,128]{0,2,1:T(8,128)(4,1)} copy(pred[192,16,128]{2,1,0:T(8,128)(4,1)} %bitcast.26) | data formatting | bytes 786432 | tf_op jit(solution)/shard_map/convert_element_type | solution.py:69
  64.0 0.0 copy-start.2
  64.0 2.0 %fusion.6 = f32[192,768]{1,0:T(8,128)S(1)} fusion(bf16[16,144,768]{2,1,0:T(8,128)(2,1)S(1)} %all-to-all-done, pred[192,16,128]{0,2,1:T(8,128)(4,1)} %copy.12), kind=kOutput, calls=%fused_computation.9 | convolution fusion | flops 679477248 | bytes 4521984 | tf_op jit(solution)/shard_map/dot_general | solution.py:72
  66.1 2.6 %collective-permute-start = (f32[96,768]{1,0:T(8,128)S(1)}, f32[96,768]{1,0:T(8,128)S(1)}, u32[]{:S(2)}, u32[]{:S(2)}) collective-permute-start(f32[96,768]{1,0:T(8,128)S(1)} %slice.25), channel_id=1, source_target_pairs={{0,4},{4,0},{1,5},{5,1},{2,6},{6,2},{3,7},{7,3},{8,12},{12,8},{9,1... | collective-permute-start | bytes 884744 | tf_op jit(solution)/shard_map/ppermute | solution.py:73
  68.8 13.1 %collective-permute-done = f32[96,768]{1,0:T(8,128)S(1)} collective-permute-done((f32[96,768]{1,0:T(8,128)S(1)}, f32[96,768]{1,0:T(8,128)S(1)}, u32[]{:S(2)}, u32[]{:S(2)}) %collective-permute-start) | collective-permute-done | bytes 294944 | tf_op jit(solution)/shard_map/ppermute | solution.py:73
  81.9 0.1 multiply_reduce_fusion
  82.0 0.1 multiply_convert_fusion
  82.1 0.0 copy-done.2
  82.1 0.0 copy-start
  82.1 0.2 fusion.17
  82.4 15.5 %all_to_all.15 = f32[16,16,768]{2,1,0:T(8,128)S(1)} all-to-all(f32[16,16,768]{2,1,0:T(8,128)S(1)} %bitcast.24), channel_id=1, replica_groups=mesh['y'=2,'core'=2,'zh'=2,'zr'=4] {'y','core','zr'}, dimensions={0} | all-to-all | bytes 1572864 | tf_op jit(solution)/shard_map/all_to_all | solution.py:81
  97.9 3.2 %collective-permute-start.1 = (f32[16,768]{1,0:T(8,128)S(1)}, f32[16,768]{1,0:T(8,128)S(1)}, u32[]{:S(2)}, u32[]{:S(2)}) collective-permute-start(f32[16,768]{1,0:T(8,128)S(1)} %reduce_sum.38), channel_id=1, source_target_pairs={{0,4},{4,0},{1,5},{5,1},{2,6},{6,2},{3,7},{7,3},{8,12},{12,8},{9,1... | collective-permute-start | bytes 147464 | tf_op jit(solution)/shard_map/ppermute | solution.py:85
  101.1 3.1 %collective-permute-done.1 = f32[16,768]{1,0:T(8,128)S(1)} collective-permute-done((f32[16,768]{1,0:T(8,128)S(1)}, f32[16,768]{1,0:T(8,128)S(1)}, u32[]{:S(2)}, u32[]{:S(2)}) %collective-permute-start.1) | collective-permute-done | bytes 49184 | tf_op jit(solution)/shard_map/ppermute | solution.py:85
  104.2 0.1 multiply_reduce_fusion.1
  104.3 0.1 multiply_convert_fusion.1
  104.4 10.7 %all_to_all.16 = bf16[16,16,768]{2,1,0:T(8,128)(2,1)S(1)} all-to-all(bf16[16,16,768]{2,1,0:T(8,128)(2,1)S(1)} %broadcast_in_dim.8), channel_id=1, replica_groups=mesh['y'=2,'core'=2,'zh'=2,'zr'=4] {'y','core','zr'}, dimensions={0} | all-to-all | bytes 786432 | tf_op jit(solution)/shard_map/all_to_all | solution.py:87
  115.1 0.0 copy-done
  115.1 0.9 fusion.10
  116.0 0.7 copy.15
  (15 shorter events, 0.2 us)
Async XLA Ops:
  5.5 0.9 copy-start.1
  9.3 51.0 %all-to-all-start = ((bf16[16,144,768]{2,1,0:T(8,128)(2,1)}), bf16[16,144,768]{2,1,0:T(8,128)(2,1)S(1)}, u32[]{:S(2)}, u32[]{:S(2)}) async-start(bf16[16,144,768]{2,1,0:T(8,128)(2,1)} %bitcast.4), calls=%async_computation | async-start | bytes 7077888 | tf_op jit(solution)/shard_map/all_to_all | solution.py:56
  64.0 18.1 %copy-start.2 = (s32[96]{0:T(128)S(1)}, s32[96]{0:T(128)}, u32[]{:S(2)}) copy-start(s32[96]{0:T(128)} %param.9) | copy-start | bytes 1156
  66.1 15.7 %collective-permute-start = (f32[96,768]{1,0:T(8,128)S(1)}, f32[96,768]{1,0:T(8,128)S(1)}, u32[]{:S(2)}, u32[]{:S(2)}) collective-permute-start(f32[96,768]{1,0:T(8,128)S(1)} %slice.25), channel_id=1, source_target_pairs={{0,4},{4,0},{1,5},{5,1},{2,6},{6,2},{3,7},{7,3},{8,12},{12,8},{9,1... | collective-permute-start | bytes 884744 | tf_op jit(solution)/shard_map/ppermute | solution.py:73
  82.1 33.0 %copy-start = (bf16[96,768]{1,0:T(8,128)(2,1)}, bf16[96,768]{1,0:T(8,128)(2,1)S(1)}, u32[]{:S(2)}) copy-start(bf16[96,768]{1,0:T(8,128)(2,1)S(1)} %multiply_convert_fusion) | copy-start | bytes 442372
  97.9 6.3 %collective-permute-start.1 = (f32[16,768]{1,0:T(8,128)S(1)}, f32[16,768]{1,0:T(8,128)S(1)}, u32[]{:S(2)}, u32[]{:S(2)}) collective-permute-start(f32[16,768]{1,0:T(8,128)S(1)} %reduce_sum.38), channel_id=1, source_target_pairs={{0,4},{4,0},{1,5},{5,1},{2,6},{6,2},{3,7},{7,3},{8,12},{12,8},{9,1... | collective-permute-start | bytes 147464 | tf_op jit(solution)/shard_map/ppermute | solution.py:85

commit v6 on v5

--- a/solution.py
+++ b/solution.py
@@ -56,19 +56,18 @@
     got = lax.all_to_all(
         send.reshape(group, span + extra, width), near, split_axis=0, concat_axis=0, tiled=True
     )
-    got_slot = got[:, span, :span].astype(jnp.int32).reshape(devices * capacity) - 1
+    got_slot = jnp.concatenate(
+        [got[:, span, :span].astype(jnp.int32) - 1, jnp.full((group, extra), -1, jnp.int32)], axis=1
+    ).reshape(group * (span + extra))
     got_rows = got.reshape(group * (span + extra), width)
 
     me = lax.axis_index("zh")
-    block = (jnp.arange(devices * capacity, dtype=jnp.int32) // capacity) % 2
-    wanted = jnp.stack([1 - me, me])
-    label_ids = jnp.arange(owned, dtype=jnp.int32)
+    block = (jnp.arange(group * (span + extra), dtype=jnp.int32) % (span + extra)) // capacity
+    row_label = jnp.arange(2 * owned, dtype=jnp.int32) % owned
+    row_block = jnp.where(jnp.arange(2 * owned, dtype=jnp.int32) < owned, 1 - me, me)
     onehot = (
-        (label_ids[None, :, None] == got_slot[None, None, :])
-        & (block[None, None, :] == wanted[:, None, None])
-    ).astype(bf16).reshape(2 * owned, group, span)
-    onehot = jnp.concatenate([onehot, jnp.zeros((2 * owned, group, extra), bf16)], axis=2)
-    onehot = onehot.reshape(2 * owned, group * (span + extra))
+        (row_label[:, None] == got_slot[None, :]) & (row_block[:, None] == block[None, :])
+    ).astype(bf16)
     partial = jnp.dot(onehot, got_rows, preferred_element_type=f32)
     mirrored = lax.ppermute(partial[:owned], "zh", [(0, 1), (1, 0)])
     label_sums = partial[owned:] + mirrored

time: 117 us -> 114 us (0.974)
  local copies, waits for them, and re-layouts: 4.41 us -> 1.72 us
    convert_element_type x1 -> x0, local copies, waits for them, and re-layouts: 2.4 us -> none  [local(): onehot = ((label_ids[None, :, None] == got_slot[None, None, :]) & (block[...]
    select_n x1 -> x2, other arithmetic: 0.01 us -> 1.18 us  [the longest x1 0.62 us: local(): jnp.arange(group * (span + extra), dtype=jnp.int32) % (span + extra) // c...]
  transfers between devices with their start and end apart: 3 -> 3, of which waited for: 3 -> 3; matrix products, arithmetic and copies ran while one was open for 0% -> 1% of each run, Pallas kernels for 0% -> 0%
where the time goes in v6:
time: 114 us; the launch traced here: 113 us
  waiting for transfers between devices  59.6 us (52%)
  blocking collectives  26.2 us (23%)
  starting transfers between devices  12.1 us (11%)
  matrix products  8.49 us (7%)
  other arithmetic  4.44 us (4%)
  local copies, waits for them, and re-layouts  1.72 us (2%)
    all_to_all x1, waiting for transfers between devices, local(): lax.all_to_all(send.reshape(group, span + extra, width), near, split_axis...  43.5 us
    all_to_all x1, blocking collectives, local(): lax.all_to_all(partial_sums.reshape(group, share, width), near, split_axi...  15.5 us
    ppermute x1, waiting for transfers between devices, local(): mirrored = lax.ppermute(partial[:owned], 'zh', [(0, 1), (1, 0)])  13.1 us
    all_to_all x1, blocking collectives, local(): lax.all_to_all(jnp.broadcast_to(own[None], (group, share, width)), near,...  10.7 us
    all_to_all x1, starting transfers between devices, local(): lax.all_to_all(send.reshape(group, span + extra, width), near, split_axis...  6.32 us
    ppermute x1, starting transfers between devices, local(): sums = half_sums + lax.ppermute(half_sums, 'zh', [(0, 1), (1, 0)])  3.17 us
    ppermute x1, waiting for transfers between devices, local(): sums = half_sums + lax.ppermute(half_sums, 'zh', [(0, 1), (1, 0)])  3.07 us
    dot_general x1, matrix products, local(): send = jnp.dot(chooser, table, preferred_element_type=f32).astype(bf16)  2.84 us
  transfers between devices with their start and end apart: 3, of which 3 were waited for; matrix products, arithmetic and copies ran while one was open for 1% of the time, Pallas kernels for 0%

profile of v6, /device:TPU:0, one launch (start us, length us, event | category | flops | bytes accessed | tf_op | source)
XLA Modules:
  0.0 113.4 jit_solution(5911403884852854222)
XLA Ops:
  0.7 1.3 %fusion.10 = f32[1024]{0:T(1024)S(1)} fusion(s32[1024]{0:T(1024)} %bitcast.22), kind=kOutput, calls=%fused_computation.16 | convolution fusion | flops 68353024 | bytes 8192 | tf_op jit(solution)/shard_map/dot_general | solution.py:29
  2.0 0.7 fusion.35
  2.7 0.7 add_convert_fusion.1
  3.4 0.7 add_convert_fusion
  4.1 1.5 %fusion.3 = s32[2048,2]{0,1:T(2,128)S(1)} fusion(s32[1024]{0:T(1024)S(1)} %fusion.35, bf16[1024,1]{0,1:T(2,128)(2,1)S(1)} %stack.13, bf16[1024,1]{0,1:T(2,128)(2,1)S(1)} %stack.12), kind=kOutput, calls=%fused_computation.6 | convolution fusion | flops 10498048 | bytes 24576 | tf_op jit(solution)/shard_map/dot_general | solution.py:39
  5.5 0.0 copy-start.1
  5.6 0.3 iota_compare_fusion.10
  5.9 0.1 pad_convert_fusion
  6.1 0.2 maximum_maximum_fusion
  6.3 0.2 copy-done.1
  6.5 2.8 %convolution_convert_fusion = bf16[2304,768]{1,0:T(8,128)(2,1)} fusion(bf16[2304,256]{1,0:T(8,128)(2,1)S(1)} %bitcast.15, bf16[128,768]{1,0:T(8,128)(2,1)S(1)} %fusion.18, bf16[128,768]{1,0:T(8,128)(2,1)S(1)} %copy-done.1), kind=kOutput, calls=%fused_computation.2 | convolution fusion | flops 908525568 | bytes 5111808 | tf_op jit(solution)/shard_map/dot_general | solution.py:54
  9.3 6.3 %all-to-all-start = ((bf16[16,144,768]{2,1,0:T(8,128)(2,1)}), bf16[16,144,768]{2,1,0:T(8,128)(2,1)S(1)}, u32[]{:S(2)}, u32[]{:S(2)}) async-start(bf16[16,144,768]{2,1,0:T(8,128)(2,1)} %bitcast.4), calls=%async_computation | async-start | bytes 7077888 | tf_op jit(solution)/shard_map/all_to_all | solution.py:56
  15.6 0.6 compare_select_fusion
  16.2 0.6 add_select_fusion
  16.8 43.5 %all-to-all-done = bf16[16,144,768]{2,1,0:T(8,128)(2,1)S(1)} async-done(((bf16[16,144,768]{2,1,0:T(8,128)(2,1)}), bf16[16,144,768]{2,1,0:T(8,128)(2,1)S(1)}, u32[]{:S(2)}, u32[]{:S(2)}) %all-to-all-start) | async-done | bytes 3538976 | tf_op jit(solution)/shard_map/all_to_all | solution.py:56
  60.3 0.7 eq.105
  61.0 0.0 copy-start.2
  61.0 1.7 %fusion.4 = f32[192,768]{1,0:T(8,128)S(1)} fusion(bf16[2304,768]{1,0:T(8,128)(2,1)S(1)} %bitcast.16, s32[2304]{0:T(1024)} %add_select_fusion, s32[2304]{0:T(1024)} %eq.105, s32[192]{0:T(256)} %get-tuple-element.7, s32[192]{0:T(256)} %get-tuple-element.8), kind=kOutput, calls=%fused_computation.7 | convolution fusion | flops 680804352 | bytes 4148736 | tf_op jit(solution)/shard_map/dot_general | solution.py:71
  62.8 2.6 %collective-permute-start = (f32[96,768]{1,0:T(8,128)S(1)}, f32[96,768]{1,0:T(8,128)S(1)}, u32[]{:S(2)}, u32[]{:S(2)}) collective-permute-start(f32[96,768]{1,0:T(8,128)S(1)} %slice.25), channel_id=1, source_target_pairs={{0,4},{4,0},{1,5},{5,1},{2,6},{6,2},{3,7},{7,3},{8,12},{12,8},{9,1... | collective-permute-start | bytes 884744 | tf_op jit(solution)/shard_map/ppermute | solution.py:72
  65.4 13.1 %collective-permute-done = f32[96,768]{1,0:T(8,128)S(1)} collective-permute-done((f32[96,768]{1,0:T(8,128)S(1)}, f32[96,768]{1,0:T(8,128)S(1)}, u32[]{:S(2)}, u32[]{:S(2)}) %collective-permute-start) | collective-permute-done | bytes 294944 | tf_op jit(solution)/shard_map/ppermute | solution.py:72
  78.5 0.1 multiply_reduce_fusion
  78.6 0.1 multiply_convert_fusion
  78.7 0.0 copy-done.2
  78.7 0.0 copy-start
  78.8 0.2 fusion.20
  79.0 15.5 %all_to_all.15 = f32[16,16,768]{2,1,0:T(8,128)S(1)} all-to-all(f32[16,16,768]{2,1,0:T(8,128)S(1)} %bitcast.19), channel_id=1, replica_groups=mesh['y'=2,'core'=2,'zh'=2,'zr'=4] {'y','core','zr'}, dimensions={0} | all-to-all | bytes 1572864 | tf_op jit(solution)/shard_map/all_to_all | solution.py:80
  94.5 3.2 %collective-permute-start.1 = (f32[16,768]{1,0:T(8,128)S(1)}, f32[16,768]{1,0:T(8,128)S(1)}, u32[]{:S(2)}, u32[]{:S(2)}) collective-permute-start(f32[16,768]{1,0:T(8,128)S(1)} %reduce_sum.38), channel_id=1, source_target_pairs={{0,4},{4,0},{1,5},{5,1},{2,6},{6,2},{3,7},{7,3},{8,12},{12,8},{9,1... | collective-permute-start | bytes 147464 | tf_op jit(solution)/shard_map/ppermute | solution.py:84
  97.7 3.1 %collective-permute-done.1 = f32[16,768]{1,0:T(8,128)S(1)} collective-permute-done((f32[16,768]{1,0:T(8,128)S(1)}, f32[16,768]{1,0:T(8,128)S(1)}, u32[]{:S(2)}, u32[]{:S(2)}) %collective-permute-start.1) | collective-permute-done | bytes 49184 | tf_op jit(solution)/shard_map/ppermute | solution.py:84
  100.8 0.1 multiply_reduce_fusion.1
  100.9 0.1 multiply_convert_fusion.1
  101.0 10.7 %all_to_all.16 = bf16[16,16,768]{2,1,0:T(8,128)(2,1)S(1)} all-to-all(bf16[16,16,768]{2,1,0:T(8,128)(2,1)S(1)} %broadcast_in_dim.18), channel_id=1, replica_groups=mesh['y'=2,'core'=2,'zh'=2,'zr'=4] {'y','core','zr'}, dimensions={0} | all-to-all | bytes 786432 | tf_op jit(solution)/shard_map/all_to_all | solution.py:86
  111.7 0.0 copy-done
  111.7 0.9 fusion.9
  112.7 0.7 copy.12
  (15 shorter events, 0.2 us)
Async XLA Ops:
  5.5 0.9 copy-start.1
  9.3 51.0 %all-to-all-start = ((bf16[16,144,768]{2,1,0:T(8,128)(2,1)}), bf16[16,144,768]{2,1,0:T(8,128)(2,1)S(1)}, u32[]{:S(2)}, u32[]{:S(2)}) async-start(bf16[16,144,768]{2,1,0:T(8,128)(2,1)} %bitcast.4), calls=%async_computation | async-start | bytes 7077888 | tf_op jit(solution)/shard_map/all_to_all | solution.py:56
  61.0 17.7 %copy-start.2 = (s32[96]{0:T(128)S(1)}, s32[96]{0:T(128)}, u32[]{:S(2)}) copy-start(s32[96]{0:T(128)} %param.9) | copy-start | bytes 1156
  62.8 15.7 %collective-permute-start = (f32[96,768]{1,0:T(8,128)S(1)}, f32[96,768]{1,0:T(8,128)S(1)}, u32[]{:S(2)}, u32[]{:S(2)}) collective-permute-start(f32[96,768]{1,0:T(8,128)S(1)} %slice.25), channel_id=1, source_target_pairs={{0,4},{4,0},{1,5},{5,1},{2,6},{6,2},{3,7},{7,3},{8,12},{12,8},{9,1... | collective-permute-start | bytes 884744 | tf_op jit(solution)/shard_map/ppermute | solution.py:72
  78.7 33.0 %copy-start = (bf16[96,768]{1,0:T(8,128)(2,1)}, bf16[96,768]{1,0:T(8,128)(2,1)S(1)}, u32[]{:S(2)}) copy-start(bf16[96,768]{1,0:T(8,128)(2,1)S(1)} %multiply_convert_fusion) | copy-start | bytes 442372
  94.5 6.2 %collective-permute-start.1 = (f32[16,768]{1,0:T(8,128)S(1)}, f32[16,768]{1,0:T(8,128)S(1)}, u32[]{:S(2)}, u32[]{:S(2)}) collective-permute-start(f32[16,768]{1,0:T(8,128)S(1)} %reduce_sum.38), channel_id=1, source_target_pairs={{0,4},{4,0},{1,5},{5,1},{2,6},{6,2},{3,7},{7,3},{8,12},{12,8},{9,1... | collective-permute-start | bytes 147464 | tf_op jit(solution)/shard_map/ppermute | solution.py:84

commit v7 on v5

--- a/solution.py
+++ b/solution.py
@@ -32,46 +32,61 @@
     o_row, o_col = owner // cols, owner % cols
     o_zh, o_zr = o_col // halves, o_col % halves
     proxy = o_row * halves + o_zr
-    position = proxy * (2 * capacity) + o_zh * capacity + rank
+    me = lax.axis_index("zh")
+    later = (o_zh == me).astype(jnp.int32)
+    position = later * (group * capacity) + proxy * capacity + rank
 
     place = (jnp.arange(devices * capacity, dtype=jnp.int32)[:, None] == position[None, :]).astype(bf16)
-    tags = jnp.stack([pair_doc + 1, pair_slot + 1], axis=1).astype(bf16)
+    tags = (jnp.stack([pair_doc, pair_slot], axis=1) + 1).astype(bf16)
     picked = jnp.dot(place, tags, preferred_element_type=f32).astype(jnp.int32)
     send_doc, slot_plus = picked[:, 0] - 1, picked[:, 1]
+    first_doc, second_doc = send_doc[: group * capacity], send_doc[group * capacity :]
 
-    span, extra = 2 * capacity, 16
-    doc_part = (send_doc[:, None] == jnp.arange(docs, dtype=jnp.int32)[None, :]).astype(bf16)
+    extra = 16
+    doc_part = (first_doc[:, None] == jnp.arange(docs, dtype=jnp.int32)[None, :]).astype(bf16)
     doc_part = jnp.concatenate(
-        [doc_part.reshape(group, span, docs), jnp.zeros((group, extra, docs), bf16)], axis=1
+        [doc_part.reshape(group, capacity, docs), jnp.zeros((group, extra, docs), bf16)], axis=1
     )
-    slot_row = slot_plus.astype(bf16).reshape(group, 1, span)
+    slot_row = slot_plus.astype(bf16).reshape(2, group, capacity).transpose(1, 0, 2)
+    slot_row = slot_row.reshape(group, 1, 2 * capacity)
     slot_part = jnp.concatenate(
-        [jnp.zeros((group, span, span), bf16), slot_row, jnp.zeros((group, extra - 1, span), bf16)],
+        [
+            jnp.zeros((group, capacity, 2 * capacity), bf16),
+            slot_row,
+            jnp.zeros((group, extra - 1, 2 * capacity), bf16),
+        ],
         axis=1,
     )
-    chooser = jnp.concatenate([doc_part, slot_part], axis=2).reshape(group * (span + extra), docs + span)
-    table = jnp.concatenate([doc_embed, jnp.eye(span, width, dtype=bf16)], axis=0)
-    send = jnp.dot(chooser, table, preferred_element_type=f32).astype(bf16)
+    chooser = jnp.concatenate([doc_part, slot_part], axis=2)
+    chooser = chooser.reshape(group * (capacity + extra), docs + 2 * capacity)
+    table = jnp.concatenate([doc_embed, jnp.eye(2 * capacity, width, dtype=bf16)], axis=0)
+    send_first = jnp.dot(chooser, table, preferred_element_type=f32).astype(bf16)
+    pick = (second_doc[:, None] == jnp.arange(docs, dtype=jnp.int32)[None, :]).astype(bf16)
+    send_second = jnp.dot(pick, doc_embed, preferred_element_type=f32).astype(bf16)
 
-    got = lax.all_to_all(
-        send.reshape(group, span + extra, width), near, split_axis=0, concat_axis=0, tiled=True
+    got_first = lax.all_to_all(
+        send_first.reshape(group, capacity + extra, width), near, split_axis=0, concat_axis=0, tiled=True
     )
-    got_slot = got[:, span, :span].astype(jnp.int32).reshape(devices * capacity) - 1
-    got_rows = got.reshape(group * (span + extra), width)
+    got_second = lax.all_to_all(
+        send_second.reshape(group, capacity, width), near, split_axis=0, concat_axis=0, tiled=True
+    )
+    slots = got_first[:, capacity, : 2 * capacity].astype(jnp.int32) - 1
+    first_slot = jnp.concatenate(
+        [slots[:, :capacity], jnp.full((group, extra), -1, jnp.int32)], axis=1
+    ).reshape(group * (capacity + extra))
+    second_slot = slots[:, capacity:].reshape(group * capacity)
 
-    me = lax.axis_index("zh")
-    block = (jnp.arange(devices * capacity, dtype=jnp.int32) // capacity) % 2
-    wanted = jnp.stack([1 - me, me])
     label_ids = jnp.arange(owned, dtype=jnp.int32)
-    onehot = (
-        (label_ids[None, :, None] == got_slot[None, None, :])
-        & (block[None, None, :] == wanted[:, None, None])
-    ).astype(bf16).reshape(2 * owned, group, span)
-    onehot = jnp.concatenate([onehot, jnp.zeros((2 * owned, group, extra), bf16)], axis=2)
-    onehot = onehot.reshape(2 * owned, group * (span + extra))
-    partial = jnp.dot(onehot, got_rows, preferred_element_type=f32)
-    mirrored = lax.ppermute(partial[:owned], "zh", [(0, 1), (1, 0)])
-    label_sums = partial[owned:] + mirrored
+    first_hot = (label_ids[:, None] == first_slot[None, :]).astype(bf16)
+    mirror_part = jnp.dot(
+        first_hot, got_first.reshape(group * (capacity + extra), width), preferred_element_type=f32
+    )
+    mirrored = lax.ppermute(mirror_part, "zh", [(0, 1), (1, 0)])
+    second_hot = (label_ids[:, None] == second_slot[None, :]).astype(bf16)
+    own_part = jnp.dot(
+        second_hot, got_second.reshape(group * capacity, width), preferred_element_type=f32
+    )
+    label_sums = own_part + mirrored
     label_vectors = rms_scale(label_sums).astype(bf16)
     members = (jnp.arange(CLUSTERS, dtype=jnp.int32)[:, None] == label_cluster[None, :]).astype(bf16)
     partial_sums = jnp.dot(members, label_vectors, preferred_element_type=f32)

time: 117 us -> 108 us (0.923)
  waiting for transfers between devices: 60.6 us -> 51 us
  local copies, waits for them, and re-layouts: 4.41 us -> 2.15 us
  blocking collectives: 26.2 us -> 28.2 us
  other arithmetic: 3.76 us -> 2.11 us
  matrix products: 8.81 us -> 10 us
    ppermute x1, waiting for transfers between devices: 13.1 us -> 0.01 us  [local(): mirrored = lax.ppermute(mirror_part, 'zh', [(0, 1), (1, 0)])]
    all_to_all x1 -> x2, starting transfers between devices: 6.32 us -> 10 us  [the longest x1 6.32 us: local(): lax.all_to_all(send_first.reshape(group, capacity + extra, width), near,...]
    ppermute x1, starting transfers between devices: 3.18 us -> 0.57 us  [local(): sums = half_sums + lax.ppermute(half_sums, 'zh', [(0, 1), (1, 0)])]
    convert_element_type x1 -> x2, local copies, waits for them, and re-layouts: 2.4 us -> 0.09 us  [local(): slot_plus.astype(bf16).reshape(2, group, capacity).transpose(1, 0, 2)]
    ppermute x1, waiting for transfers between devices: 3.07 us -> 5.2 us  [local(): sums = half_sums + lax.ppermute(half_sums, 'zh', [(0, 1), (1, 0)])]
    all_to_all x1, blocking collectives: 15.5 us -> 17.5 us  [local(): lax.all_to_all(partial_sums.reshape(group, share, width), near, split_axi...]
    another operation x3 -> x0, other arithmetic: 1.46 us -> none
    all_to_all x1 -> x2, waiting for transfers between devices: 44.5 us -> 45.8 us  [the longest x1 23.9 us: local(): lax.all_to_all(send_first.reshape(group, capacity + extra, width), near,...]
  transfers between devices with their start and end apart: 3 -> 4, of which waited for: 3 -> 3; matrix products, arithmetic and copies ran while one was open for 0% -> 4% of each run, Pallas kernels for 0% -> 0%
where the time goes in v7:
time: 108 us; the launch traced here: 107 us
  waiting for transfers between devices  51 us (47%)
  blocking collectives  28.2 us (26%)
  starting transfers between devices  13.2 us (12%)
  matrix products  10 us (9%)
  local copies, waits for them, and re-layouts  2.15 us (2%)
  other arithmetic  2.11 us (2%)
    all_to_all x1, waiting for transfers between devices, local(): lax.all_to_all(send_first.reshape(group, capacity + extra, width), near,...  23.9 us
    all_to_all x1, waiting for transfers between devices, local(): lax.all_to_all(send_second.reshape(group, capacity, width), near, split_a...  21.9 us
    all_to_all x1, blocking collectives, local(): lax.all_to_all(partial_sums.reshape(group, share, width), near, split_axi...  17.5 us
    all_to_all x1, blocking collectives, local(): lax.all_to_all(jnp.broadcast_to(own[None], (group, share, width)), near,...  10.7 us
    all_to_all x1, starting transfers between devices, local(): lax.all_to_all(send_first.reshape(group, capacity + extra, width), near,...  6.32 us
    ppermute x1, waiting for transfers between devices, local(): sums = half_sums + lax.ppermute(half_sums, 'zh', [(0, 1), (1, 0)])  5.2 us
    all_to_all x1, starting transfers between devices, local(): lax.all_to_all(send_second.reshape(group, capacity, width), near, split_a...  3.71 us
    ppermute x1, starting transfers between devices, local(): mirrored = lax.ppermute(mirror_part, 'zh', [(0, 1), (1, 0)])  2.58 us
  transfers between devices with their start and end apart: 4, of which 3 were waited for; matrix products, arithmetic and copies ran while one was open for 4% of the time, Pallas kernels for 0%

profile of v7, /device:TPU:0, one launch (start us, length us, event | category | flops | bytes accessed | tf_op | source)
XLA Modules:
  0.0 107.4 jit_solution(7719431698614894145)
XLA Ops:
  0.6 1.3 %fusion.6 = f32[1024]{0:T(1024)S(1)} fusion(s32[1024]{0:T(1024)} %bitcast.34), kind=kOutput, calls=%fused_computation.12 | convolution fusion | flops 68353024 | bytes 8192 | tf_op jit(solution)/shard_map/dot_general | solution.py:29
  1.9 0.7 fusion.28
  2.7 2.2 %fusion.3 = s32[2048,2]{0,1:T(2,128)S(1)} fusion(s32[1024]{0:T(1024)S(1)} %fusion.28, s32[1024,1]{0,1:T(1,128)} %bitcast.36, s32[1024,1]{0,1:T(1,128)} %bitcast.37), kind=kOutput, calls=%fused_computation.6 | convolution fusion | flops 10496000 | bytes 28672 | tf_op jit(solution)/shard_map/dot_general | solution.py:41
  4.8 0.0 copy-start.1
  4.9 0.1 convert_element_type.57
  5.0 0.1 reshape.167
  5.1 0.1 slice.32
  5.2 0.2 iota_compare_fusion.11
  5.4 0.1 pad_convert_fusion
  5.5 0.1 maximum_maximum_fusion
  5.6 0.2 copy-done.1
  5.8 2.0 %convolution_convert_fusion = bf16[1280,768]{1,0:T(8,128)(2,1)} fusion(bf16[1280,256]{1,0:T(8,128)(2,1)S(1)} %bitcast.29, bf16[128,768]{1,0:T(8,128)(2,1)S(1)} %fusion.11, bf16[128,768]{1,0:T(8,128)(2,1)S(1)} %copy-done.1), kind=kOutput, calls=%fused_computation.5 | convolution fusion | flops 505085952 | bytes 3014656 | tf_op jit(solution)/shard_map/dot_general | solution.py:63
  7.7 6.3 %all-to-all-start = ((bf16[16,80,768]{2,1,0:T(8,128)(2,1)}), bf16[16,80,768]{2,1,0:T(8,128)(2,1)S(1)}, u32[]{:S(2)}, u32[]{:S(2)}) async-start(bf16[16,80,768]{2,1,0:T(8,128)(2,1)} %bitcast.23), calls=%async_computation | async-start | bytes 3932160 | tf_op jit(solution)/shard_map/all_to_all | solution.py:67
  14.1 1.8 %convolution_convert_fusion.1 = bf16[1024,768]{1,0:T(8,128)(2,1)} fusion(bf16[128,768]{1,0:T(8,128)(2,1)S(1)} %copy-done.1, s32[1024]{0:T(1024)S(1)} %bitcast.33), kind=kOutput, calls=%fused_computation.7 | convolution fusion | flops 202244096 | bytes 1773568 | tf_op jit(solution)/shard_map/dot_general | solution.py:65
  15.8 0.0 copy-start.3
  15.8 23.9 %all-to-all-done = bf16[16,80,768]{2,1,0:T(8,128)(2,1)S(1)} async-done(((bf16[16,80,768]{2,1,0:T(8,128)(2,1)}), bf16[16,80,768]{2,1,0:T(8,128)(2,1)S(1)}, u32[]{:S(2)}, u32[]{:S(2)}) %all-to-all-start) | async-done | bytes 1966112 | tf_op jit(solution)/shard_map/all_to_all | solution.py:67
  39.7 3.7 %all-to-all-start.1 = ((bf16[16,64,768]{2,1,0:T(8,128)(2,1)}), bf16[16,64,768]{2,1,0:T(8,128)(2,1)S(1)}, u32[]{:S(2)}, u32[]{:S(2)}) async-start(bf16[16,64,768]{2,1,0:T(8,128)(2,1)} %bitcast.25), calls=%async_computation.1 | async-start | bytes 3145728 | tf_op jit(solution)/shard_map/all_to_all | solution.py:70
  43.5 0.0 copy-done.3
  43.5 0.6 slice_select_fusion
  44.1 0.8 eq.132
  44.8 1.2 %fusion.7 = f32[96,768]{1,0:T(8,128)} fusion(bf16[1280,768]{1,0:T(8,128)(2,1)S(1)} %bitcast.22, s32[1280]{0:T(1024)S(1)} %eq.132), kind=kOutput, calls=%fused_computation.18 | convolution fusion | flops 188866560 | bytes 2266112 | tf_op jit(solution)/shard_map/dot_general | solution.py:81
  46.0 0.0 copy-start.2
  46.0 2.6 %collective-permute-start = (f32[96,768]{1,0:T(8,128)}, f32[96,768]{1,0:T(8,128)S(1)}, u32[]{:S(2)}, u32[]{:S(2)}) collective-permute-start(f32[96,768]{1,0:T(8,128)} %fusion.7), channel_id=1, source_target_pairs={{0,4},{4,0},{1,5},{5,1},{2,6},{6,2},{3,7},{7,3},{8,12},{12,8},{9,1... | collective-permute-start | bytes 884744 | tf_op jit(solution)/shard_map/ppermute | solution.py:84
  48.6 0.1 slice.43
  48.7 0.1 eq.125
  48.7 21.9 %all-to-all-done.1 = bf16[16,64,768]{2,1,0:T(8,128)(2,1)S(1)} async-done(((bf16[16,64,768]{2,1,0:T(8,128)(2,1)}), bf16[16,64,768]{2,1,0:T(8,128)(2,1)S(1)}, u32[]{:S(2)}, u32[]{:S(2)}) %all-to-all-start.1) | async-done | bytes 1572896 | tf_op jit(solution)/shard_map/all_to_all | solution.py:70
  70.6 0.0 collective-permute-done
  70.6 0.5 multiply_reduce_fusion
  71.1 0.1 multiply_convert_fusion
  71.2 0.0 copy-done.2
  71.2 0.0 copy-start
  71.3 0.2 fusion.16
  71.5 17.5 %all_to_all.20 = f32[16,16,768]{2,1,0:T(8,128)S(1)} all-to-all(f32[16,16,768]{2,1,0:T(8,128)S(1)} %bitcast.28), channel_id=1, replica_groups=mesh['y'=2,'core'=2,'zh'=2,'zr'=4] {'y','core','zr'}, dimensions={0} | all-to-all | bytes 1572864 | tf_op jit(solution)/shard_map/all_to_all | solution.py:96
  89.0 0.6 collective-permute-start.1
  89.6 5.2 %collective-permute-done.1 = f32[16,768]{1,0:T(8,128)S(1)} collective-permute-done((f32[16,768]{1,0:T(8,128)S(1)}, f32[16,768]{1,0:T(8,128)S(1)}, u32[]{:S(2)}, u32[]{:S(2)}) %collective-permute-start.1) | collective-permute-done | bytes 49184 | tf_op jit(solution)/shard_map/ppermute | solution.py:100
  94.8 0.1 multiply_reduce_fusion.1
  94.9 0.1 multiply_convert_fusion.1
  95.1 10.7 %all_to_all.21 = bf16[16,16,768]{2,1,0:T(8,128)(2,1)S(1)} all-to-all(bf16[16,16,768]{2,1,0:T(8,128)(2,1)S(1)} %broadcast_in_dim.8), channel_id=1, replica_groups=mesh['y'=2,'core'=2,'zh'=2,'zr'=4] {'y','core','zr'}, dimensions={0} | all-to-all | bytes 786432 | tf_op jit(solution)/shard_map/all_to_all | solution.py:102
  105.8 0.0 copy-done
  105.8 0.9 fusion.5
  106.7 0.7 copy.15
  (14 shorter events, 0.2 us)
Async XLA Ops:
  4.8 0.9 copy-start.1
  7.7 32.0 %all-to-all-start = ((bf16[16,80,768]{2,1,0:T(8,128)(2,1)}), bf16[16,80,768]{2,1,0:T(8,128)(2,1)S(1)}, u32[]{:S(2)}, u32[]{:S(2)}) async-start(bf16[16,80,768]{2,1,0:T(8,128)(2,1)} %bitcast.23), calls=%async_computation | async-start | bytes 3932160 | tf_op jit(solution)/shard_map/all_to_all | solution.py:67
  15.8 27.6 %copy-start.3 = (pred[80]{0:T(512)(128)(4,1)S(1)}, pred[80]{0:T(512)(128)(4,1)}, u32[]{:S(2)}) copy-start(pred[80]{0:T(512)(128)(4,1)} %constant.83.clone.1) | copy-start | bytes 244
  39.7 30.9 %all-to-all-start.1 = ((bf16[16,64,768]{2,1,0:T(8,128)(2,1)}), bf16[16,64,768]{2,1,0:T(8,128)(2,1)S(1)}, u32[]{:S(2)}, u32[]{:S(2)}) async-start(bf16[16,64,768]{2,1,0:T(8,128)(2,1)} %bitcast.25), calls=%async_computation.1 | async-start | bytes 3145728 | tf_op jit(solution)/shard_map/all_to_all | solution.py:70
  46.0 25.2 %copy-start.2 = (s32[96]{0:T(128)S(1)}, s32[96]{0:T(128)}, u32[]{:S(2)}) copy-start(s32[96]{0:T(128)} %param.9) | copy-start | bytes 1156
  46.0 24.6 %collective-permute-start = (f32[96,768]{1,0:T(8,128)}, f32[96,768]{1,0:T(8,128)S(1)}, u32[]{:S(2)}, u32[]{:S(2)}) collective-permute-start(f32[96,768]{1,0:T(8,128)} %fusion.7), channel_id=1, source_target_pairs={{0,4},{4,0},{1,5},{5,1},{2,6},{6,2},{3,7},{7,3},{8,12},{12,8},{9,1... | collective-permute-start | bytes 884744 | tf_op jit(solution)/shard_map/ppermute | solution.py:84
  71.2 34.5 %copy-start = (bf16[96,768]{1,0:T(8,128)(2,1)}, bf16[96,768]{1,0:T(8,128)(2,1)S(1)}, u32[]{:S(2)}) copy-start(bf16[96,768]{1,0:T(8,128)(2,1)S(1)} %multiply_convert_fusion) | copy-start | bytes 442372
  89.0 5.8 %collective-permute-start.1 = (f32[16,768]{1,0:T(8,128)S(1)}, f32[16,768]{1,0:T(8,128)S(1)}, u32[]{:S(2)}, u32[]{:S(2)}) collective-permute-start(f32[16,768]{1,0:T(8,128)S(1)} %reduce_sum.38), channel_id=1, source_target_pairs={{0,4},{4,0},{1,5},{5,1},{2,6},{6,2},{3,7},{7,3},{8,12},{12,8},{9,1... | collective-permute-start | bytes 147464 | tf_op jit(solution)/shard_map/ppermute | solution.py:100

commit v8 on v7

--- a/solution.py
+++ b/solution.py
@@ -92,16 +92,24 @@
     partial_sums = jnp.dot(members, label_vectors, preferred_element_type=f32)
 
     if CLUSTERS % group == 0:
+        chips = ("y", "zr")
+        count = group // 2
         share = CLUSTERS // group
+        pair = lax.all_to_all(
+            partial_sums.reshape(2, CLUSTERS // 2, width), "core", split_axis=0, concat_axis=0, tiled=True
+        )
         parts = lax.all_to_all(
-            partial_sums.reshape(group, share, width), near, split_axis=0, concat_axis=0, tiled=True
+            jnp.sum(pair, axis=0).reshape(count, share, width), chips, split_axis=0, concat_axis=0, tiled=True
         )
         half_sums = jnp.sum(parts, axis=0)
         sums = half_sums + lax.ppermute(half_sums, "zh", [(0, 1), (1, 0)])
         own = rms_scale(sums).astype(bf16)
+        core_c = lax.all_to_all(
+            jnp.broadcast_to(own[None], (count, share, width)), chips, split_axis=0, concat_axis=0, tiled=True
+        ).reshape(CLUSTERS // 2, width)
         centroids = lax.all_to_all(
-            jnp.broadcast_to(own[None], (group, share, width)),
-            near,
+            jnp.broadcast_to(core_c[None], (2, CLUSTERS // 2, width)),
+            "core",
             split_axis=0,
             concat_axis=0,
             tiled=True,

time: 108 us -> 110 us (1.019)
  blocking collectives: 28.2 us -> 30.6 us
    all_to_all x2 -> x4, blocking collectives: 28.2 us -> 30.6 us  [the longest x1 13.2 us: local(): lax.all_to_all(jnp.sum(pair, axis=0).reshape(count, share, width), chips,...]
where the time goes in v8:
time: 110 us
  waiting for transfers between devices  50.7 us (46%)
  blocking collectives  30.6 us (28%)
  starting transfers between devices  13.2 us (12%)
  matrix products  10 us (9%)
  local copies, waits for them, and re-layouts  2.16 us (2%)
  other arithmetic  2.14 us (2%)
    all_to_all x1, waiting for transfers between devices, local(): lax.all_to_all(send_first.reshape(group, capacity + extra, width), near,...  23.9 us
    all_to_all x1, waiting for transfers between devices, local(): lax.all_to_all(send_second.reshape(group, capacity, width), near, split_a...  21.9 us
    all_to_all x1, blocking collectives, local(): lax.all_to_all(jnp.sum(pair, axis=0).reshape(count, share, width), chips,...  13.2 us
    all_to_all x1, blocking collectives, local(): lax.all_to_all(jnp.broadcast_to(own[None], (count, share, width)), chips,...  9.02 us
    all_to_all x1, starting transfers between devices, local(): lax.all_to_all(send_first.reshape(group, capacity + extra, width), near,...  6.32 us
    ppermute x1, waiting for transfers between devices, local(): sums = half_sums + lax.ppermute(half_sums, 'zh', [(0, 1), (1, 0)])  4.87 us
    all_to_all x1, blocking collectives, local(): lax.all_to_all(partial_sums.reshape(2, CLUSTERS // 2, width), 'core', spl...  4.37 us
    all_to_all x1, blocking collectives, local(): lax.all_to_all(jnp.broadcast_to(core_c[None], (2, CLUSTERS // 2, width)),...  4.05 us
  transfers between devices with their start and end apart: 4, of which 3 were waited for; matrix products, arithmetic and copies ran while one was open for 4% of the time, Pallas kernels for 0%

profile of v8, /device:TPU:0, one launch (start us, length us, event | category | flops | bytes accessed | tf_op | source)
XLA Modules:
  0.0 109.6 jit_solution(11184331683265767432)
XLA Ops:
  0.6 1.3 %fusion.6 = f32[1024]{0:T(1024)S(1)} fusion(s32[1024]{0:T(1024)} %bitcast.38), kind=kOutput, calls=%fused_computation.12 | convolution fusion | flops 68353024 | bytes 8192 | tf_op jit(solution)/shard_map/dot_general | solution.py:29
  1.9 0.7 fusion.28
  2.7 2.2 %fusion.3 = s32[2048,2]{0,1:T(2,128)S(1)} fusion(s32[1024]{0:T(1024)S(1)} %fusion.28, s32[1024,1]{0,1:T(1,128)} %bitcast.40, s32[1024,1]{0,1:T(1,128)} %bitcast.41), kind=kOutput, calls=%fused_computation.6 | convolution fusion | flops 10496000 | bytes 28672 | tf_op jit(solution)/shard_map/dot_general | solution.py:41
  4.8 0.0 copy-start.1
  4.9 0.1 convert_element_type.57
  5.0 0.1 reshape.172
  5.1 0.1 slice.32
  5.2 0.2 iota_compare_fusion.11
  5.4 0.1 pad_convert_fusion
  5.5 0.1 maximum_maximum_fusion
  5.6 0.2 copy-done.1
  5.8 2.0 %convolution_convert_fusion = bf16[1280,768]{1,0:T(8,128)(2,1)} fusion(bf16[1280,256]{1,0:T(8,128)(2,1)S(1)} %bitcast.31, bf16[128,768]{1,0:T(8,128)(2,1)S(1)} %fusion.11, bf16[128,768]{1,0:T(8,128)(2,1)S(1)} %copy-done.1), kind=kOutput, calls=%fused_computation.5 | convolution fusion | flops 505085952 | bytes 3014656 | tf_op jit(solution)/shard_map/dot_general | solution.py:63
  7.7 6.3 %all-to-all-start = ((bf16[16,80,768]{2,1,0:T(8,128)(2,1)}), bf16[16,80,768]{2,1,0:T(8,128)(2,1)S(1)}, u32[]{:S(2)}, u32[]{:S(2)}) async-start(bf16[16,80,768]{2,1,0:T(8,128)(2,1)} %bitcast.25), calls=%async_computation | async-start | bytes 3932160 | tf_op jit(solution)/shard_map/all_to_all | solution.py:67
  14.1 1.8 %convolution_convert_fusion.1 = bf16[1024,768]{1,0:T(8,128)(2,1)} fusion(bf16[128,768]{1,0:T(8,128)(2,1)S(1)} %copy-done.1, s32[1024]{0:T(1024)S(1)} %bitcast.37), kind=kOutput, calls=%fused_computation.7 | convolution fusion | flops 202244096 | bytes 1773568 | tf_op jit(solution)/shard_map/dot_general | solution.py:65
  15.8 0.0 copy-start.3
  15.8 23.9 %all-to-all-done = bf16[16,80,768]{2,1,0:T(8,128)(2,1)S(1)} async-done(((bf16[16,80,768]{2,1,0:T(8,128)(2,1)}), bf16[16,80,768]{2,1,0:T(8,128)(2,1)S(1)}, u32[]{:S(2)}, u32[]{:S(2)}) %all-to-all-start) | async-done | bytes 1966112 | tf_op jit(solution)/shard_map/all_to_all | solution.py:67
  39.7 3.7 %all-to-all-start.1 = ((bf16[16,64,768]{2,1,0:T(8,128)(2,1)}), bf16[16,64,768]{2,1,0:T(8,128)(2,1)S(1)}, u32[]{:S(2)}, u32[]{:S(2)}) async-start(bf16[16,64,768]{2,1,0:T(8,128)(2,1)} %bitcast.27), calls=%async_computation.1 | async-start | bytes 3145728 | tf_op jit(solution)/shard_map/all_to_all | solution.py:70
  43.5 0.0 copy-done.3
  43.5 0.6 slice_select_fusion
  44.1 0.8 eq.132
  44.8 1.2 %fusion.7 = f32[96,768]{1,0:T(8,128)} fusion(bf16[1280,768]{1,0:T(8,128)(2,1)S(1)} %bitcast.24, s32[1280]{0:T(1024)S(1)} %eq.132), kind=kOutput, calls=%fused_computation.18 | convolution fusion | flops 188866560 | bytes 2266112 | tf_op jit(solution)/shard_map/dot_general | solution.py:81
  46.0 0.0 copy-start.2
  46.0 2.6 %collective-permute-start = (f32[96,768]{1,0:T(8,128)}, f32[96,768]{1,0:T(8,128)S(1)}, u32[]{:S(2)}, u32[]{:S(2)}) collective-permute-start(f32[96,768]{1,0:T(8,128)} %fusion.7), channel_id=1, source_target_pairs={{0,4},{4,0},{1,5},{5,1},{2,6},{6,2},{3,7},{7,3},{8,12},{12,8},{9,1... | collective-permute-start | bytes 884744 | tf_op jit(solution)/shard_map/ppermute | solution.py:84
  48.6 0.1 slice.43
  48.7 0.1 eq.125
  48.7 21.9 %all-to-all-done.1 = bf16[16,64,768]{2,1,0:T(8,128)(2,1)S(1)} async-done(((bf16[16,64,768]{2,1,0:T(8,128)(2,1)}), bf16[16,64,768]{2,1,0:T(8,128)(2,1)S(1)}, u32[]{:S(2)}, u32[]{:S(2)}) %all-to-all-start.1) | async-done | bytes 1572896 | tf_op jit(solution)/shard_map/all_to_all | solution.py:70
  70.6 0.0 collective-permute-done
  70.6 0.5 multiply_reduce_fusion
  71.1 0.1 multiply_convert_fusion
  71.2 0.0 copy-done.2
  71.2 0.0 copy-start
  71.3 0.2 fusion.16
  71.5 4.4 %all_to_all.30 = f32[2,128,768]{2,1,0:T(8,128)S(1)} all-to-all(f32[2,128,768]{2,1,0:T(8,128)S(1)} %bitcast.30), channel_id=1, replica_groups=mesh['y'=2,'core'=2,'zh'=2,'zr'=4] {'core'}, dimensions={0} | all-to-all | bytes 1572864 | tf_op jit(solution)/shard_map/all_to_all | solution.py:98
  75.9 0.1 reduce_sum.47
  75.9 13.2 %all_to_all.31 = f32[8,16,768]{2,1,0:T(8,128)S(1)} all-to-all(f32[8,16,768]{2,1,0:T(8,128)S(1)} %bitcast.32), channel_id=1, replica_groups=mesh['y'=2,'core'=2,'zh'=2,'zr'=4] {'y','zr'}, dimensions={0} | all-to-all | bytes 786432 | tf_op jit(solution)/shard_map/all_to_all | solution.py:101
  89.2 0.6 collective-permute-start.1
  89.7 4.9 %collective-permute-done.1 = f32[16,768]{1,0:T(8,128)S(1)} collective-permute-done((f32[16,768]{1,0:T(8,128)S(1)}, f32[16,768]{1,0:T(8,128)S(1)}, u32[]{:S(2)}, u32[]{:S(2)}) %collective-permute-start.1) | collective-permute-done | bytes 49184 | tf_op jit(solution)/shard_map/ppermute | solution.py:105
  94.6 0.1 multiply_reduce_fusion.1
  94.7 0.1 multiply_convert_fusion.1
  94.8 9.0 %all_to_all.32 = bf16[8,16,768]{2,1,0:T(8,128)(2,1)S(1)} all-to-all(bf16[8,16,768]{2,1,0:T(8,128)(2,1)S(1)} %broadcast_in_dim.12), channel_id=1, replica_groups=mesh['y'=2,'core'=2,'zh'=2,'zr'=4] {'y','zr'}, dimensions={0} | all-to-all | bytes 393216 | tf_op jit(solution)/shard_map/all_to_all | solution.py:107
  103.9 4.0 %all_to_all.33 = bf16[2,128,768]{2,1,0:T(8,128)(2,1)S(1)} all-to-all(bf16[2,128,768]{2,1,0:T(8,128)(2,1)S(1)} %broadcast_in_dim.14), channel_id=1, replica_groups=mesh['y'=2,'core'=2,'zh'=2,'zr'=4] {'core'}, dimensions={0} | all-to-all | bytes 786432 | tf_op jit(solution)/shard_map/all_to_all | solution.py:110
  107.9 0.0 copy-done
  107.9 0.9 fusion.5
  108.9 0.7 copy.15
  (15 shorter events, 0.2 us)
Async XLA Ops:
  4.8 0.9 copy-start.1
  7.7 32.0 %all-to-all-start = ((bf16[16,80,768]{2,1,0:T(8,128)(2,1)}), bf16[16,80,768]{2,1,0:T(8,128)(2,1)S(1)}, u32[]{:S(2)}, u32[]{:S(2)}) async-start(bf16[16,80,768]{2,1,0:T(8,128)(2,1)} %bitcast.25), calls=%async_computation | async-start | bytes 3932160 | tf_op jit(solution)/shard_map/all_to_all | solution.py:67
  15.8 27.6 %copy-start.3 = (pred[80]{0:T(512)(128)(4,1)S(1)}, pred[80]{0:T(512)(128)(4,1)}, u32[]{:S(2)}) copy-start(pred[80]{0:T(512)(128)(4,1)} %constant.83.clone.1) | copy-start | bytes 244
  39.7 30.9 %all-to-all-start.1 = ((bf16[16,64,768]{2,1,0:T(8,128)(2,1)}), bf16[16,64,768]{2,1,0:T(8,128)(2,1)S(1)}, u32[]{:S(2)}, u32[]{:S(2)}) async-start(bf16[16,64,768]{2,1,0:T(8,128)(2,1)} %bitcast.27), calls=%async_computation.1 | async-start | bytes 3145728 | tf_op jit(solution)/shard_map/all_to_all | solution.py:70
  46.0 25.2 %copy-start.2 = (s32[96]{0:T(128)S(1)}, s32[96]{0:T(128)}, u32[]{:S(2)}) copy-start(s32[96]{0:T(128)} %param.9) | copy-start | bytes 1156
  46.0 24.6 %collective-permute-start = (f32[96,768]{1,0:T(8,128)}, f32[96,768]{1,0:T(8,128)S(1)}, u32[]{:S(2)}, u32[]{:S(2)}) collective-permute-start(f32[96,768]{1,0:T(8,128)} %fusion.7), channel_id=1, source_target_pairs={{0,4},{4,0},{1,5},{5,1},{2,6},{6,2},{3,7},{7,3},{8,12},{12,8},{9,1... | collective-permute-start | bytes 884744 | tf_op jit(solution)/shard_map/ppermute | solution.py:84
  71.2 36.7 %copy-start = (bf16[96,768]{1,0:T(8,128)(2,1)}, bf16[96,768]{1,0:T(8,128)(2,1)S(1)}, u32[]{:S(2)}) copy-start(bf16[96,768]{1,0:T(8,128)(2,1)S(1)} %multiply_convert_fusion) | copy-start | bytes 442372
  89.2 5.4 %collective-permute-start.1 = (f32[16,768]{1,0:T(8,128)S(1)}, f32[16,768]{1,0:T(8,128)S(1)}, u32[]{:S(2)}, u32[]{:S(2)}) collective-permute-start(f32[16,768]{1,0:T(8,128)S(1)} %reduce_sum.48), channel_id=1, source_target_pairs={{0,4},{4,0},{1,5},{5,1},{2,6},{6,2},{3,7},{7,3},{8,12},{12,8},{9,1... | collective-permute-start | bytes 147464 | tf_op jit(solution)/shard_map/ppermute | solution.py:105

commit v9 on v7

--- a/solution.py
+++ b/solution.py
@@ -42,50 +42,37 @@
     send_doc, slot_plus = picked[:, 0] - 1, picked[:, 1]
     first_doc, second_doc = send_doc[: group * capacity], send_doc[group * capacity :]
 
-    extra = 16
+    lanes = 128
+    wide = width + lanes
     doc_part = (first_doc[:, None] == jnp.arange(docs, dtype=jnp.int32)[None, :]).astype(bf16)
-    doc_part = jnp.concatenate(
-        [doc_part.reshape(group, capacity, docs), jnp.zeros((group, extra, docs), bf16)], axis=1
+    slot_part = slot_plus.astype(bf16).reshape(2, group * capacity).T
+    chooser = jnp.concatenate([doc_part, slot_part], axis=1)
+    table = jnp.concatenate(
+        [
+            jnp.concatenate([doc_embed, jnp.zeros((docs, lanes), bf16)], axis=1),
+            jnp.concatenate([jnp.zeros((2, width), bf16), jnp.eye(2, lanes, dtype=bf16)], axis=1),
+        ],
+        axis=0,
     )
-    slot_row = slot_plus.astype(bf16).reshape(2, group, capacity).transpose(1, 0, 2)
-    slot_row = slot_row.reshape(group, 1, 2 * capacity)
-    slot_part = jnp.concatenate(
-        [
-            jnp.zeros((group, capacity, 2 * capacity), bf16),
-            slot_row,
-            jnp.zeros((group, extra - 1, 2 * capacity), bf16),
-        ],
-        axis=1,
-    )
-    chooser = jnp.concatenate([doc_part, slot_part], axis=2)
-    chooser = chooser.reshape(group * (capacity + extra), docs + 2 * capacity)
-    table = jnp.concatenate([doc_embed, jnp.eye(2 * capacity, width, dtype=bf16)], axis=0)
     send_first = jnp.dot(chooser, table, preferred_element_type=f32).astype(bf16)
     pick = (second_doc[:, None] == jnp.arange(docs, dtype=jnp.int32)[None, :]).astype(bf16)
     send_second = jnp.dot(pick, doc_embed, preferred_element_type=f32).astype(bf16)
 
     got_first = lax.all_to_all(
-        send_first.reshape(group, capacity + extra, width), near, split_axis=0, concat_axis=0, tiled=True
-    )
+        send_first.reshape(group, capacity, wide), near, split_axis=0, concat_axis=0, tiled=True
+    ).reshape(group * capacity, wide)
     got_second = lax.all_to_all(
         send_second.reshape(group, capacity, width), near, split_axis=0, concat_axis=0, tiled=True
-    )
-    slots = got_first[:, capacity, : 2 * capacity].astype(jnp.int32) - 1
-    first_slot = jnp.concatenate(
-        [slots[:, :capacity], jnp.full((group, extra), -1, jnp.int32)], axis=1
-    ).reshape(group * (capacity + extra))
-    second_slot = slots[:, capacity:].reshape(group * capacity)
+    ).reshape(group * capacity, width)
+    first_slot = got_first[:, width].astype(jnp.int32) - 1
+    second_slot = got_first[:, width + 1].astype(jnp.int32) - 1
 
     label_ids = jnp.arange(owned, dtype=jnp.int32)
     first_hot = (label_ids[:, None] == first_slot[None, :]).astype(bf16)
-    mirror_part = jnp.dot(
-        first_hot, got_first.reshape(group * (capacity + extra), width), preferred_element_type=f32
-    )
+    mirror_part = jnp.dot(first_hot, got_first, preferred_element_type=f32)[:, :width]
     mirrored = lax.ppermute(mirror_part, "zh", [(0, 1), (1, 0)])
     second_hot = (label_ids[:, None] == second_slot[None, :]).astype(bf16)
-    own_part = jnp.dot(
-        second_hot, got_second.reshape(group * capacity, width), preferred_element_type=f32
-    )
+    own_part = jnp.dot(second_hot, got_second, preferred_element_type=f32)
     label_sums = own_part + mirrored
     label_vectors = rms_scale(label_sums).astype(bf16)
     members = (jnp.arange(CLUSTERS, dtype=jnp.int32)[:, None] == label_cluster[None, :]).astype(bf16)

time: 108 us -> 106 us (0.981)
  local copies, waits for them, and re-layouts: 2.15 us -> 1.01 us
    all_to_all x1, waiting for transfers between devices: 23.9 us -> 22.3 us  [local(): lax.all_to_all(send_first.reshape(group, capacity, wide), near, split_axi...]
    all_to_all x1, waiting for transfers between devices: 21.9 us -> 23.1 us  [local(): lax.all_to_all(send_second.reshape(group, capacity, width), near, split_a...]
  transfers between devices with their start and end apart: 4 -> 4, of which waited for: 3 -> 3; matrix products, arithmetic and copies ran while one was open for 4% -> 3% of each run, Pallas kernels for 0% -> 0%
where the time goes in v9:
time: 106 us; the launch traced here: 105 us
  waiting for transfers between devices  50.6 us (48%)
  blocking collectives  28.2 us (27%)
  starting transfers between devices  13.2 us (12%)
  matrix products  9.98 us (9%)
  other arithmetic  1.76 us (2%)
    all_to_all x1, waiting for transfers between devices, local(): lax.all_to_all(send_second.reshape(group, capacity, width), near, split_a...  23.1 us
    all_to_all x1, waiting for transfers between devices, local(): lax.all_to_all(send_first.reshape(group, capacity, wide), near, split_axi...  22.3 us
    all_to_all x1, blocking collectives, local(): lax.all_to_all(partial_sums.reshape(group, share, width), near, split_axi...  17.5 us
    all_to_all x1, blocking collectives, local(): lax.all_to_all(jnp.broadcast_to(own[None], (group, share, width)), near,...  10.7 us
    all_to_all x1, starting transfers between devices, local(): lax.all_to_all(send_first.reshape(group, capacity, wide), near, split_axi...  6.32 us
    ppermute x1, waiting for transfers between devices, local(): sums = half_sums + lax.ppermute(half_sums, 'zh', [(0, 1), (1, 0)])  5.21 us
    all_to_all x1, starting transfers between devices, local(): lax.all_to_all(send_second.reshape(group, capacity, width), near, split_a...  3.71 us
    ppermute x1, starting transfers between devices, local(): mirrored = lax.ppermute(mirror_part, 'zh', [(0, 1), (1, 0)])  2.58 us
  transfers between devices with their start and end apart: 4, of which 3 were waited for; matrix products, arithmetic and copies ran while one was open for 3% of the time, Pallas kernels for 0%

profile of v9, /device:TPU:0, one launch (start us, length us, event | category | flops | bytes accessed | tf_op | source)
XLA Modules:
  0.0 105.5 jit_solution(17400959066572097475)
XLA Ops:
  0.7 1.3 %fusion.8 = f32[1024]{0:T(1024)S(1)} fusion(s32[1024]{0:T(1024)} %bitcast.27), kind=kOutput, calls=%fused_computation.14 | convolution fusion | flops 68353024 | bytes 8192 | tf_op jit(solution)/shard_map/dot_general | solution.py:29
  2.0 0.7 fusion.35
  2.7 0.0 copy-start.1
  2.7 2.2 %fusion.3 = s32[2048,2]{0,1:T(2,128)S(1)} fusion(s32[1024]{0:T(1024)S(1)} %fusion.35, s32[1024,1]{0,1:T(1,128)} %bitcast.29, s32[1024,1]{0,1:T(1,128)} %bitcast.30), kind=kOutput, calls=%fused_computation.5 | convolution fusion | flops 10496000 | bytes 28672 | tf_op jit(solution)/shard_map/dot_general | solution.py:41
  5.0 0.2 fusion.12
  5.2 0.2 copy.11
  5.4 0.0 copy-done.1
  5.4 2.0 %convolution_convert_fusion = bf16[1024,896]{1,0:T(8,128)(2,1)} fusion(bf16[1024,2]{1,0:T(8,128)(2,1)S(1)} %copy.11, bf16[1024,128]{1,0:T(8,128)(2,1)S(1)} %fusion.12, bf16[128,768]{1,0:T(8,128)(2,1)S(1)} %copy-done.1, bf16[2,896]{1,0:T(2,128)(2,1)S(1)} %pad_convert_fusion), kind=kOutput, calls=%fused_computation.6 | convolution fusion | flops 240699904 | bytes 2301440 | tf_op jit(solution)/shard_map/dot_general | solution.py:57
  7.4 6.3 %all-to-all-start = ((bf16[16,64,896]{2,1,0:T(8,128)(2,1)}), bf16[16,64,896]{2,1,0:T(8,128)(2,1)S(1)}, u32[]{:S(2)}, u32[]{:S(2)}) async-start(bf16[16,64,896]{2,1,0:T(8,128)(2,1)} %bitcast.23), calls=%async_computation | async-start | bytes 3670016 | tf_op jit(solution)/shard_map/all_to_all | solution.py:61
  13.7 1.8 %convolution_convert_fusion.1 = bf16[1024,768]{1,0:T(8,128)(2,1)} fusion(bf16[128,768]{1,0:T(8,128)(2,1)S(1)} %copy-done.1, s32[1024]{0:T(1024)S(1)} %bitcast.25), kind=kOutput, calls=%fused_computation.7 | convolution fusion | flops 202244096 | bytes 1773568 | tf_op jit(solution)/shard_map/dot_general | solution.py:59
  15.5 22.3 %all-to-all-done = bf16[16,64,896]{2,1,0:T(8,128)(2,1)S(1)} async-done(((bf16[16,64,896]{2,1,0:T(8,128)(2,1)}), bf16[16,64,896]{2,1,0:T(8,128)(2,1)S(1)}, u32[]{:S(2)}, u32[]{:S(2)}) %all-to-all-start) | async-done | bytes 1835040 | tf_op jit(solution)/shard_map/all_to_all | solution.py:61
  37.8 3.7 %all-to-all-start.1 = ((bf16[16,64,768]{2,1,0:T(8,128)(2,1)}), bf16[16,64,768]{2,1,0:T(8,128)(2,1)S(1)}, u32[]{:S(2)}, u32[]{:S(2)}) async-start(bf16[16,64,768]{2,1,0:T(8,128)(2,1)} %bitcast.8), calls=%async_computation.1 | async-start | bytes 3145728 | tf_op jit(solution)/shard_map/all_to_all | solution.py:64
  41.5 0.4 add_reduce_fusion.1
  41.9 0.0 copy-start.2
  41.9 1.1 %fusion.4 = f32[96,768]{1,0:T(8,128)} fusion(bf16[1024,896]{1,0:T(8,128)(2,1)S(1)} %bitcast.22, s32[1024]{0:T(1024)S(1)} %get-tuple-element.4), kind=kOutput, calls=%fused_computation.8 | convolution fusion | flops 151093248 | bytes 1871872 | tf_op jit(solution)/shard_map/dot_general | solution.py:72
  43.0 2.6 %collective-permute-start = (f32[96,768]{1,0:T(8,128)}, f32[96,768]{1,0:T(8,128)S(1)}, u32[]{:S(2)}, u32[]{:S(2)}) collective-permute-start(f32[96,768]{1,0:T(8,128)} %fusion.4), channel_id=1, source_target_pairs={{0,4},{4,0},{1,5},{5,1},{2,6},{6,2},{3,7},{7,3},{8,12},{12,8},{9,1... | collective-permute-start | bytes 884744 | tf_op jit(solution)/shard_map/ppermute | solution.py:73
  45.6 23.1 %all-to-all-done.1 = bf16[16,64,768]{2,1,0:T(8,128)(2,1)S(1)} async-done(((bf16[16,64,768]{2,1,0:T(8,128)(2,1)}), bf16[16,64,768]{2,1,0:T(8,128)(2,1)S(1)}, u32[]{:S(2)}, u32[]{:S(2)}) %all-to-all-start.1) | async-done | bytes 1572896 | tf_op jit(solution)/shard_map/all_to_all | solution.py:64
  68.7 0.0 collective-permute-done
  68.7 0.5 multiply_reduce_fusion
  69.2 0.1 multiply_convert_fusion
  69.3 0.0 copy-done.2
  69.3 0.0 copy-start
  69.3 0.2 fusion.23
  69.6 17.5 %all_to_all.20 = f32[16,16,768]{2,1,0:T(8,128)S(1)} all-to-all(f32[16,16,768]{2,1,0:T(8,128)S(1)} %bitcast.20), channel_id=1, replica_groups=mesh['y'=2,'core'=2,'zh'=2,'zr'=4] {'y','core','zr'}, dimensions={0} | all-to-all | bytes 1572864 | tf_op jit(solution)/shard_map/all_to_all | solution.py:83
  87.1 0.6 collective-permute-start.1
  87.7 5.2 %collective-permute-done.1 = f32[16,768]{1,0:T(8,128)S(1)} collective-permute-done((f32[16,768]{1,0:T(8,128)S(1)}, f32[16,768]{1,0:T(8,128)S(1)}, u32[]{:S(2)}, u32[]{:S(2)}) %collective-permute-start.1) | collective-permute-done | bytes 49184 | tf_op jit(solution)/shard_map/ppermute | solution.py:87
  92.9 0.1 multiply_reduce_fusion.1
  93.0 0.1 multiply_convert_fusion.1
  93.1 10.7 %all_to_all.21 = bf16[16,16,768]{2,1,0:T(8,128)(2,1)S(1)} all-to-all(bf16[16,16,768]{2,1,0:T(8,128)(2,1)S(1)} %broadcast_in_dim.2), channel_id=1, replica_groups=mesh['y'=2,'core'=2,'zh'=2,'zr'=4] {'y','core','zr'}, dimensions={0} | all-to-all | bytes 786432 | tf_op jit(solution)/shard_map/all_to_all | solution.py:89
  103.8 0.0 copy-done
  103.8 0.9 fusion.7
  104.7 0.7 copy.13
  (10 shorter events, 0.2 us)
Async XLA Ops:
  2.7 2.7 %copy-start.1 = (bf16[128,768]{1,0:T(8,128)(2,1)S(1)}, bf16[128,768]{1,0:T(8,128)(2,1)}, u32[]{:S(2)}) copy-start(bf16[128,768]{1,0:T(8,128)(2,1)} %param.5) | copy-start | bytes 589828
  7.4 30.4 %all-to-all-start = ((bf16[16,64,896]{2,1,0:T(8,128)(2,1)}), bf16[16,64,896]{2,1,0:T(8,128)(2,1)S(1)}, u32[]{:S(2)}, u32[]{:S(2)}) async-start(bf16[16,64,896]{2,1,0:T(8,128)(2,1)} %bitcast.23), calls=%async_computation | async-start | bytes 3670016 | tf_op jit(solution)/shard_map/all_to_all | solution.py:61
  37.8 30.9 %all-to-all-start.1 = ((bf16[16,64,768]{2,1,0:T(8,128)(2,1)}), bf16[16,64,768]{2,1,0:T(8,128)(2,1)S(1)}, u32[]{:S(2)}, u32[]{:S(2)}) async-start(bf16[16,64,768]{2,1,0:T(8,128)(2,1)} %bitcast.8), calls=%async_computation.1 | async-start | bytes 3145728 | tf_op jit(solution)/shard_map/all_to_all | solution.py:64
  41.9 27.4 %copy-start.2 = (s32[96]{0:T(128)S(1)}, s32[96]{0:T(128)}, u32[]{:S(2)}) copy-start(s32[96]{0:T(128)} %param.9) | copy-start | bytes 1156
  43.0 25.6 %collective-permute-start = (f32[96,768]{1,0:T(8,128)}, f32[96,768]{1,0:T(8,128)S(1)}, u32[]{:S(2)}, u32[]{:S(2)}) collective-permute-start(f32[96,768]{1,0:T(8,128)} %fusion.4), channel_id=1, source_target_pairs={{0,4},{4,0},{1,5},{5,1},{2,6},{6,2},{3,7},{7,3},{8,12},{12,8},{9,1... | collective-permute-start | bytes 884744 | tf_op jit(solution)/shard_map/ppermute | solution.py:73
  69.3 34.5 %copy-start = (bf16[96,768]{1,0:T(8,128)(2,1)}, bf16[96,768]{1,0:T(8,128)(2,1)S(1)}, u32[]{:S(2)}) copy-start(bf16[96,768]{1,0:T(8,128)(2,1)S(1)} %multiply_convert_fusion) | copy-start | bytes 442372
  87.1 5.8 %collective-permute-start.1 = (f32[16,768]{1,0:T(8,128)S(1)}, f32[16,768]{1,0:T(8,128)S(1)}, u32[]{:S(2)}, u32[]{:S(2)}) collective-permute-start(f32[16,768]{1,0:T(8,128)S(1)} %reduce_sum.38), channel_id=1, source_target_pairs={{0,4},{4,0},{1,5},{5,1},{2,6},{6,2},{3,7},{7,3},{8,12},{12,8},{9,1... | collective-permute-start | bytes 147464 | tf_op jit(solution)/shard_map/ppermute | solution.py:87

commit v10 on v9

--- a/solution.py
+++ b/solution.py
@@ -23,23 +23,37 @@
     owner = pair_owner[:, 0]
     f32, bf16 = jnp.float32, jnp.bfloat16
 
-    owner_hits = (owner[:, None] == jnp.arange(devices, dtype=jnp.int32)[None, :]).astype(bf16)
-    pid = jnp.arange(pairs, dtype=jnp.int32)
-    earlier = (pid[None, :] < pid[:, None]).astype(bf16)
-    before = jnp.dot(earlier, owner_hits, preferred_element_type=f32)
-    rank = jnp.sum(before * owner_hits.astype(f32), axis=1).astype(jnp.int32)
     cols = 2 * halves
     o_row, o_col = owner // cols, owner % cols
     o_zh, o_zr = o_col // halves, o_col % halves
     proxy = o_row * halves + o_zr
     me = lax.axis_index("zh")
     later = (o_zh == me).astype(jnp.int32)
-    position = later * (group * capacity) + proxy * capacity + rank
+    block = later * group + proxy
 
-    place = (jnp.arange(devices * capacity, dtype=jnp.int32)[:, None] == position[None, :]).astype(bf16)
-    tags = (jnp.stack([pair_doc, pair_slot], axis=1) + 1).astype(bf16)
-    picked = jnp.dot(place, tags, preferred_element_type=f32).astype(jnp.int32)
-    send_doc, slot_plus = picked[:, 0] - 1, picked[:, 1]
+    chunk = 32
+    hits = (block[:, None] == jnp.arange(devices, dtype=jnp.int32)[None, :]).astype(bf16)
+    hits3 = hits.reshape(pairs // chunk, chunk, devices)
+    step = jnp.arange(chunk, dtype=jnp.int32)
+    inside = (step[None, :] < step[:, None]).astype(bf16)
+    within = jnp.einsum("ij,cjo->cio", inside, hits3, preferred_element_type=f32)
+    totals = jnp.sum(hits3.astype(f32), axis=1)
+    lead = jnp.arange(pairs // chunk, dtype=jnp.int32)
+    ahead = (lead[None, :] < lead[:, None]).astype(f32)
+    offsets = jnp.dot(ahead, totals, preferred_element_type=f32)
+    counts = (within + offsets[:, None, :]).reshape(pairs, devices)
+    rank = jnp.sum(counts * hits.astype(f32), axis=1).astype(jnp.int32)
+
+    at_rank = (rank[:, None] == jnp.arange(capacity, dtype=jnp.int32)[None, :]).astype(f32)
+    tagged = jnp.concatenate(
+        [at_rank * (pair_doc + 1).astype(f32)[:, None], at_rank * (pair_slot + 1).astype(f32)[:, None]],
+        axis=1,
+    ).astype(bf16)
+    picked = lax.dot_general(
+        hits, tagged, (((0,), (0,)), ((), ())), preferred_element_type=f32
+    ).astype(jnp.int32)
+    send_doc = picked[:, :capacity].reshape(devices * capacity) - 1
+    slot_plus = picked[:, capacity:].reshape(devices * capacity)
     first_doc, second_doc = send_doc[: group * capacity], send_doc[group * capacity :]
 
     lanes = 128

time: 106 us -> 107 us (level)
  matrix products: 9.98 us -> 7.38 us
  other arithmetic: 1.76 us -> 3.59 us
  local copies, waits for them, and re-layouts: 1.01 us -> 2.62 us
    dot_general x2 -> x3, matrix products: 3.51 us -> 0.91 us  [the longest x1 0.51 us: local(): lax.dot_general(hits, tagged, (((0,), (0,)), ((), ())), preferred_element...]
where the time goes in v10:
time: 107 us; the launch traced here: 106 us
  waiting for transfers between devices  50.5 us (47%)
  blocking collectives  28.2 us (26%)
  starting transfers between devices  13.2 us (12%)
  matrix products  7.38 us (7%)
  other arithmetic  3.59 us (3%)
  local copies, waits for them, and re-layouts  2.62 us (2%)
    all_to_all x1, waiting for transfers between devices, local(): lax.all_to_all(send_second.reshape(group, capacity, width), near, split_a...  23.1 us
    all_to_all x1, waiting for transfers between devices, local(): lax.all_to_all(send_first.reshape(group, capacity, wide), near, split_axi...  22.2 us
    all_to_all x1, blocking collectives, local(): lax.all_to_all(partial_sums.reshape(group, share, width), near, split_axi...  17.5 us
    all_to_all x1, blocking collectives, local(): lax.all_to_all(jnp.broadcast_to(own[None], (group, share, width)), near,...  10.7 us
    all_to_all x1, starting transfers between devices, local(): lax.all_to_all(send_first.reshape(group, capacity, wide), near, split_axi...  6.32 us
    ppermute x1, waiting for transfers between devices, local(): sums = half_sums + lax.ppermute(half_sums, 'zh', [(0, 1), (1, 0)])  5.21 us
    all_to_all x1, starting transfers between devices, local(): lax.all_to_all(send_second.reshape(group, capacity, width), near, split_a...  3.71 us
    ppermute x1, starting transfers between devices, local(): mirrored = lax.ppermute(mirror_part, 'zh', [(0, 1), (1, 0)])  2.59 us
  transfers between devices with their start and end apart: 4, of which 3 were waited for; matrix products, arithmetic and copies ran while one was open for 3% of the time, Pallas kernels for 0%

profile of v10, /device:TPU:0, one launch (start us, length us, event | category | flops | bytes accessed | tf_op | source)
XLA Modules:
  0.0 106.3 jit_solution(2806020149778834438)
XLA Ops:
  0.6 0.0 copy-start.2
  0.6 0.0 copy-start.3
  0.7 0.7 broadcast_compare_fusion
  1.4 0.0 copy-start.1
  1.4 0.9 copy.19
  2.3 0.3 copy.22
  2.6 1.1 %fusion.10 = s32[1024]{0:T(1024)S(1)} fusion(pred[1024,1]{1,0:T(8,128)(4,1)S(1)} %copy.22, s32[1024,1]{1,0:T(8,128)S(1)} %copy.19, s32[]{:T(128)S(6)} %axis_index.15), kind=kLoop, calls=%fused_computation.27 | loop fusion | flops 43008 | bytes 9220 | tf_op jit(solution)/shard_map/add | solution.py:32
  3.7 0.1 eq.124
  3.8 0.2 convert_reduce_fusion
  4.0 0.1 fusion.37
  4.2 0.3 fusion.4
  4.5 0.1 convert_element_type.78
  4.5 0.0 copy-done.2
  4.5 0.0 copy-done.3
  4.5 0.5 select_convert_fusion.1
  5.0 0.5 convolution_convert_fusion.2
  5.5 0.1 slice_add_fusion
  5.6 0.1 slice.30
  5.7 0.1 convert_element_type.83
  5.8 0.2 copy.25
  6.0 0.2 fusion.17
  6.2 0.0 copy-done.1
  6.2 2.0 %convolution_convert_fusion = bf16[1024,896]{1,0:T(8,128)(2,1)} fusion(bf16[1024,2]{1,0:T(8,128)(2,1)S(1)} %copy.25, bf16[1024,128]{1,0:T(8,128)(2,1)S(1)} %fusion.17, bf16[128,768]{1,0:T(8,128)(2,1)S(1)} %copy-done.1, bf16[2,896]{1,0:T(2,128)(2,1)S(1)} %pad_convert_fusion), kind=kOutput, calls=%fused_computation | convolution fusion | flops 240699904 | bytes 2301440 | tf_op jit(solution)/shard_map/dot_general | solution.py:71
  8.2 6.3 %all-to-all-start = ((bf16[16,64,896]{2,1,0:T(8,128)(2,1)}), bf16[16,64,896]{2,1,0:T(8,128)(2,1)S(1)}, u32[]{:S(2)}, u32[]{:S(2)}) async-start(bf16[16,64,896]{2,1,0:T(8,128)(2,1)} %bitcast.28), calls=%async_computation | async-start | bytes 3670016 | tf_op jit(solution)/shard_map/all_to_all | solution.py:75
  14.5 0.1 slice.34
  14.6 1.8 %convolution_convert_fusion.1 = bf16[1024,768]{1,0:T(8,128)(2,1)} fusion(bf16[128,768]{1,0:T(8,128)(2,1)S(1)} %copy-done.1, s32[1024]{0:T(1024)S(1)} %slice.34), kind=kOutput, calls=%fused_computation.1 | convolution fusion | flops 202244096 | bytes 1773568 | tf_op jit(solution)/shard_map/dot_general | solution.py:73
  16.3 22.2 %all-to-all-done = bf16[16,64,896]{2,1,0:T(8,128)(2,1)S(1)} async-done(((bf16[16,64,896]{2,1,0:T(8,128)(2,1)}), bf16[16,64,896]{2,1,0:T(8,128)(2,1)S(1)}, u32[]{:S(2)}, u32[]{:S(2)}) %all-to-all-start) | async-done | bytes 1835040 | tf_op jit(solution)/shard_map/all_to_all | solution.py:75
  38.6 3.7 %all-to-all-start.1 = ((bf16[16,64,768]{2,1,0:T(8,128)(2,1)}), bf16[16,64,768]{2,1,0:T(8,128)(2,1)S(1)}, u32[]{:S(2)}, u32[]{:S(2)}) async-start(bf16[16,64,768]{2,1,0:T(8,128)(2,1)} %bitcast.5), calls=%async_computation.1 | async-start | bytes 3145728 | tf_op jit(solution)/shard_map/all_to_all | solution.py:78
  42.3 0.4 add_reduce_fusion.1
  42.7 0.0 copy-start.4
  42.7 1.1 %fusion = f32[96,768]{1,0:T(8,128)} fusion(bf16[1024,896]{1,0:T(8,128)(2,1)S(1)} %bitcast.27, s32[1024]{0:T(1024)S(1)} %get-tuple-element.4), kind=kOutput, calls=%fused_computation.2 | convolution fusion | flops 151093248 | bytes 1871872 | tf_op jit(solution)/shard_map/dot_general | solution.py:86
  43.9 2.6 %collective-permute-start = (f32[96,768]{1,0:T(8,128)}, f32[96,768]{1,0:T(8,128)S(1)}, u32[]{:S(2)}, u32[]{:S(2)}) collective-permute-start(f32[96,768]{1,0:T(8,128)} %fusion), channel_id=1, source_target_pairs={{0,4},{4,0},{1,5},{5,1},{2,6},{6,2},{3,7},{7,3},{8,12},{12,8},{9,1... | collective-permute-start | bytes 884744 | tf_op jit(solution)/shard_map/ppermute | solution.py:87
  46.4 23.1 %all-to-all-done.1 = bf16[16,64,768]{2,1,0:T(8,128)(2,1)S(1)} async-done(((bf16[16,64,768]{2,1,0:T(8,128)(2,1)}), bf16[16,64,768]{2,1,0:T(8,128)(2,1)S(1)}, u32[]{:S(2)}, u32[]{:S(2)}) %all-to-all-start.1) | async-done | bytes 1572896 | tf_op jit(solution)/shard_map/all_to_all | solution.py:78
  69.5 0.0 collective-permute-done
  69.5 0.5 multiply_reduce_fusion
  70.0 0.1 multiply_convert_fusion
  70.1 0.0 copy-done.4
  70.1 0.0 copy-start
  70.1 0.2 fusion.34
  70.4 17.5 %all_to_all.20 = f32[16,16,768]{2,1,0:T(8,128)S(1)} all-to-all(f32[16,16,768]{2,1,0:T(8,128)S(1)} %bitcast.25), channel_id=1, replica_groups=mesh['y'=2,'core'=2,'zh'=2,'zr'=4] {'y','core','zr'}, dimensions={0} | all-to-all | bytes 1572864 | tf_op jit(solution)/shard_map/all_to_all | solution.py:97
  87.9 0.6 collective-permute-start.1
  88.5 5.2 %collective-permute-done.1 = f32[16,768]{1,0:T(8,128)S(1)} collective-permute-done((f32[16,768]{1,0:T(8,128)S(1)}, f32[16,768]{1,0:T(8,128)S(1)}, u32[]{:S(2)}, u32[]{:S(2)}) %collective-permute-start.1) | collective-permute-done | bytes 49184 | tf_op jit(solution)/shard_map/ppermute | solution.py:101
  93.7 0.1 multiply_reduce_fusion.1
  93.8 0.1 multiply_convert_fusion.1
  93.9 10.7 %all_to_all.21 = bf16[16,16,768]{2,1,0:T(8,128)(2,1)S(1)} all-to-all(bf16[16,16,768]{2,1,0:T(8,128)(2,1)S(1)} %broadcast_in_dim.2), channel_id=1, replica_groups=mesh['y'=2,'core'=2,'zh'=2,'zr'=4] {'y','core','zr'}, dimensions={0} | all-to-all | bytes 786432 | tf_op jit(solution)/shard_map/all_to_all | solution.py:103
  104.6 0.0 copy-done
  104.6 0.9 fusion.5
  105.5 0.7 copy.27
  (9 shorter events, 0.1 us)
Async XLA Ops:
  0.6 3.9 %copy-start.2 = (s32[1024]{0:T(1024)S(1)}, s32[1024]{0:T(1024)}, u32[]{:S(2)}) copy-start(s32[1024]{0:T(1024)} %param.8) | copy-start | bytes 12292
  0.6 3.9 %copy-start.3 = (s32[1024]{0:T(1024)S(1)}, s32[1024]{0:T(1024)}, u32[]{:S(2)}) copy-start(s32[1024]{0:T(1024)} %param.6) | copy-start | bytes 12292
  1.4 4.8 %copy-start.1 = (bf16[128,768]{1,0:T(8,128)(2,1)S(1)}, bf16[128,768]{1,0:T(8,128)(2,1)}, u32[]{:S(2)}) copy-start(bf16[128,768]{1,0:T(8,128)(2,1)} %param.5) | copy-start | bytes 589828
  8.2 30.4 %all-to-all-start = ((bf16[16,64,896]{2,1,0:T(8,128)(2,1)}), bf16[16,64,896]{2,1,0:T(8,128)(2,1)S(1)}, u32[]{:S(2)}, u32[]{:S(2)}) async-start(bf16[16,64,896]{2,1,0:T(8,128)(2,1)} %bitcast.28), calls=%async_computation | async-start | bytes 3670016 | tf_op jit(solution)/shard_map/all_to_all | solution.py:75
  38.6 30.9 %all-to-all-start.1 = ((bf16[16,64,768]{2,1,0:T(8,128)(2,1)}), bf16[16,64,768]{2,1,0:T(8,128)(2,1)S(1)}, u32[]{:S(2)}, u32[]{:S(2)}) async-start(bf16[16,64,768]{2,1,0:T(8,128)(2,1)} %bitcast.5), calls=%async_computation.1 | async-start | bytes 3145728 | tf_op jit(solution)/shard_map/all_to_all | solution.py:78
  42.7 27.4 %copy-start.4 = (s32[96]{0:T(128)S(1)}, s32[96]{0:T(128)}, u32[]{:S(2)}) copy-start(s32[96]{0:T(128)} %param.9) | copy-start | bytes 1156
  43.9 25.6 %collective-permute-start = (f32[96,768]{1,0:T(8,128)}, f32[96,768]{1,0:T(8,128)S(1)}, u32[]{:S(2)}, u32[]{:S(2)}) collective-permute-start(f32[96,768]{1,0:T(8,128)} %fusion), channel_id=1, source_target_pairs={{0,4},{4,0},{1,5},{5,1},{2,6},{6,2},{3,7},{7,3},{8,12},{12,8},{9,1... | collective-permute-start | bytes 884744 | tf_op jit(solution)/shard_map/ppermute | solution.py:87
  70.1 34.5 %copy-start = (bf16[96,768]{1,0:T(8,128)(2,1)}, bf16[96,768]{1,0:T(8,128)(2,1)S(1)}, u32[]{:S(2)}) copy-start(bf16[96,768]{1,0:T(8,128)(2,1)S(1)} %multiply_convert_fusion) | copy-start | bytes 442372
  87.9 5.8 %collective-permute-start.1 = (f32[16,768]{1,0:T(8,128)S(1)}, f32[16,768]{1,0:T(8,128)S(1)}, u32[]{:S(2)}, u32[]{:S(2)}) collective-permute-start(f32[16,768]{1,0:T(8,128)S(1)} %reduce_sum.48), channel_id=1, source_target_pairs={{0,4},{4,0},{1,5},{5,1},{2,6},{6,2},{3,7},{7,3},{8,12},{12,8},{9,1... | collective-permute-start | bytes 147464 | tf_op jit(solution)/shard_map/ppermute | solution.py:101

commit v11 on v10

--- a/solution.py
+++ b/solution.py
@@ -20,19 +20,16 @@
     docs, width = doc_embed.shape
     owned = label_cluster.shape[0]
     capacity = 2 * pairs // devices
-    owner = pair_owner[:, 0]
     f32, bf16 = jnp.float32, jnp.bfloat16
 
-    cols = 2 * halves
-    o_row, o_col = owner // cols, owner % cols
-    o_zh, o_zr = o_col // halves, o_col % halves
-    proxy = o_row * halves + o_zr
     me = lax.axis_index("zh")
-    later = (o_zh == me).astype(jnp.int32)
-    block = later * group + proxy
+    b = jnp.arange(devices, dtype=jnp.int32)
+    b_later, b_proxy = b // group, b % group
+    b_zh = jnp.where(b_later == 1, me, 1 - me)
+    block_owner = (b_proxy // halves) * (2 * halves) + b_zh * halves + b_proxy % halves
 
     chunk = 32
-    hits = (block[:, None] == jnp.arange(devices, dtype=jnp.int32)[None, :]).astype(bf16)
+    hits = (pair_owner == block_owner[None, :]).astype(bf16)
     hits3 = hits.reshape(pairs // chunk, chunk, devices)
     step = jnp.arange(chunk, dtype=jnp.int32)
     inside = (step[None, :] < step[:, None]).astype(bf16)

time: 107 us -> 107 us (level)
    unnamed x0 -> x1, other arithmetic: none -> 1.35 us
    add x1, other arithmetic: 1.1 us -> 0.01 us  [local(): b_proxy // halves * (2 * halves) + b_zh * halves + b_proxy % halves]
where the time goes in v11:
time: 107 us
  waiting for transfers between devices  50.5 us (47%)
  blocking collectives  28.2 us (26%)
  starting transfers between devices  13.2 us (12%)
  matrix products  8.12 us (8%)
  other arithmetic  3.92 us (4%)
  local copies, waits for them, and re-layouts  1.9 us (2%)
    all_to_all x1, waiting for transfers between devices, local(): lax.all_to_all(send_second.reshape(group, capacity, width), near, split_a...  23.1 us
    all_to_all x1, waiting for transfers between devices, local(): lax.all_to_all(send_first.reshape(group, capacity, wide), near, split_axi...  22.2 us
    all_to_all x1, blocking collectives, local(): lax.all_to_all(partial_sums.reshape(group, share, width), near, split_axi...  17.5 us
    all_to_all x1, blocking collectives, local(): lax.all_to_all(jnp.broadcast_to(own[None], (group, share, width)), near,...  10.7 us
    all_to_all x1, starting transfers between devices, local(): lax.all_to_all(send_first.reshape(group, capacity, wide), near, split_axi...  6.31 us
    ppermute x1, waiting for transfers between devices, local(): sums = half_sums + lax.ppermute(half_sums, 'zh', [(0, 1), (1, 0)])  5.21 us
    all_to_all x1, starting transfers between devices, local(): lax.all_to_all(send_second.reshape(group, capacity, width), near, split_a...  3.71 us
    ppermute x1, starting transfers between devices, local(): mirrored = lax.ppermute(mirror_part, 'zh', [(0, 1), (1, 0)])  2.59 us
  transfers between devices with their start and end apart: 4, of which 3 were waited for; matrix products, arithmetic and copies ran while one was open for 3% of the time, Pallas kernels for 0%

profile of v11, /device:TPU:0, one launch (start us, length us, event | category | flops | bytes accessed | tf_op | source)
XLA Modules:
  0.0 106.6 jit_solution(11940578956936769212)
XLA Ops:
  0.6 0.0 copy-start.1
  0.7 0.5 broadcast.242
  1.2 1.3 %reduce.8 = s32[1024]{0:T(1024)S(1)} reduce(s32[1024,1]{0,1:T(1,128)} %param.7, s32[]{:T(128)} %broadcast.242), dimensions={1}, to_apply=%param.7.reduce_sub_computation.3 | reduce | bytes 8196 | tf_op args[2]
  2.6 0.1 eq.124
  2.6 0.3 convert_reduce_fusion
  2.9 0.1 fusion.31
  3.0 0.3 fusion.4
  3.4 0.1 convert_element_type.77
  3.5 0.7 add_convert_fusion
  4.2 0.5 select_convert_fusion.1
  4.6 1.2 %convolution_convert_fusion.2 = s32[32,128]{1,0:T(8,128)S(1)} fusion(bf16[1024,64]{1,0:T(8,128)(2,1)S(1)} %get-tuple-element.12, bf16[1024,64]{1,0:T(8,128)(2,1)S(1)} %get-tuple-element.11, s32[32]{0:T(128)S(1)} %fusion.34, s32[1024]{0:T(1024)} %bitcast.32), kind=kOutput, calls=%fused_computation.11 | convolution fusion | flops 8949760 | bytes 282752 | tf_op jit(solution)/shard_map/dot_general | solution.py:49
  5.8 0.1 slice_add_fusion
  5.9 0.1 slice.30
  6.0 0.1 convert_element_type.82
  6.1 0.2 copy.11
  6.3 0.2 fusion.10
  6.5 0.0 copy-done.1
  6.5 2.0 %convolution_convert_fusion = bf16[1024,896]{1,0:T(8,128)(2,1)} fusion(bf16[1024,2]{1,0:T(8,128)(2,1)S(1)} %copy.11, bf16[1024,128]{1,0:T(8,128)(2,1)S(1)} %fusion.10, bf16[128,768]{1,0:T(8,128)(2,1)S(1)} %copy-done.1, bf16[2,896]{1,0:T(2,128)(2,1)S(1)} %pad_convert_fusion), kind=kOutput, calls=%fused_computation | convolution fusion | flops 240699904 | bytes 2301440 | tf_op jit(solution)/shard_map/dot_general | solution.py:68
  8.5 6.3 %all-to-all-start = ((bf16[16,64,896]{2,1,0:T(8,128)(2,1)}), bf16[16,64,896]{2,1,0:T(8,128)(2,1)S(1)}, u32[]{:S(2)}, u32[]{:S(2)}) async-start(bf16[16,64,896]{2,1,0:T(8,128)(2,1)} %bitcast.30), calls=%async_computation | async-start | bytes 3670016 | tf_op jit(solution)/shard_map/all_to_all | solution.py:72
  14.8 0.1 slice.34
  14.9 1.8 %convolution_convert_fusion.1 = bf16[1024,768]{1,0:T(8,128)(2,1)} fusion(bf16[128,768]{1,0:T(8,128)(2,1)S(1)} %copy-done.1, s32[1024]{0:T(1024)S(1)} %slice.34), kind=kOutput, calls=%fused_computation.1 | convolution fusion | flops 202244096 | bytes 1773568 | tf_op jit(solution)/shard_map/dot_general | solution.py:70
  16.6 22.2 %all-to-all-done = bf16[16,64,896]{2,1,0:T(8,128)(2,1)S(1)} async-done(((bf16[16,64,896]{2,1,0:T(8,128)(2,1)}), bf16[16,64,896]{2,1,0:T(8,128)(2,1)S(1)}, u32[]{:S(2)}, u32[]{:S(2)}) %all-to-all-start) | async-done | bytes 1835040 | tf_op jit(solution)/shard_map/all_to_all | solution.py:72
  38.9 3.7 %all-to-all-start.1 = ((bf16[16,64,768]{2,1,0:T(8,128)(2,1)}), bf16[16,64,768]{2,1,0:T(8,128)(2,1)S(1)}, u32[]{:S(2)}, u32[]{:S(2)}) async-start(bf16[16,64,768]{2,1,0:T(8,128)(2,1)} %bitcast.6), calls=%async_computation.1 | async-start | bytes 3145728 | tf_op jit(solution)/shard_map/all_to_all | solution.py:75
  42.6 0.4 add_reduce_fusion.1
  43.0 0.0 copy-start.2
  43.1 1.1 %fusion = f32[96,768]{1,0:T(8,128)} fusion(bf16[1024,896]{1,0:T(8,128)(2,1)S(1)} %bitcast.29, s32[1024]{0:T(1024)S(1)} %get-tuple-element.4), kind=kOutput, calls=%fused_computation.2 | convolution fusion | flops 151093248 | bytes 1871872 | tf_op jit(solution)/shard_map/dot_general | solution.py:83
  44.2 2.6 %collective-permute-start = (f32[96,768]{1,0:T(8,128)}, f32[96,768]{1,0:T(8,128)S(1)}, u32[]{:S(2)}, u32[]{:S(2)}) collective-permute-start(f32[96,768]{1,0:T(8,128)} %fusion), channel_id=1, source_target_pairs={{0,4},{4,0},{1,5},{5,1},{2,6},{6,2},{3,7},{7,3},{8,12},{12,8},{9,1... | collective-permute-start | bytes 884744 | tf_op jit(solution)/shard_map/ppermute | solution.py:84
  46.8 23.1 %all-to-all-done.1 = bf16[16,64,768]{2,1,0:T(8,128)(2,1)S(1)} async-done(((bf16[16,64,768]{2,1,0:T(8,128)(2,1)}), bf16[16,64,768]{2,1,0:T(8,128)(2,1)S(1)}, u32[]{:S(2)}, u32[]{:S(2)}) %all-to-all-start.1) | async-done | bytes 1572896 | tf_op jit(solution)/shard_map/all_to_all | solution.py:75
  69.8 0.0 collective-permute-done
  69.8 0.5 multiply_reduce_fusion
  70.3 0.1 multiply_convert_fusion
  70.4 0.0 copy-done.2
  70.4 0.0 copy-start
  70.4 0.2 fusion.28
  70.7 17.5 %all_to_all.20 = f32[16,16,768]{2,1,0:T(8,128)S(1)} all-to-all(f32[16,16,768]{2,1,0:T(8,128)S(1)} %bitcast.27), channel_id=1, replica_groups=mesh['y'=2,'core'=2,'zh'=2,'zr'=4] {'y','core','zr'}, dimensions={0} | all-to-all | bytes 1572864 | tf_op jit(solution)/shard_map/all_to_all | solution.py:94
  88.2 0.6 collective-permute-start.1
  88.8 5.2 %collective-permute-done.1 = f32[16,768]{1,0:T(8,128)S(1)} collective-permute-done((f32[16,768]{1,0:T(8,128)S(1)}, f32[16,768]{1,0:T(8,128)S(1)}, u32[]{:S(2)}, u32[]{:S(2)}) %collective-permute-start.1) | collective-permute-done | bytes 49184 | tf_op jit(solution)/shard_map/ppermute | solution.py:98
  94.0 0.1 multiply_reduce_fusion.1
  94.1 0.1 multiply_convert_fusion.1
  94.2 10.7 %all_to_all.21 = bf16[16,16,768]{2,1,0:T(8,128)(2,1)S(1)} all-to-all(bf16[16,16,768]{2,1,0:T(8,128)(2,1)S(1)} %broadcast_in_dim.12), channel_id=1, replica_groups=mesh['y'=2,'core'=2,'zh'=2,'zr'=4] {'y','core','zr'}, dimensions={0} | all-to-all | bytes 786432 | tf_op jit(solution)/shard_map/all_to_all | solution.py:100
  104.9 0.0 copy-done
  104.9 0.9 fusion.5
  105.9 0.7 copy.13
  (9 shorter events, 0.1 us)
Async XLA Ops:
  0.6 5.9 %copy-start.1 = (bf16[128,768]{1,0:T(8,128)(2,1)S(1)}, bf16[128,768]{1,0:T(8,128)(2,1)}, u32[]{:S(2)}) copy-start(bf16[128,768]{1,0:T(8,128)(2,1)} %param.5) | copy-start | bytes 589828
  8.5 30.4 %all-to-all-start = ((bf16[16,64,896]{2,1,0:T(8,128)(2,1)}), bf16[16,64,896]{2,1,0:T(8,128)(2,1)S(1)}, u32[]{:S(2)}, u32[]{:S(2)}) async-start(bf16[16,64,896]{2,1,0:T(8,128)(2,1)} %bitcast.30), calls=%async_computation | async-start | bytes 3670016 | tf_op jit(solution)/shard_map/all_to_all | solution.py:72
  38.9 30.9 %all-to-all-start.1 = ((bf16[16,64,768]{2,1,0:T(8,128)(2,1)}), bf16[16,64,768]{2,1,0:T(8,128)(2,1)S(1)}, u32[]{:S(2)}, u32[]{:S(2)}) async-start(bf16[16,64,768]{2,1,0:T(8,128)(2,1)} %bitcast.6), calls=%async_computation.1 | async-start | bytes 3145728 | tf_op jit(solution)/shard_map/all_to_all | solution.py:75
  43.0 27.4 %copy-start.2 = (s32[96]{0:T(128)S(1)}, s32[96]{0:T(128)}, u32[]{:S(2)}) copy-start(s32[96]{0:T(128)} %param.9) | copy-start | bytes 1156
  44.2 25.6 %collective-permute-start = (f32[96,768]{1,0:T(8,128)}, f32[96,768]{1,0:T(8,128)S(1)}, u32[]{:S(2)}, u32[]{:S(2)}) collective-permute-start(f32[96,768]{1,0:T(8,128)} %fusion), channel_id=1, source_target_pairs={{0,4},{4,0},{1,5},{5,1},{2,6},{6,2},{3,7},{7,3},{8,12},{12,8},{9,1... | collective-permute-start | bytes 884744 | tf_op jit(solution)/shard_map/ppermute | solution.py:84
  70.4 34.5 %copy-start = (bf16[96,768]{1,0:T(8,128)(2,1)}, bf16[96,768]{1,0:T(8,128)(2,1)S(1)}, u32[]{:S(2)}) copy-start(bf16[96,768]{1,0:T(8,128)(2,1)S(1)} %multiply_convert_fusion) | copy-start | bytes 442372
  88.2 5.8 %collective-permute-start.1 = (f32[16,768]{1,0:T(8,128)S(1)}, f32[16,768]{1,0:T(8,128)S(1)}, u32[]{:S(2)}, u32[]{:S(2)}) collective-permute-start(f32[16,768]{1,0:T(8,128)S(1)} %reduce_sum.48), channel_id=1, source_target_pairs={{0,4},{4,0},{1,5},{5,1},{2,6},{6,2},{3,7},{7,3},{8,12},{12,8},{9,1... | collective-permute-start | bytes 147464 | tf_op jit(solution)/shard_map/ppermute | solution.py:98

commit v12 on v11

--- a/solution.py
+++ b/solution.py
@@ -28,26 +28,23 @@
     b_zh = jnp.where(b_later == 1, me, 1 - me)
     block_owner = (b_proxy // halves) * (2 * halves) + b_zh * halves + b_proxy % halves
 
-    chunk = 32
-    hits = (pair_owner == block_owner[None, :]).astype(bf16)
-    hits3 = hits.reshape(pairs // chunk, chunk, devices)
-    step = jnp.arange(chunk, dtype=jnp.int32)
-    inside = (step[None, :] < step[:, None]).astype(bf16)
-    within = jnp.einsum("ij,cjo->cio", inside, hits3, preferred_element_type=f32)
-    totals = jnp.sum(hits3.astype(f32), axis=1)
-    lead = jnp.arange(pairs // chunk, dtype=jnp.int32)
-    ahead = (lead[None, :] < lead[:, None]).astype(f32)
-    offsets = jnp.dot(ahead, totals, preferred_element_type=f32)
-    counts = (within + offsets[:, None, :]).reshape(pairs, devices)
-    rank = jnp.sum(counts * hits.astype(f32), axis=1).astype(jnp.int32)
+    owner_row = pair_owner.reshape(1, pairs)
+    hits_t = (block_owner[:, None] == owner_row).astype(bf16)
+    pid = jnp.arange(pairs, dtype=jnp.int32)
+    earlier_t = (pid[:, None] < pid[None, :]).astype(bf16)
+    before_t = jnp.dot(hits_t, earlier_t, preferred_element_type=f32)
+    rank_row = jnp.sum(before_t * hits_t.astype(f32), axis=0, keepdims=True).astype(jnp.int32)
 
-    at_rank = (rank[:, None] == jnp.arange(capacity, dtype=jnp.int32)[None, :]).astype(f32)
-    tagged = jnp.concatenate(
-        [at_rank * (pair_doc + 1).astype(f32)[:, None], at_rank * (pair_slot + 1).astype(f32)[:, None]],
-        axis=1,
+    at_rank_t = (jnp.arange(capacity, dtype=jnp.int32)[:, None] == rank_row).astype(f32)
+    tagged_t = jnp.concatenate(
+        [
+            at_rank_t * (pair_doc.reshape(1, pairs) + 1).astype(f32),
+            at_rank_t * (pair_slot.reshape(1, pairs) + 1).astype(f32),
+        ],
+        axis=0,
     ).astype(bf16)
     picked = lax.dot_general(
-        hits, tagged, (((0,), (0,)), ((), ())), preferred_element_type=f32
+        hits_t, tagged_t, (((1,), (1,)), ((), ())), preferred_element_type=f32
     ).astype(jnp.int32)
     send_doc = picked[:, :capacity].reshape(devices * capacity) - 1
     slot_plus = picked[:, capacity:].reshape(devices * capacity)

time: 107 us -> 105 us (0.981)
  other arithmetic: 3.92 us -> 1.86 us
    unnamed x1 -> x0, other arithmetic: 1.35 us -> none
where the time goes in v12:
time: 105 us; the launch traced here: 104 us
  waiting for transfers between devices  50.5 us (48%)
  blocking collectives  28.2 us (27%)
  starting transfers between devices  13.2 us (13%)
  matrix products  8.57 us (8%)
  other arithmetic  1.86 us (2%)
  local copies, waits for them, and re-layouts  1.24 us (1%)
    all_to_all x1, waiting for transfers between devices, local(): lax.all_to_all(send_second.reshape(group, capacity, width), near, split_a...  23.1 us
    all_to_all x1, waiting for transfers between devices, local(): lax.all_to_all(send_first.reshape(group, capacity, wide), near, split_axi...  22.2 us
    all_to_all x1, blocking collectives, local(): lax.all_to_all(partial_sums.reshape(group, share, width), near, split_axi...  17.5 us
    all_to_all x1, blocking collectives, local(): lax.all_to_all(jnp.broadcast_to(own[None], (group, share, width)), near,...  10.7 us
    all_to_all x1, starting transfers between devices, local(): lax.all_to_all(send_first.reshape(group, capacity, wide), near, split_axi...  6.31 us
    ppermute x1, waiting for transfers between devices, local(): sums = half_sums + lax.ppermute(half_sums, 'zh', [(0, 1), (1, 0)])  5.21 us
    all_to_all x1, starting transfers between devices, local(): lax.all_to_all(send_second.reshape(group, capacity, width), near, split_a...  3.71 us
    ppermute x1, starting transfers between devices, local(): mirrored = lax.ppermute(mirror_part, 'zh', [(0, 1), (1, 0)])  2.59 us
  transfers between devices with their start and end apart: 4, of which 3 were waited for; matrix products, arithmetic and copies ran while one was open for 3% of the time, Pallas kernels for 0%

profile of v12, /device:TPU:0, one launch (start us, length us, event | category | flops | bytes accessed | tf_op | source)
XLA Modules:
  0.0 104.3 jit_solution(8954041053965921741)
XLA Ops:
  0.6 0.0 copy-start.1
  0.7 1.2 %fusion.5 = f32[1024]{0:T(1024)S(1)} fusion(s32[1024]{0:T(1024)} %bitcast.21, s32[32]{0:T(128)S(1)} %fusion.31), kind=kOutput, calls=%fused_computation.10 | convolution fusion | flops 68353024 | bytes 8320 | tf_op jit(solution)/shard_map/dot_general | solution.py:35
  1.9 0.7 add_convert_fusion
  2.7 0.9 convolution_convert_fusion.2
  3.6 0.1 slice_add_fusion
  3.7 0.1 slice.30
  3.7 0.1 convert_element_type.76
  3.8 0.2 copy.11
  4.0 0.2 fusion.9
  4.2 0.0 copy-done.1
  4.3 2.0 %convolution_convert_fusion = bf16[1024,896]{1,0:T(8,128)(2,1)} fusion(bf16[1024,2]{1,0:T(8,128)(2,1)S(1)} %copy.11, bf16[1024,128]{1,0:T(8,128)(2,1)S(1)} %fusion.9, bf16[128,768]{1,0:T(8,128)(2,1)S(1)} %copy-done.1, bf16[2,896]{1,0:T(2,128)(2,1)S(1)} %pad_convert_fusion), kind=kOutput, calls=%fused_computation.2 | convolution fusion | flops 240699904 | bytes 2301440 | tf_op jit(solution)/shard_map/dot_general | solution.py:65
  6.2 6.3 %all-to-all-start = ((bf16[16,64,896]{2,1,0:T(8,128)(2,1)}), bf16[16,64,896]{2,1,0:T(8,128)(2,1)S(1)}, u32[]{:S(2)}, u32[]{:S(2)}) async-start(bf16[16,64,896]{2,1,0:T(8,128)(2,1)} %bitcast.19), calls=%async_computation | async-start | bytes 3670016 | tf_op jit(solution)/shard_map/all_to_all | solution.py:69
  12.5 0.1 slice.34
  12.6 1.8 %convolution_convert_fusion.1 = bf16[1024,768]{1,0:T(8,128)(2,1)} fusion(bf16[128,768]{1,0:T(8,128)(2,1)S(1)} %copy-done.1, s32[1024]{0:T(1024)S(1)} %slice.34), kind=kOutput, calls=%fused_computation.3 | convolution fusion | flops 202244096 | bytes 1773568 | tf_op jit(solution)/shard_map/dot_general | solution.py:67
  14.4 22.2 %all-to-all-done = bf16[16,64,896]{2,1,0:T(8,128)(2,1)S(1)} async-done(((bf16[16,64,896]{2,1,0:T(8,128)(2,1)}), bf16[16,64,896]{2,1,0:T(8,128)(2,1)S(1)}, u32[]{:S(2)}, u32[]{:S(2)}) %all-to-all-start) | async-done | bytes 1835040 | tf_op jit(solution)/shard_map/all_to_all | solution.py:69
  36.6 3.7 %all-to-all-start.1 = ((bf16[16,64,768]{2,1,0:T(8,128)(2,1)}), bf16[16,64,768]{2,1,0:T(8,128)(2,1)S(1)}, u32[]{:S(2)}, u32[]{:S(2)}) async-start(bf16[16,64,768]{2,1,0:T(8,128)(2,1)} %bitcast.4), calls=%async_computation.1 | async-start | bytes 3145728 | tf_op jit(solution)/shard_map/all_to_all | solution.py:72
  40.3 0.4 add_reduce_fusion.1
  40.8 0.0 copy-start.2
  40.8 1.1 %fusion.1 = f32[96,768]{1,0:T(8,128)} fusion(bf16[1024,896]{1,0:T(8,128)(2,1)S(1)} %bitcast.18, s32[1024]{0:T(1024)S(1)} %get-tuple-element.4), kind=kOutput, calls=%fused_computation.4 | convolution fusion | flops 151093248 | bytes 1871872 | tf_op jit(solution)/shard_map/dot_general | solution.py:80
  41.9 2.6 %collective-permute-start = (f32[96,768]{1,0:T(8,128)}, f32[96,768]{1,0:T(8,128)S(1)}, u32[]{:S(2)}, u32[]{:S(2)}) collective-permute-start(f32[96,768]{1,0:T(8,128)} %fusion.1), channel_id=1, source_target_pairs={{0,4},{4,0},{1,5},{5,1},{2,6},{6,2},{3,7},{7,3},{8,12},{12,8},{9,1... | collective-permute-start | bytes 884744 | tf_op jit(solution)/shard_map/ppermute | solution.py:81
  44.5 23.1 %all-to-all-done.1 = bf16[16,64,768]{2,1,0:T(8,128)(2,1)S(1)} async-done(((bf16[16,64,768]{2,1,0:T(8,128)(2,1)}), bf16[16,64,768]{2,1,0:T(8,128)(2,1)S(1)}, u32[]{:S(2)}, u32[]{:S(2)}) %all-to-all-start.1) | async-done | bytes 1572896 | tf_op jit(solution)/shard_map/all_to_all | solution.py:72
  67.5 0.0 collective-permute-done
  67.5 0.5 multiply_reduce_fusion
  68.0 0.1 multiply_convert_fusion
  68.1 0.0 copy-done.2
  68.1 0.0 copy-start
  68.2 0.2 fusion.24
  68.4 17.5 %all_to_all.20 = f32[16,16,768]{2,1,0:T(8,128)S(1)} all-to-all(f32[16,16,768]{2,1,0:T(8,128)S(1)} %bitcast.16), channel_id=1, replica_groups=mesh['y'=2,'core'=2,'zh'=2,'zr'=4] {'y','core','zr'}, dimensions={0} | all-to-all | bytes 1572864 | tf_op jit(solution)/shard_map/all_to_all | solution.py:91
  86.0 0.6 collective-permute-start.1
  86.5 5.2 %collective-permute-done.1 = f32[16,768]{1,0:T(8,128)S(1)} collective-permute-done((f32[16,768]{1,0:T(8,128)S(1)}, f32[16,768]{1,0:T(8,128)S(1)}, u32[]{:S(2)}, u32[]{:S(2)}) %collective-permute-start.1) | collective-permute-done | bytes 49184 | tf_op jit(solution)/shard_map/ppermute | solution.py:95
  91.7 0.1 multiply_reduce_fusion.1
  91.9 0.1 multiply_convert_fusion.1
  92.0 10.7 %all_to_all.21 = bf16[16,16,768]{2,1,0:T(8,128)(2,1)S(1)} all-to-all(bf16[16,16,768]{2,1,0:T(8,128)(2,1)S(1)} %broadcast_in_dim.12), channel_id=1, replica_groups=mesh['y'=2,'core'=2,'zh'=2,'zr'=4] {'y','core','zr'}, dimensions={0} | all-to-all | bytes 786432 | tf_op jit(solution)/shard_map/all_to_all | solution.py:97
  102.7 0.0 copy-done
  102.7 0.9 fusion.4
  103.6 0.7 copy.13
  (10 shorter events, 0.2 us)
Async XLA Ops:
  0.6 3.6 %copy-start.1 = (bf16[128,768]{1,0:T(8,128)(2,1)S(1)}, bf16[128,768]{1,0:T(8,128)(2,1)}, u32[]{:S(2)}) copy-start(bf16[128,768]{1,0:T(8,128)(2,1)} %param.5) | copy-start | bytes 589828
  6.2 30.4 %all-to-all-start = ((bf16[16,64,896]{2,1,0:T(8,128)(2,1)}), bf16[16,64,896]{2,1,0:T(8,128)(2,1)S(1)}, u32[]{:S(2)}, u32[]{:S(2)}) async-start(bf16[16,64,896]{2,1,0:T(8,128)(2,1)} %bitcast.19), calls=%async_computation | async-start | bytes 3670016 | tf_op jit(solution)/shard_map/all_to_all | solution.py:69
  36.6 30.9 %all-to-all-start.1 = ((bf16[16,64,768]{2,1,0:T(8,128)(2,1)}), bf16[16,64,768]{2,1,0:T(8,128)(2,1)S(1)}, u32[]{:S(2)}, u32[]{:S(2)}) async-start(bf16[16,64,768]{2,1,0:T(8,128)(2,1)} %bitcast.4), calls=%async_computation.1 | async-start | bytes 3145728 | tf_op jit(solution)/shard_map/all_to_all | solution.py:72
  40.8 27.4 %copy-start.2 = (s32[96]{0:T(128)S(1)}, s32[96]{0:T(128)}, u32[]{:S(2)}) copy-start(s32[96]{0:T(128)} %param.9) | copy-start | bytes 1156
  41.9 25.6 %collective-permute-start = (f32[96,768]{1,0:T(8,128)}, f32[96,768]{1,0:T(8,128)S(1)}, u32[]{:S(2)}, u32[]{:S(2)}) collective-permute-start(f32[96,768]{1,0:T(8,128)} %fusion.1), channel_id=1, source_target_pairs={{0,4},{4,0},{1,5},{5,1},{2,6},{6,2},{3,7},{7,3},{8,12},{12,8},{9,1... | collective-permute-start | bytes 884744 | tf_op jit(solution)/shard_map/ppermute | solution.py:81
  68.1 34.5 %copy-start = (bf16[96,768]{1,0:T(8,128)(2,1)}, bf16[96,768]{1,0:T(8,128)(2,1)S(1)}, u32[]{:S(2)}) copy-start(bf16[96,768]{1,0:T(8,128)(2,1)S(1)} %multiply_convert_fusion) | copy-start | bytes 442372
  86.0 5.8 %collective-permute-start.1 = (f32[16,768]{1,0:T(8,128)S(1)}, f32[16,768]{1,0:T(8,128)S(1)}, u32[]{:S(2)}, u32[]{:S(2)}) collective-permute-start(f32[16,768]{1,0:T(8,128)S(1)} %reduce_sum.38), channel_id=1, source_target_pairs={{0,4},{4,0},{1,5},{5,1},{2,6},{6,2},{3,7},{7,3},{8,12},{12,8},{9,1... | collective-permute-start | bytes 147464 | tf_op jit(solution)/shard_map/ppermute | solution.py:95

commit v13 on v12

--- a/solution.py
+++ b/solution.py
@@ -53,16 +53,13 @@
     lanes = 128
     wide = width + lanes
     doc_part = (first_doc[:, None] == jnp.arange(docs, dtype=jnp.int32)[None, :]).astype(bf16)
-    slot_part = slot_plus.astype(bf16).reshape(2, group * capacity).T
-    chooser = jnp.concatenate([doc_part, slot_part], axis=1)
-    table = jnp.concatenate(
-        [
-            jnp.concatenate([doc_embed, jnp.zeros((docs, lanes), bf16)], axis=1),
-            jnp.concatenate([jnp.zeros((2, width), bf16), jnp.eye(2, lanes, dtype=bf16)], axis=1),
-        ],
-        axis=0,
+    table = jnp.concatenate([doc_embed, jnp.zeros((docs, lanes), bf16)], axis=1)
+    lane = jnp.arange(wide, dtype=jnp.int32)[None, :]
+    slot_pair = slot_plus.astype(f32).reshape(2, group * capacity)
+    slot_lanes = jnp.where(
+        lane == width, slot_pair[0][:, None], jnp.where(lane == width + 1, slot_pair[1][:, None], 0.0)
     )
-    send_first = jnp.dot(chooser, table, preferred_element_type=f32).astype(bf16)
+    send_first = (jnp.dot(doc_part, table, preferred_element_type=f32) + slot_lanes).astype(bf16)
     pick = (second_doc[:, None] == jnp.arange(docs, dtype=jnp.int32)[None, :]).astype(bf16)
     send_second = jnp.dot(pick, doc_embed, preferred_element_type=f32).astype(bf16)
 

time: 105 us -> 105 us (level)
  no operation moved by 1% of the time
where the time goes in v13:
time: 105 us; the launch traced here: 104 us
  waiting for transfers between devices  50.5 us (48%)
  blocking collectives  28.2 us (27%)
  starting transfers between devices  13.2 us (13%)
  matrix products  8.79 us (8%)
  other arithmetic  1.65 us (2%)
  local copies, waits for them, and re-layouts  1.08 us (1%)
    all_to_all x1, waiting for transfers between devices, local(): lax.all_to_all(send_second.reshape(group, capacity, width), near, split_a...  23.1 us
    all_to_all x1, waiting for transfers between devices, local(): lax.all_to_all(send_first.reshape(group, capacity, wide), near, split_axi...  22.2 us
    all_to_all x1, blocking collectives, local(): lax.all_to_all(partial_sums.reshape(group, share, width), near, split_axi...  17.5 us
    all_to_all x1, blocking collectives, local(): lax.all_to_all(jnp.broadcast_to(own[None], (group, share, width)), near,...  10.7 us
    all_to_all x1, starting transfers between devices, local(): lax.all_to_all(send_first.reshape(group, capacity, wide), near, split_axi...  6.32 us
    ppermute x1, waiting for transfers between devices, local(): sums = half_sums + lax.ppermute(half_sums, 'zh', [(0, 1), (1, 0)])  5.21 us
    all_to_all x1, starting transfers between devices, local(): lax.all_to_all(send_second.reshape(group, capacity, width), near, split_a...  3.71 us
    ppermute x1, starting transfers between devices, local(): mirrored = lax.ppermute(mirror_part, 'zh', [(0, 1), (1, 0)])  2.59 us
  transfers between devices with their start and end apart: 4, of which 3 were waited for; matrix products, arithmetic and copies ran while one was open for 3% of the time, Pallas kernels for 0%

profile of v13, /device:TPU:0, one launch (start us, length us, event | category | flops | bytes accessed | tf_op | source)
XLA Modules:
  0.0 104.1 jit_solution(4115568378687159012)
XLA Ops:
  0.6 0.0 copy-start.1
  0.7 1.2 %fusion.5 = f32[1024]{0:T(1024)S(1)} fusion(s32[1024]{0:T(1024)} %bitcast.19, s32[32]{0:T(128)S(1)} %fusion.22), kind=kOutput, calls=%fused_computation.10 | convolution fusion | flops 68353024 | bytes 8320 | tf_op jit(solution)/shard_map/dot_general | solution.py:35
  1.9 0.7 add_convert_fusion.1
  2.6 0.9 convolution_convert_fusion.1
  3.6 0.1 slice_add_fusion
  3.6 0.1 slice.43
  3.7 0.1 slice.46
  3.8 0.1 slice.48
  3.9 0.0 copy-done.1
  3.9 2.2 %add_convert_fusion = bf16[1024,896]{1,0:T(8,128)(2,1)} fusion(f32[1024]{0:T(1024)S(1)} %slice.48, f32[1024]{0:T(1024)S(1)} %slice.46, pred[896]{0:T(1024)(128)(4,1)S(1)} %get-tuple-element.19, pred[896]{0:T(1024)(128)(4,1)S(1)} %get-tuple-element.20, s32[1024]{0:T(1024)S(1)} %slice.43, bf16[128,768]{1,0:T(8,128)(2,1)S(1)} %copy-done.1), kind=kOutput, calls=%fused_computation.2 | convolution fusion | flops 238682112 | bytes 2045696 | tf_op jit(solution)/shard_map/dot_general | solution.py:62
  6.0 6.3 %all-to-all-start = ((bf16[16,64,896]{2,1,0:T(8,128)(2,1)}), bf16[16,64,896]{2,1,0:T(8,128)(2,1)S(1)}, u32[]{:S(2)}, u32[]{:S(2)}) async-start(bf16[16,64,896]{2,1,0:T(8,128)(2,1)} %bitcast.18), calls=%async_computation | async-start | bytes 3670016 | tf_op jit(solution)/shard_map/all_to_all | solution.py:66
  12.4 0.1 slice.51
  12.4 1.8 %convolution_convert_fusion = bf16[1024,768]{1,0:T(8,128)(2,1)} fusion(bf16[128,768]{1,0:T(8,128)(2,1)S(1)} %copy-done.1, s32[1024]{0:T(1024)S(1)} %slice.51), kind=kOutput, calls=%fused_computation.3 | convolution fusion | flops 202244096 | bytes 1773568 | tf_op jit(solution)/shard_map/dot_general | solution.py:64
  14.2 22.2 %all-to-all-done = bf16[16,64,896]{2,1,0:T(8,128)(2,1)S(1)} async-done(((bf16[16,64,896]{2,1,0:T(8,128)(2,1)}), bf16[16,64,896]{2,1,0:T(8,128)(2,1)S(1)}, u32[]{:S(2)}, u32[]{:S(2)}) %all-to-all-start) | async-done | bytes 1835040 | tf_op jit(solution)/shard_map/all_to_all | solution.py:66
  36.4 3.7 %all-to-all-start.1 = ((bf16[16,64,768]{2,1,0:T(8,128)(2,1)}), bf16[16,64,768]{2,1,0:T(8,128)(2,1)S(1)}, u32[]{:S(2)}, u32[]{:S(2)}) async-start(bf16[16,64,768]{2,1,0:T(8,128)(2,1)} %bitcast.3), calls=%async_computation.1 | async-start | bytes 3145728 | tf_op jit(solution)/shard_map/all_to_all | solution.py:69
  40.2 0.4 add_reduce_fusion.1
  40.6 0.0 copy-start.2
  40.6 1.1 %fusion.1 = f32[96,768]{1,0:T(8,128)} fusion(bf16[1024,896]{1,0:T(8,128)(2,1)S(1)} %bitcast.17, s32[1024]{0:T(1024)S(1)} %get-tuple-element.4), kind=kOutput, calls=%fused_computation.4 | convolution fusion | flops 151093248 | bytes 1871872 | tf_op jit(solution)/shard_map/dot_general | solution.py:77
  41.7 2.6 %collective-permute-start = (f32[96,768]{1,0:T(8,128)}, f32[96,768]{1,0:T(8,128)S(1)}, u32[]{:S(2)}, u32[]{:S(2)}) collective-permute-start(f32[96,768]{1,0:T(8,128)} %fusion.1), channel_id=1, source_target_pairs={{0,4},{4,0},{1,5},{5,1},{2,6},{6,2},{3,7},{7,3},{8,12},{12,8},{9,1... | collective-permute-start | bytes 884744 | tf_op jit(solution)/shard_map/ppermute | solution.py:78
  44.3 23.1 %all-to-all-done.1 = bf16[16,64,768]{2,1,0:T(8,128)(2,1)S(1)} async-done(((bf16[16,64,768]{2,1,0:T(8,128)(2,1)}), bf16[16,64,768]{2,1,0:T(8,128)(2,1)S(1)}, u32[]{:S(2)}, u32[]{:S(2)}) %all-to-all-start.1) | async-done | bytes 1572896 | tf_op jit(solution)/shard_map/all_to_all | solution.py:69
  67.4 0.0 collective-permute-done
  67.4 0.5 multiply_reduce_fusion
  67.8 0.1 multiply_convert_fusion
  68.0 0.0 copy-done.2
  68.0 0.0 copy-start
  68.0 0.2 fusion.16
  68.2 17.5 %all_to_all.20 = f32[16,16,768]{2,1,0:T(8,128)S(1)} all-to-all(f32[16,16,768]{2,1,0:T(8,128)S(1)} %bitcast.15), channel_id=1, replica_groups=mesh['y'=2,'core'=2,'zh'=2,'zr'=4] {'y','core','zr'}, dimensions={0} | all-to-all | bytes 1572864 | tf_op jit(solution)/shard_map/all_to_all | solution.py:88
  85.8 0.6 collective-permute-start.1
  86.3 5.2 %collective-permute-done.1 = f32[16,768]{1,0:T(8,128)S(1)} collective-permute-done((f32[16,768]{1,0:T(8,128)S(1)}, f32[16,768]{1,0:T(8,128)S(1)}, u32[]{:S(2)}, u32[]{:S(2)}) %collective-permute-start.1) | collective-permute-done | bytes 49184 | tf_op jit(solution)/shard_map/ppermute | solution.py:92
  91.5 0.1 multiply_reduce_fusion.1
  91.7 0.1 multiply_convert_fusion.1
  91.8 10.7 %all_to_all.21 = bf16[16,16,768]{2,1,0:T(8,128)(2,1)S(1)} all-to-all(bf16[16,16,768]{2,1,0:T(8,128)(2,1)S(1)} %broadcast_in_dim.76), channel_id=1, replica_groups=mesh['y'=2,'core'=2,'zh'=2,'zr'=4] {'y','core','zr'}, dimensions={0} | all-to-all | bytes 786432 | tf_op jit(solution)/shard_map/all_to_all | solution.py:94
  102.5 0.0 copy-done
  102.5 0.9 fusion.4
  103.4 0.7 copy.10
  (10 shorter events, 0.2 us)
Async XLA Ops:
  0.6 3.2 %copy-start.1 = (bf16[128,768]{1,0:T(8,128)(2,1)S(1)}, bf16[128,768]{1,0:T(8,128)(2,1)}, u32[]{:S(2)}) copy-start(bf16[128,768]{1,0:T(8,128)(2,1)} %param.5) | copy-start | bytes 589828
  6.0 30.4 %all-to-all-start = ((bf16[16,64,896]{2,1,0:T(8,128)(2,1)}), bf16[16,64,896]{2,1,0:T(8,128)(2,1)S(1)}, u32[]{:S(2)}, u32[]{:S(2)}) async-start(bf16[16,64,896]{2,1,0:T(8,128)(2,1)} %bitcast.18), calls=%async_computation | async-start | bytes 3670016 | tf_op jit(solution)/shard_map/all_to_all | solution.py:66
  36.4 30.9 %all-to-all-start.1 = ((bf16[16,64,768]{2,1,0:T(8,128)(2,1)}), bf16[16,64,768]{2,1,0:T(8,128)(2,1)S(1)}, u32[]{:S(2)}, u32[]{:S(2)}) async-start(bf16[16,64,768]{2,1,0:T(8,128)(2,1)} %bitcast.3), calls=%async_computation.1 | async-start | bytes 3145728 | tf_op jit(solution)/shard_map/all_to_all | solution.py:69
  40.6 27.4 %copy-start.2 = (s32[96]{0:T(128)S(1)}, s32[96]{0:T(128)}, u32[]{:S(2)}) copy-start(s32[96]{0:T(128)} %param.9) | copy-start | bytes 1156
  41.7 25.6 %collective-permute-start = (f32[96,768]{1,0:T(8,128)}, f32[96,768]{1,0:T(8,128)S(1)}, u32[]{:S(2)}, u32[]{:S(2)}) collective-permute-start(f32[96,768]{1,0:T(8,128)} %fusion.1), channel_id=1, source_target_pairs={{0,4},{4,0},{1,5},{5,1},{2,6},{6,2},{3,7},{7,3},{8,12},{12,8},{9,1... | collective-permute-start | bytes 884744 | tf_op jit(solution)/shard_map/ppermute | solution.py:78
  68.0 34.5 %copy-start = (bf16[96,768]{1,0:T(8,128)(2,1)}, bf16[96,768]{1,0:T(8,128)(2,1)S(1)}, u32[]{:S(2)}) copy-start(bf16[96,768]{1,0:T(8,128)(2,1)S(1)} %multiply_convert_fusion) | copy-start | bytes 442372
  85.8 5.8 %collective-permute-start.1 = (f32[16,768]{1,0:T(8,128)S(1)}, f32[16,768]{1,0:T(8,128)S(1)}, u32[]{:S(2)}, u32[]{:S(2)}) collective-permute-start(f32[16,768]{1,0:T(8,128)S(1)} %reduce_sum.38), channel_id=1, source_target_pairs={{0,4},{4,0},{1,5},{5,1},{2,6},{6,2},{3,7},{7,3},{8,12},{12,8},{9,1... | collective-permute-start | bytes 147464 | tf_op jit(solution)/shard_map/ppermute | solution.py:92

commit v14 on v13

--- a/solution.py
+++ b/solution.py
@@ -12,7 +12,7 @@
 
 def local(doc_embed, pair_doc, pair_owner, pair_slot, label_cluster):
     axes = ("y", "core", "zh", "zr")
-    near = ("y", "core", "zr")
+    near = ("zr", "y", "core")
     devices = lax.axis_size(axes)
     halves = lax.axis_size("zr")
     group = devices // 2
@@ -26,7 +26,8 @@
     b = jnp.arange(devices, dtype=jnp.int32)
     b_later, b_proxy = b // group, b % group
     b_zh = jnp.where(b_later == 1, me, 1 - me)
-    block_owner = (b_proxy // halves) * (2 * halves) + b_zh * halves + b_proxy % halves
+    rows = group // halves
+    block_owner = (b_proxy % rows) * (2 * halves) + b_zh * halves + b_proxy // rows
 
     owner_row = pair_owner.reshape(1, pairs)
     hits_t = (block_owner[:, None] == owner_row).astype(bf16)

time: 105 us -> 109 us (1.038)
  waiting for transfers between devices: 50.5 us -> 53.1 us
  blocking collectives: 28.2 us -> 29.8 us
    all_to_all x1, waiting for transfers between devices: 22.2 us -> 24.2 us  [local(): lax.all_to_all(send_first.reshape(group, capacity, wide), near, split_axi...]
where the time goes in v14:
time: 109 us; the launch traced here: 108 us
  waiting for transfers between devices  53.1 us (49%)
  blocking collectives  29.8 us (27%)
  starting transfers between devices  13.3 us (12%)
  matrix products  8.79 us (8%)
  other arithmetic  1.65 us (2%)
    all_to_all x1, waiting for transfers between devices, local(): lax.all_to_all(send_first.reshape(group, capacity, wide), near, split_axi...  24.2 us
    all_to_all x1, waiting for transfers between devices, local(): lax.all_to_all(send_second.reshape(group, capacity, width), near, split_a...  23.9 us
    all_to_all x1, blocking collectives, local(): lax.all_to_all(partial_sums.reshape(group, share, width), near, split_axi...  18.1 us
    all_to_all x1, blocking collectives, local(): lax.all_to_all(jnp.broadcast_to(own[None], (group, share, width)), near,...  11.7 us
    all_to_all x1, starting transfers between devices, local(): lax.all_to_all(send_first.reshape(group, capacity, wide), near, split_axi...  6.32 us
    ppermute x1, waiting for transfers between devices, local(): sums = half_sums + lax.ppermute(half_sums, 'zh', [(0, 1), (1, 0)])  4.86 us
    all_to_all x1, starting transfers between devices, local(): lax.all_to_all(send_second.reshape(group, capacity, width), near, split_a...  3.71 us
    ppermute x1, starting transfers between devices, local(): mirrored = lax.ppermute(mirror_part, 'zh', [(0, 1), (1, 0)])  2.59 us
  transfers between devices with their start and end apart: 4, of which 3 were waited for; matrix products, arithmetic and copies ran while one was open for 3% of the time, Pallas kernels for 0%

profile of v14, /device:TPU:0, one launch (start us, length us, event | category | flops | bytes accessed | tf_op | source)
XLA Modules:
  0.0 108.5 jit_solution(1792593049899321706)
XLA Ops:
  0.6 0.0 copy-start.1
  0.7 1.2 %fusion.5 = f32[1024]{0:T(1024)S(1)} fusion(s32[1024]{0:T(1024)} %bitcast.19, s32[32]{0:T(128)S(1)} %fusion.24), kind=kOutput, calls=%fused_computation.10 | convolution fusion | flops 68353024 | bytes 8320 | tf_op jit(solution)/shard_map/dot_general | solution.py:36
  1.9 0.7 add_convert_fusion.1
  2.6 0.9 convolution_convert_fusion.1
  3.6 0.1 slice_add_fusion
  3.6 0.1 slice.43
  3.7 0.1 slice.46
  3.8 0.1 slice.48
  3.9 0.0 copy-done.1
  3.9 2.2 %add_convert_fusion = bf16[1024,896]{1,0:T(8,128)(2,1)} fusion(f32[1024]{0:T(1024)S(1)} %slice.48, f32[1024]{0:T(1024)S(1)} %slice.46, pred[896]{0:T(1024)(128)(4,1)S(1)} %get-tuple-element.19, pred[896]{0:T(1024)(128)(4,1)S(1)} %get-tuple-element.20, s32[1024]{0:T(1024)S(1)} %slice.43, bf16[128,768]{1,0:T(8,128)(2,1)S(1)} %copy-done.1), kind=kOutput, calls=%fused_computation.2 | convolution fusion | flops 238682112 | bytes 2045696 | tf_op jit(solution)/shard_map/dot_general | solution.py:63
  6.0 6.3 %all-to-all-start = ((bf16[16,64,896]{2,1,0:T(8,128)(2,1)}), bf16[16,64,896]{2,1,0:T(8,128)(2,1)S(1)}, u32[]{:S(2)}, u32[]{:S(2)}) async-start(bf16[16,64,896]{2,1,0:T(8,128)(2,1)} %bitcast.18), calls=%async_computation | async-start | bytes 3670016 | tf_op jit(solution)/shard_map/all_to_all | solution.py:67
  12.4 0.1 slice.51
  12.4 1.8 %convolution_convert_fusion = bf16[1024,768]{1,0:T(8,128)(2,1)} fusion(bf16[128,768]{1,0:T(8,128)(2,1)S(1)} %copy-done.1, s32[1024]{0:T(1024)S(1)} %slice.51), kind=kOutput, calls=%fused_computation.3 | convolution fusion | flops 202244096 | bytes 1773568 | tf_op jit(solution)/shard_map/dot_general | solution.py:65
  14.2 24.2 %all-to-all-done = bf16[16,64,896]{2,1,0:T(8,128)(2,1)S(1)} async-done(((bf16[16,64,896]{2,1,0:T(8,128)(2,1)}), bf16[16,64,896]{2,1,0:T(8,128)(2,1)S(1)}, u32[]{:S(2)}, u32[]{:S(2)}) %all-to-all-start) | async-done | bytes 1835040 | tf_op jit(solution)/shard_map/all_to_all | solution.py:67
  38.5 3.7 %all-to-all-start.1 = ((bf16[16,64,768]{2,1,0:T(8,128)(2,1)}), bf16[16,64,768]{2,1,0:T(8,128)(2,1)S(1)}, u32[]{:S(2)}, u32[]{:S(2)}) async-start(bf16[16,64,768]{2,1,0:T(8,128)(2,1)} %bitcast.3), calls=%async_computation.1 | async-start | bytes 3145728 | tf_op jit(solution)/shard_map/all_to_all | solution.py:70
  42.2 0.4 add_reduce_fusion.1
  42.6 0.0 copy-start.2
  42.6 1.1 %fusion.1 = f32[96,768]{1,0:T(8,128)} fusion(bf16[1024,896]{1,0:T(8,128)(2,1)S(1)} %bitcast.17, s32[1024]{0:T(1024)S(1)} %get-tuple-element.4), kind=kOutput, calls=%fused_computation.4 | convolution fusion | flops 151093248 | bytes 1871872 | tf_op jit(solution)/shard_map/dot_general | solution.py:78
  43.7 2.6 %collective-permute-start = (f32[96,768]{1,0:T(8,128)}, f32[96,768]{1,0:T(8,128)S(1)}, u32[]{:S(2)}, u32[]{:S(2)}) collective-permute-start(f32[96,768]{1,0:T(8,128)} %fusion.1), channel_id=1, source_target_pairs={{0,4},{4,0},{1,5},{5,1},{2,6},{6,2},{3,7},{7,3},{8,12},{12,8},{9,1... | collective-permute-start | bytes 884744 | tf_op jit(solution)/shard_map/ppermute | solution.py:79
  46.3 23.9 %all-to-all-done.1 = bf16[16,64,768]{2,1,0:T(8,128)(2,1)S(1)} async-done(((bf16[16,64,768]{2,1,0:T(8,128)(2,1)}), bf16[16,64,768]{2,1,0:T(8,128)(2,1)S(1)}, u32[]{:S(2)}, u32[]{:S(2)}) %all-to-all-start.1) | async-done | bytes 1572896 | tf_op jit(solution)/shard_map/all_to_all | solution.py:70
  70.3 0.0 collective-permute-done
  70.3 0.5 multiply_reduce_fusion
  70.7 0.1 multiply_convert_fusion
  70.8 0.0 copy-done.2
  70.9 0.0 copy-start
  70.9 0.2 fusion.16
  71.1 18.1 %all_to_all.20 = f32[16,16,768]{2,1,0:T(8,128)S(1)} all-to-all(f32[16,16,768]{2,1,0:T(8,128)S(1)} %bitcast.15), channel_id=1, replica_groups=mesh['y'=2,'core'=2,'zh'=2,'zr'=4] {'zr','y','core'}, dimensions={0} | all-to-all | bytes 1572864 | tf_op jit(solution)/shard_map/all_to_all | solution.py:89
  89.2 0.7 collective-permute-start.1
  90.0 4.9 %collective-permute-done.1 = f32[16,768]{1,0:T(8,128)S(1)} collective-permute-done((f32[16,768]{1,0:T(8,128)S(1)}, f32[16,768]{1,0:T(8,128)S(1)}, u32[]{:S(2)}, u32[]{:S(2)}) %collective-permute-start.1) | collective-permute-done | bytes 49184 | tf_op jit(solution)/shard_map/ppermute | solution.py:93
  94.8 0.1 multiply_reduce_fusion.1
  95.0 0.1 multiply_convert_fusion.1
  95.1 11.7 %all_to_all.21 = bf16[16,16,768]{2,1,0:T(8,128)(2,1)S(1)} all-to-all(bf16[16,16,768]{2,1,0:T(8,128)(2,1)S(1)} %broadcast_in_dim.76), channel_id=1, replica_groups=mesh['y'=2,'core'=2,'zh'=2,'zr'=4] {'zr','y','core'}, dimensions={0} | all-to-all | bytes 786432 | tf_op jit(solution)/shard_map/all_to_all | solution.py:95
  106.8 0.0 copy-done
  106.8 0.9 fusion.4
  107.7 0.7 copy.10
  (10 shorter events, 0.2 us)
Async XLA Ops:
  0.6 3.2 %copy-start.1 = (bf16[128,768]{1,0:T(8,128)(2,1)S(1)}, bf16[128,768]{1,0:T(8,128)(2,1)}, u32[]{:S(2)}) copy-start(bf16[128,768]{1,0:T(8,128)(2,1)} %param.5) | copy-start | bytes 589828
  6.0 32.4 %all-to-all-start = ((bf16[16,64,896]{2,1,0:T(8,128)(2,1)}), bf16[16,64,896]{2,1,0:T(8,128)(2,1)S(1)}, u32[]{:S(2)}, u32[]{:S(2)}) async-start(bf16[16,64,896]{2,1,0:T(8,128)(2,1)} %bitcast.18), calls=%async_computation | async-start | bytes 3670016 | tf_op jit(solution)/shard_map/all_to_all | solution.py:67
  38.5 31.8 %all-to-all-start.1 = ((bf16[16,64,768]{2,1,0:T(8,128)(2,1)}), bf16[16,64,768]{2,1,0:T(8,128)(2,1)S(1)}, u32[]{:S(2)}, u32[]{:S(2)}) async-start(bf16[16,64,768]{2,1,0:T(8,128)(2,1)} %bitcast.3), calls=%async_computation.1 | async-start | bytes 3145728 | tf_op jit(solution)/shard_map/all_to_all | solution.py:70
  42.6 28.2 %copy-start.2 = (s32[96]{0:T(128)S(1)}, s32[96]{0:T(128)}, u32[]{:S(2)}) copy-start(s32[96]{0:T(128)} %param.9) | copy-start | bytes 1156
  43.7 26.5 %collective-permute-start = (f32[96,768]{1,0:T(8,128)}, f32[96,768]{1,0:T(8,128)S(1)}, u32[]{:S(2)}, u32[]{:S(2)}) collective-permute-start(f32[96,768]{1,0:T(8,128)} %fusion.1), channel_id=1, source_target_pairs={{0,4},{4,0},{1,5},{5,1},{2,6},{6,2},{3,7},{7,3},{8,12},{12,8},{9,1... | collective-permute-start | bytes 884744 | tf_op jit(solution)/shard_map/ppermute | solution.py:79
  70.9 35.9 %copy-start = (bf16[96,768]{1,0:T(8,128)(2,1)}, bf16[96,768]{1,0:T(8,128)(2,1)S(1)}, u32[]{:S(2)}) copy-start(bf16[96,768]{1,0:T(8,128)(2,1)S(1)} %multiply_convert_fusion) | copy-start | bytes 442372
  89.2 5.6 %collective-permute-start.1 = (f32[16,768]{1,0:T(8,128)S(1)}, f32[16,768]{1,0:T(8,128)S(1)}, u32[]{:S(2)}, u32[]{:S(2)}) collective-permute-start(f32[16,768]{1,0:T(8,128)S(1)} %reduce_sum.38), channel_id=1, source_target_pairs={{0,4},{4,0},{1,5},{5,1},{2,6},{6,2},{3,7},{7,3},{8,12},{12,8},{9,1... | collective-permute-start | bytes 147464 | tf_op jit(solution)/shard_map/ppermute | solution.py:93

commit v15 on v13

--- a/solution.py
+++ b/solution.py
@@ -12,7 +12,7 @@
 
 def local(doc_embed, pair_doc, pair_owner, pair_slot, label_cluster):
     axes = ("y", "core", "zh", "zr")
-    near = ("y", "core", "zr")
+    near = ("y", "zr", "core")
     devices = lax.axis_size(axes)
     halves = lax.axis_size("zr")
     group = devices // 2
@@ -26,7 +26,12 @@
     b = jnp.arange(devices, dtype=jnp.int32)
     b_later, b_proxy = b // group, b % group
     b_zh = jnp.where(b_later == 1, me, 1 - me)
-    block_owner = (b_proxy // halves) * (2 * halves) + b_zh * halves + b_proxy % halves
+    place = {}
+    for name in reversed(near):
+        size = lax.axis_size(name)
+        place[name], b_proxy = b_proxy % size, b_proxy // size
+    b_row = place["y"] * 2 + place["core"]
+    block_owner = b_row * (2 * halves) + b_zh * halves + place["zr"]
 
     owner_row = pair_owner.reshape(1, pairs)
     hits_t = (block_owner[:, None] == owner_row).astype(bf16)

time: 105 us -> 108 us (1.029)
  waiting for transfers between devices: 50.5 us -> 53.5 us
    all_to_all x1, waiting for transfers between devices: 22.2 us -> 24 us  [local(): lax.all_to_all(send_first.reshape(group, capacity, wide), near, split_axi...]
    all_to_all x1, waiting for transfers between devices: 23.1 us -> 24.5 us  [local(): lax.all_to_all(send_second.reshape(group, capacity, width), near, split_a...]
where the time goes in v15:
time: 108 us; the launch traced here: 107 us
  waiting for transfers between devices  53.5 us (50%)
  blocking collectives  28.9 us (27%)
  starting transfers between devices  12.7 us (12%)
  matrix products  8.79 us (8%)
  other arithmetic  1.66 us (2%)
  local copies, waits for them, and re-layouts  1.08 us (1%)
    all_to_all x1, waiting for transfers between devices, local(): lax.all_to_all(send_second.reshape(group, capacity, width), near, split_a...  24.5 us
    all_to_all x1, waiting for transfers between devices, local(): lax.all_to_all(send_first.reshape(group, capacity, wide), near, split_axi...  24 us
    all_to_all x1, blocking collectives, local(): lax.all_to_all(partial_sums.reshape(group, share, width), near, split_axi...  17.2 us
    all_to_all x1, blocking collectives, local(): lax.all_to_all(jnp.broadcast_to(own[None], (group, share, width)), near,...  11.7 us
    all_to_all x1, starting transfers between devices, local(): lax.all_to_all(send_first.reshape(group, capacity, wide), near, split_axi...  6.32 us
    ppermute x1, waiting for transfers between devices, local(): sums = half_sums + lax.ppermute(half_sums, 'zh', [(0, 1), (1, 0)])  4.98 us
    all_to_all x1, starting transfers between devices, local(): lax.all_to_all(send_second.reshape(group, capacity, width), near, split_a...  3.71 us
    ppermute x1, starting transfers between devices, local(): mirrored = lax.ppermute(mirror_part, 'zh', [(0, 1), (1, 0)])  2.59 us
  transfers between devices with their start and end apart: 4, of which 3 were waited for; matrix products, arithmetic and copies ran while one was open for 3% of the time, Pallas kernels for 0%

profile of v15, /device:TPU:0, one launch (start us, length us, event | category | flops | bytes accessed | tf_op | source)
XLA Modules:
  0.0 107.4 jit_solution(7794148812328746907)
XLA Ops:
  0.6 0.0 copy-start.1
  0.7 1.2 %fusion.5 = f32[1024]{0:T(1024)S(1)} fusion(s32[1024]{0:T(1024)} %bitcast.19, s32[32]{0:T(128)S(1)} %fusion.23), kind=kOutput, calls=%fused_computation.10 | convolution fusion | flops 68353024 | bytes 8320 | tf_op jit(solution)/shard_map/dot_general | solution.py:40
  1.9 0.7 add_convert_fusion.1
  2.7 0.9 convolution_convert_fusion.1
  3.6 0.1 slice_add_fusion
  3.7 0.1 slice.43
  3.7 0.1 slice.46
  3.8 0.1 slice.48
  3.9 0.0 copy-done.1
  3.9 2.2 %add_convert_fusion = bf16[1024,896]{1,0:T(8,128)(2,1)} fusion(f32[1024]{0:T(1024)S(1)} %slice.48, f32[1024]{0:T(1024)S(1)} %slice.46, pred[896]{0:T(1024)(128)(4,1)S(1)} %get-tuple-element.19, pred[896]{0:T(1024)(128)(4,1)S(1)} %get-tuple-element.20, s32[1024]{0:T(1024)S(1)} %slice.43, bf16[128,768]{1,0:T(8,128)(2,1)S(1)} %copy-done.1), kind=kOutput, calls=%fused_computation.2 | convolution fusion | flops 238682112 | bytes 2045696 | tf_op jit(solution)/shard_map/dot_general | solution.py:67
  6.0 6.3 %all-to-all-start = ((bf16[16,64,896]{2,1,0:T(8,128)(2,1)}), bf16[16,64,896]{2,1,0:T(8,128)(2,1)S(1)}, u32[]{:S(2)}, u32[]{:S(2)}) async-start(bf16[16,64,896]{2,1,0:T(8,128)(2,1)} %bitcast.18), calls=%async_computation | async-start | bytes 3670016 | tf_op jit(solution)/shard_map/all_to_all | solution.py:71
  12.4 0.1 slice.51
  12.4 1.8 %convolution_convert_fusion = bf16[1024,768]{1,0:T(8,128)(2,1)} fusion(bf16[128,768]{1,0:T(8,128)(2,1)S(1)} %copy-done.1, s32[1024]{0:T(1024)S(1)} %slice.51), kind=kOutput, calls=%fused_computation.3 | convolution fusion | flops 202244096 | bytes 1773568 | tf_op jit(solution)/shard_map/dot_general | solution.py:69
  14.2 24.0 %all-to-all-done = bf16[16,64,896]{2,1,0:T(8,128)(2,1)S(1)} async-done(((bf16[16,64,896]{2,1,0:T(8,128)(2,1)}), bf16[16,64,896]{2,1,0:T(8,128)(2,1)S(1)}, u32[]{:S(2)}, u32[]{:S(2)}) %all-to-all-start) | async-done | bytes 1835040 | tf_op jit(solution)/shard_map/all_to_all | solution.py:71
  38.2 3.7 %all-to-all-start.1 = ((bf16[16,64,768]{2,1,0:T(8,128)(2,1)}), bf16[16,64,768]{2,1,0:T(8,128)(2,1)S(1)}, u32[]{:S(2)}, u32[]{:S(2)}) async-start(bf16[16,64,768]{2,1,0:T(8,128)(2,1)} %bitcast.3), calls=%async_computation.1 | async-start | bytes 3145728 | tf_op jit(solution)/shard_map/all_to_all | solution.py:74
  41.9 0.4 add_reduce_fusion.1
  42.4 0.0 copy-start.2
  42.4 1.1 %fusion.1 = f32[96,768]{1,0:T(8,128)} fusion(bf16[1024,896]{1,0:T(8,128)(2,1)S(1)} %bitcast.17, s32[1024]{0:T(1024)S(1)} %get-tuple-element.4), kind=kOutput, calls=%fused_computation.4 | convolution fusion | flops 151093248 | bytes 1871872 | tf_op jit(solution)/shard_map/dot_general | solution.py:82
  43.5 2.6 %collective-permute-start = (f32[96,768]{1,0:T(8,128)}, f32[96,768]{1,0:T(8,128)S(1)}, u32[]{:S(2)}, u32[]{:S(2)}) collective-permute-start(f32[96,768]{1,0:T(8,128)} %fusion.1), channel_id=1, source_target_pairs={{0,4},{4,0},{1,5},{5,1},{2,6},{6,2},{3,7},{7,3},{8,12},{12,8},{9,1... | collective-permute-start | bytes 884744 | tf_op jit(solution)/shard_map/ppermute | solution.py:83
  46.1 24.5 %all-to-all-done.1 = bf16[16,64,768]{2,1,0:T(8,128)(2,1)S(1)} async-done(((bf16[16,64,768]{2,1,0:T(8,128)(2,1)}), bf16[16,64,768]{2,1,0:T(8,128)(2,1)S(1)}, u32[]{:S(2)}, u32[]{:S(2)}) %all-to-all-start.1) | async-done | bytes 1572896 | tf_op jit(solution)/shard_map/all_to_all | solution.py:74
  70.6 0.0 collective-permute-done
  70.6 0.5 multiply_reduce_fusion
  71.1 0.1 multiply_convert_fusion
  71.2 0.0 copy-done.2
  71.2 0.0 copy-start
  71.2 0.2 fusion.16
  71.5 17.2 %all_to_all.20 = f32[16,16,768]{2,1,0:T(8,128)S(1)} all-to-all(f32[16,16,768]{2,1,0:T(8,128)S(1)} %bitcast.15), channel_id=1, replica_groups=mesh['y'=2,'core'=2,'zh'=2,'zr'=4] {'y','zr','core'}, dimensions={0} | all-to-all | bytes 1572864 | tf_op jit(solution)/shard_map/all_to_all | solution.py:93
  88.7 0.1 collective-permute-start.1
  88.8 5.0 %collective-permute-done.1 = f32[16,768]{1,0:T(8,128)S(1)} collective-permute-done((f32[16,768]{1,0:T(8,128)S(1)}, f32[16,768]{1,0:T(8,128)S(1)}, u32[]{:S(2)}, u32[]{:S(2)}) %collective-permute-start.1) | collective-permute-done | bytes 49184 | tf_op jit(solution)/shard_map/ppermute | solution.py:97
  93.8 0.1 multiply_reduce_fusion.1
  93.9 0.1 multiply_convert_fusion.1
  94.1 11.7 %all_to_all.21 = bf16[16,16,768]{2,1,0:T(8,128)(2,1)S(1)} all-to-all(bf16[16,16,768]{2,1,0:T(8,128)(2,1)S(1)} %broadcast_in_dim.76), channel_id=1, replica_groups=mesh['y'=2,'core'=2,'zh'=2,'zr'=4] {'y','zr','core'}, dimensions={0} | all-to-all | bytes 786432 | tf_op jit(solution)/shard_map/all_to_all | solution.py:99
  105.8 0.0 copy-done
  105.8 0.9 fusion.4
  106.7 0.7 copy.10
  (10 shorter events, 0.2 us)
Async XLA Ops:
  0.6 3.2 %copy-start.1 = (bf16[128,768]{1,0:T(8,128)(2,1)S(1)}, bf16[128,768]{1,0:T(8,128)(2,1)}, u32[]{:S(2)}) copy-start(bf16[128,768]{1,0:T(8,128)(2,1)} %param.5) | copy-start | bytes 589828
  6.0 32.2 %all-to-all-start = ((bf16[16,64,896]{2,1,0:T(8,128)(2,1)}), bf16[16,64,896]{2,1,0:T(8,128)(2,1)S(1)}, u32[]{:S(2)}, u32[]{:S(2)}) async-start(bf16[16,64,896]{2,1,0:T(8,128)(2,1)} %bitcast.18), calls=%async_computation | async-start | bytes 3670016 | tf_op jit(solution)/shard_map/all_to_all | solution.py:71
  38.2 32.4 %all-to-all-start.1 = ((bf16[16,64,768]{2,1,0:T(8,128)(2,1)}), bf16[16,64,768]{2,1,0:T(8,128)(2,1)S(1)}, u32[]{:S(2)}, u32[]{:S(2)}) async-start(bf16[16,64,768]{2,1,0:T(8,128)(2,1)} %bitcast.3), calls=%async_computation.1 | async-start | bytes 3145728 | tf_op jit(solution)/shard_map/all_to_all | solution.py:74
  42.4 28.8 %copy-start.2 = (s32[96]{0:T(128)S(1)}, s32[96]{0:T(128)}, u32[]{:S(2)}) copy-start(s32[96]{0:T(128)} %param.9) | copy-start | bytes 1156
  43.5 27.1 %collective-permute-start = (f32[96,768]{1,0:T(8,128)}, f32[96,768]{1,0:T(8,128)S(1)}, u32[]{:S(2)}, u32[]{:S(2)}) collective-permute-start(f32[96,768]{1,0:T(8,128)} %fusion.1), channel_id=1, source_target_pairs={{0,4},{4,0},{1,5},{5,1},{2,6},{6,2},{3,7},{7,3},{8,12},{12,8},{9,1... | collective-permute-start | bytes 884744 | tf_op jit(solution)/shard_map/ppermute | solution.py:83
  71.2 34.6 %copy-start = (bf16[96,768]{1,0:T(8,128)(2,1)}, bf16[96,768]{1,0:T(8,128)(2,1)S(1)}, u32[]{:S(2)}) copy-start(bf16[96,768]{1,0:T(8,128)(2,1)S(1)} %multiply_convert_fusion) | copy-start | bytes 442372
  88.7 5.1 %collective-permute-start.1 = (f32[16,768]{1,0:T(8,128)S(1)}, f32[16,768]{1,0:T(8,128)S(1)}, u32[]{:S(2)}, u32[]{:S(2)}) collective-permute-start(f32[16,768]{1,0:T(8,128)S(1)} %reduce_sum.38), channel_id=1, source_target_pairs={{0,4},{4,0},{1,5},{5,1},{2,6},{6,2},{3,7},{7,3},{8,12},{12,8},{9,1... | collective-permute-start | bytes 147464 | tf_op jit(solution)/shard_map/ppermute | solution.py:97

commit v16 on v15

--- a/solution.py
+++ b/solution.py
@@ -12,7 +12,7 @@
 
 def local(doc_embed, pair_doc, pair_owner, pair_slot, label_cluster):
     axes = ("y", "core", "zh", "zr")
-    near = ("y", "zr", "core")
+    near = ("core", "y", "zr")
     devices = lax.axis_size(axes)
     halves = lax.axis_size("zr")
     group = devices // 2

time: 108 us -> 106 us (0.981)
  waiting for transfers between devices: 53.5 us -> 49.3 us
  blocking collectives: 28.9 us -> 30.2 us
  starting transfers between devices: 12.7 us -> 14 us
    all_to_all x1, waiting for transfers between devices: 24 us -> 21.3 us  [local(): lax.all_to_all(send_first.reshape(group, capacity, wide), near, split_axi...]
    all_to_all x1, waiting for transfers between devices: 24.5 us -> 22.5 us  [local(): lax.all_to_all(send_second.reshape(group, capacity, width), near, split_a...]
    all_to_all x1, blocking collectives: 17.2 us -> 19 us  [local(): lax.all_to_all(partial_sums.reshape(group, share, width), near, split_axi...]
    all_to_all x1, starting transfers between devices: 3.71 us -> 5 us  [local(): lax.all_to_all(send_second.reshape(group, capacity, width), near, split_a...]
where the time goes in v16:
time: 106 us
  waiting for transfers between devices  49.3 us (47%)
  blocking collectives  30.2 us (28%)
  starting transfers between devices  14 us (13%)
  matrix products  8.79 us (8%)
  other arithmetic  1.66 us (2%)
  local copies, waits for them, and re-layouts  1.08 us (1%)
    all_to_all x1, waiting for transfers between devices, local(): lax.all_to_all(send_second.reshape(group, capacity, width), near, split_a...  22.5 us
    all_to_all x1, waiting for transfers between devices, local(): lax.all_to_all(send_first.reshape(group, capacity, wide), near, split_axi...  21.3 us
    all_to_all x1, blocking collectives, local(): lax.all_to_all(partial_sums.reshape(group, share, width), near, split_axi...  19 us
    all_to_all x1, blocking collectives, local(): lax.all_to_all(jnp.broadcast_to(own[None], (group, share, width)), near,...  11.2 us
    all_to_all x1, starting transfers between devices, local(): lax.all_to_all(send_first.reshape(group, capacity, wide), near, split_axi...  6.32 us
    ppermute x1, waiting for transfers between devices, local(): sums = half_sums + lax.ppermute(half_sums, 'zh', [(0, 1), (1, 0)])  5.5 us
    all_to_all x1, starting transfers between devices, local(): lax.all_to_all(send_second.reshape(group, capacity, width), near, split_a...  5 us
    ppermute x1, starting transfers between devices, local(): mirrored = lax.ppermute(mirror_part, 'zh', [(0, 1), (1, 0)])  2.59 us
  transfers between devices with their start and end apart: 4, of which 3 were waited for; matrix products, arithmetic and copies ran while one was open for 3% of the time, Pallas kernels for 0%

profile of v16, /device:TPU:0, one launch (start us, length us, event | category | flops | bytes accessed | tf_op | source)
XLA Modules:
  0.0 105.8 jit_solution(11519204087108404465)
XLA Ops:
  0.6 0.0 copy-start.1
  0.7 1.2 %fusion.5 = f32[1024]{0:T(1024)S(1)} fusion(s32[1024]{0:T(1024)} %bitcast.19, s32[32]{0:T(128)S(1)} %fusion.23), kind=kOutput, calls=%fused_computation.10 | convolution fusion | flops 68353024 | bytes 8320 | tf_op jit(solution)/shard_map/dot_general | solution.py:40
  1.9 0.7 add_convert_fusion.1
  2.7 0.9 convolution_convert_fusion.1
  3.6 0.1 slice_add_fusion
  3.7 0.1 slice.43
  3.7 0.1 slice.46
  3.8 0.1 slice.48
  3.9 0.0 copy-done.1
  3.9 2.2 %add_convert_fusion = bf16[1024,896]{1,0:T(8,128)(2,1)} fusion(f32[1024]{0:T(1024)S(1)} %slice.48, f32[1024]{0:T(1024)S(1)} %slice.46, pred[896]{0:T(1024)(128)(4,1)S(1)} %get-tuple-element.19, pred[896]{0:T(1024)(128)(4,1)S(1)} %get-tuple-element.20, s32[1024]{0:T(1024)S(1)} %slice.43, bf16[128,768]{1,0:T(8,128)(2,1)S(1)} %copy-done.1), kind=kOutput, calls=%fused_computation.2 | convolution fusion | flops 238682112 | bytes 2045696 | tf_op jit(solution)/shard_map/dot_general | solution.py:67
  6.0 6.3 %all-to-all-start = ((bf16[16,64,896]{2,1,0:T(8,128)(2,1)}), bf16[16,64,896]{2,1,0:T(8,128)(2,1)S(1)}, u32[]{:S(2)}, u32[]{:S(2)}) async-start(bf16[16,64,896]{2,1,0:T(8,128)(2,1)} %bitcast.18), calls=%async_computation | async-start | bytes 3670016 | tf_op jit(solution)/shard_map/all_to_all | solution.py:71
  12.4 0.1 slice.51
  12.4 1.8 %convolution_convert_fusion = bf16[1024,768]{1,0:T(8,128)(2,1)} fusion(bf16[128,768]{1,0:T(8,128)(2,1)S(1)} %copy-done.1, s32[1024]{0:T(1024)S(1)} %slice.51), kind=kOutput, calls=%fused_computation.3 | convolution fusion | flops 202244096 | bytes 1773568 | tf_op jit(solution)/shard_map/dot_general | solution.py:69
  14.2 21.3 %all-to-all-done = bf16[16,64,896]{2,1,0:T(8,128)(2,1)S(1)} async-done(((bf16[16,64,896]{2,1,0:T(8,128)(2,1)}), bf16[16,64,896]{2,1,0:T(8,128)(2,1)S(1)}, u32[]{:S(2)}, u32[]{:S(2)}) %all-to-all-start) | async-done | bytes 1835040 | tf_op jit(solution)/shard_map/all_to_all | solution.py:71
  35.6 5.0 %all-to-all-start.1 = ((bf16[16,64,768]{2,1,0:T(8,128)(2,1)}), bf16[16,64,768]{2,1,0:T(8,128)(2,1)S(1)}, u32[]{:S(2)}, u32[]{:S(2)}) async-start(bf16[16,64,768]{2,1,0:T(8,128)(2,1)} %bitcast.3), calls=%async_computation.1 | async-start | bytes 3145728 | tf_op jit(solution)/shard_map/all_to_all | solution.py:74
  40.6 0.4 add_reduce_fusion.1
  41.0 0.0 copy-start.2
  41.0 1.1 %fusion.1 = f32[96,768]{1,0:T(8,128)} fusion(bf16[1024,896]{1,0:T(8,128)(2,1)S(1)} %bitcast.17, s32[1024]{0:T(1024)S(1)} %get-tuple-element.4), kind=kOutput, calls=%fused_computation.4 | convolution fusion | flops 151093248 | bytes 1871872 | tf_op jit(solution)/shard_map/dot_general | solution.py:82
  42.1 2.6 %collective-permute-start = (f32[96,768]{1,0:T(8,128)}, f32[96,768]{1,0:T(8,128)S(1)}, u32[]{:S(2)}, u32[]{:S(2)}) collective-permute-start(f32[96,768]{1,0:T(8,128)} %fusion.1), channel_id=1, source_target_pairs={{0,4},{4,0},{1,5},{5,1},{2,6},{6,2},{3,7},{7,3},{8,12},{12,8},{9,1... | collective-permute-start | bytes 884744 | tf_op jit(solution)/shard_map/ppermute | solution.py:83
  44.7 22.5 %all-to-all-done.1 = bf16[16,64,768]{2,1,0:T(8,128)(2,1)S(1)} async-done(((bf16[16,64,768]{2,1,0:T(8,128)(2,1)}), bf16[16,64,768]{2,1,0:T(8,128)(2,1)S(1)}, u32[]{:S(2)}, u32[]{:S(2)}) %all-to-all-start.1) | async-done | bytes 1572896 | tf_op jit(solution)/shard_map/all_to_all | solution.py:74
  67.2 0.0 collective-permute-done
  67.2 0.5 multiply_reduce_fusion
  67.7 0.1 multiply_convert_fusion
  67.8 0.0 copy-done.2
  67.8 0.0 copy-start
  67.8 0.2 fusion.16
  68.0 19.0 %all_to_all.20 = f32[16,16,768]{2,1,0:T(8,128)S(1)} all-to-all(f32[16,16,768]{2,1,0:T(8,128)S(1)} %bitcast.15), channel_id=1, replica_groups=mesh['y'=2,'core'=2,'zh'=2,'zr'=4] {'core','y','zr'}, dimensions={0} | all-to-all | bytes 1572864 | tf_op jit(solution)/shard_map/all_to_all | solution.py:93
  87.1 0.1 collective-permute-start.1
  87.2 5.5 %collective-permute-done.1 = f32[16,768]{1,0:T(8,128)S(1)} collective-permute-done((f32[16,768]{1,0:T(8,128)S(1)}, f32[16,768]{1,0:T(8,128)S(1)}, u32[]{:S(2)}, u32[]{:S(2)}) %collective-permute-start.1) | collective-permute-done | bytes 49184 | tf_op jit(solution)/shard_map/ppermute | solution.py:97
  92.7 0.1 multiply_reduce_fusion.1
  92.8 0.1 multiply_convert_fusion.1
  92.9 11.2 %all_to_all.21 = bf16[16,16,768]{2,1,0:T(8,128)(2,1)S(1)} all-to-all(bf16[16,16,768]{2,1,0:T(8,128)(2,1)S(1)} %broadcast_in_dim.76), channel_id=1, replica_groups=mesh['y'=2,'core'=2,'zh'=2,'zr'=4] {'core','y','zr'}, dimensions={0} | all-to-all | bytes 786432 | tf_op jit(solution)/shard_map/all_to_all | solution.py:99
  104.1 0.0 copy-done
  104.1 0.9 fusion.4
  105.0 0.7 copy.10
  (10 shorter events, 0.2 us)
Async XLA Ops:
  0.6 3.2 %copy-start.1 = (bf16[128,768]{1,0:T(8,128)(2,1)S(1)}, bf16[128,768]{1,0:T(8,128)(2,1)}, u32[]{:S(2)}) copy-start(bf16[128,768]{1,0:T(8,128)(2,1)} %param.5) | copy-start | bytes 589828
  6.0 29.5 %all-to-all-start = ((bf16[16,64,896]{2,1,0:T(8,128)(2,1)}), bf16[16,64,896]{2,1,0:T(8,128)(2,1)S(1)}, u32[]{:S(2)}, u32[]{:S(2)}) async-start(bf16[16,64,896]{2,1,0:T(8,128)(2,1)} %bitcast.18), calls=%async_computation | async-start | bytes 3670016 | tf_op jit(solution)/shard_map/all_to_all | solution.py:71
  35.6 31.6 %all-to-all-start.1 = ((bf16[16,64,768]{2,1,0:T(8,128)(2,1)}), bf16[16,64,768]{2,1,0:T(8,128)(2,1)S(1)}, u32[]{:S(2)}, u32[]{:S(2)}) async-start(bf16[16,64,768]{2,1,0:T(8,128)(2,1)} %bitcast.3), calls=%async_computation.1 | async-start | bytes 3145728 | tf_op jit(solution)/shard_map/all_to_all | solution.py:74
  41.0 26.8 %copy-start.2 = (s32[96]{0:T(128)S(1)}, s32[96]{0:T(128)}, u32[]{:S(2)}) copy-start(s32[96]{0:T(128)} %param.9) | copy-start | bytes 1156
  42.1 25.0 %collective-permute-start = (f32[96,768]{1,0:T(8,128)}, f32[96,768]{1,0:T(8,128)S(1)}, u32[]{:S(2)}, u32[]{:S(2)}) collective-permute-start(f32[96,768]{1,0:T(8,128)} %fusion.1), channel_id=1, source_target_pairs={{0,4},{4,0},{1,5},{5,1},{2,6},{6,2},{3,7},{7,3},{8,12},{12,8},{9,1... | collective-permute-start | bytes 884744 | tf_op jit(solution)/shard_map/ppermute | solution.py:83
  67.8 36.3 %copy-start = (bf16[96,768]{1,0:T(8,128)(2,1)}, bf16[96,768]{1,0:T(8,128)(2,1)S(1)}, u32[]{:S(2)}) copy-start(bf16[96,768]{1,0:T(8,128)(2,1)S(1)} %multiply_convert_fusion) | copy-start | bytes 442372
  87.1 5.6 %collective-permute-start.1 = (f32[16,768]{1,0:T(8,128)S(1)}, f32[16,768]{1,0:T(8,128)S(1)}, u32[]{:S(2)}, u32[]{:S(2)}) collective-permute-start(f32[16,768]{1,0:T(8,128)S(1)} %reduce_sum.38), channel_id=1, source_target_pairs={{0,4},{4,0},{1,5},{5,1},{2,6},{6,2},{3,7},{7,3},{8,12},{12,8},{9,1... | collective-permute-start | bytes 147464 | tf_op jit(solution)/shard_map/ppermute | solution.py:97

commit v17 on v16

--- a/solution.py
+++ b/solution.py
@@ -11,10 +11,10 @@
 
 
 def local(doc_embed, pair_doc, pair_owner, pair_slot, label_cluster):
-    axes = ("y", "core", "zh", "zr")
-    near = ("core", "y", "zr")
+    axes = ("y", "core", "zh", "zl", "x")
+    near = ("y", "core", "x", "zl")
     devices = lax.axis_size(axes)
-    halves = lax.axis_size("zr")
+    halves = lax.axis_size(("zl", "x"))
     group = devices // 2
     pairs = pair_doc.shape[0]
     docs, width = doc_embed.shape
@@ -31,7 +31,8 @@
         size = lax.axis_size(name)
         place[name], b_proxy = b_proxy % size, b_proxy // size
     b_row = place["y"] * 2 + place["core"]
-    block_owner = b_row * (2 * halves) + b_zh * halves + place["zr"]
+    b_zr = place["zl"] * lax.axis_size("x") + place["x"]
+    block_owner = b_row * (2 * halves) + b_zh * halves + b_zr
 
     owner_row = pair_owner.reshape(1, pairs)
     hits_t = (block_owner[:, None] == owner_row).astype(bf16)
@@ -114,8 +115,8 @@
 
 def solution(mesh):
     rows, cols = mesh.shape["row"], mesh.shape["col"]
-    split = Mesh(mesh.devices.reshape(rows // 2, 2, 2, cols // 2), ("y", "core", "zh", "zr"))
-    spread = ("y", "core", "zh", "zr")
+    spread = ("y", "core", "zh", "zl", "x")
+    split = Mesh(mesh.devices.reshape(rows // 2, 2, 2, 2, cols // 4), spread)
     placed = (P(spread, None), P(spread), P(spread, None), P(spread), P(spread))
     return jax.shard_map(
         local,

time: 106 us -> 104 us (0.981)
  blocking collectives: 30.2 us -> 28.1 us
    all_to_all x1, blocking collectives: 19 us -> 17.6 us  [local(): lax.all_to_all(partial_sums.reshape(group, share, width), near, split_axi...]
    all_to_all x1, starting transfers between devices: 5 us -> 3.71 us  [local(): lax.all_to_all(send_second.reshape(group, capacity, width), near, split_a...]
where the time goes in v17:
time: 104 us
  waiting for transfers between devices  50.3 us (48%)
  blocking collectives  28.1 us (27%)
  starting transfers between devices  13 us (12%)
  matrix products  8.79 us (8%)
  other arithmetic  1.67 us (2%)
  local copies, waits for them, and re-layouts  1.08 us (1%)
    all_to_all x1, waiting for transfers between devices, local(): lax.all_to_all(send_second.reshape(group, capacity, width), near, split_a...  22.5 us
    all_to_all x1, waiting for transfers between devices, local(): lax.all_to_all(send_first.reshape(group, capacity, wide), near, split_axi...  22.2 us
    all_to_all x1, blocking collectives, local(): lax.all_to_all(partial_sums.reshape(group, share, width), near, split_axi...  17.6 us
    all_to_all x1, blocking collectives, local(): lax.all_to_all(jnp.broadcast_to(own[None], (group, share, width)), near,...  10.5 us
    all_to_all x1, starting transfers between devices, local(): lax.all_to_all(send_first.reshape(group, capacity, wide), near, split_axi...  6.31 us
    ppermute x1, waiting for transfers between devices, local(): sums = half_sums + lax.ppermute(half_sums, 'zh', [(0, 1), (1, 0)])  5.6 us
    all_to_all x1, starting transfers between devices, local(): lax.all_to_all(send_second.reshape(group, capacity, width), near, split_a...  3.71 us
    ppermute x1, starting transfers between devices, local(): mirrored = lax.ppermute(mirror_part, 'zh', [(0, 1), (1, 0)])  2.59 us
  transfers between devices with their start and end apart: 4, of which 3 were waited for; matrix products, arithmetic and copies ran while one was open for 3% of the time, Pallas kernels for 0%

profile of v17, /device:TPU:0, one launch (start us, length us, event | category | flops | bytes accessed | tf_op | source)
XLA Modules:
  0.0 103.8 jit_solution(4992378866410443331)
XLA Ops:
  0.6 0.0 copy-start.1
  0.7 1.2 %fusion.5 = f32[1024]{0:T(1024)S(1)} fusion(s32[1024]{0:T(1024)} %bitcast.19, s32[32]{0:T(128)S(1)} %fusion.24), kind=kOutput, calls=%fused_computation.10 | convolution fusion | flops 68353024 | bytes 8320 | tf_op jit(solution)/shard_map/dot_general | solution.py:41
  1.9 0.7 add_convert_fusion.1
  2.7 0.9 convolution_convert_fusion.1
  3.6 0.1 slice_add_fusion
  3.7 0.1 slice.43
  3.7 0.1 slice.46
  3.8 0.1 slice.48
  3.9 0.0 copy-done.1
  3.9 2.2 %add_convert_fusion = bf16[1024,896]{1,0:T(8,128)(2,1)} fusion(f32[1024]{0:T(1024)S(1)} %slice.48, f32[1024]{0:T(1024)S(1)} %slice.46, pred[896]{0:T(1024)(128)(4,1)S(1)} %get-tuple-element.19, pred[896]{0:T(1024)(128)(4,1)S(1)} %get-tuple-element.20, s32[1024]{0:T(1024)S(1)} %slice.43, bf16[128,768]{1,0:T(8,128)(2,1)S(1)} %copy-done.1), kind=kOutput, calls=%fused_computation.2 | convolution fusion | flops 238682112 | bytes 2045696 | tf_op jit(solution)/shard_map/dot_general | solution.py:68
  6.1 6.3 %all-to-all-start = ((bf16[16,64,896]{2,1,0:T(8,128)(2,1)}), bf16[16,64,896]{2,1,0:T(8,128)(2,1)S(1)}, u32[]{:S(2)}, u32[]{:S(2)}) async-start(bf16[16,64,896]{2,1,0:T(8,128)(2,1)} %bitcast.18), calls=%async_computation | async-start | bytes 3670016 | tf_op jit(solution)/shard_map/all_to_all | solution.py:72
  12.4 0.1 slice.51
  12.4 1.8 %convolution_convert_fusion = bf16[1024,768]{1,0:T(8,128)(2,1)} fusion(bf16[128,768]{1,0:T(8,128)(2,1)S(1)} %copy-done.1, s32[1024]{0:T(1024)S(1)} %slice.51), kind=kOutput, calls=%fused_computation.3 | convolution fusion | flops 202244096 | bytes 1773568 | tf_op jit(solution)/shard_map/dot_general | solution.py:70
  14.2 22.2 %all-to-all-done = bf16[16,64,896]{2,1,0:T(8,128)(2,1)S(1)} async-done(((bf16[16,64,896]{2,1,0:T(8,128)(2,1)}), bf16[16,64,896]{2,1,0:T(8,128)(2,1)S(1)}, u32[]{:S(2)}, u32[]{:S(2)}) %all-to-all-start) | async-done | bytes 1835040 | tf_op jit(solution)/shard_map/all_to_all | solution.py:72
  36.4 3.7 %all-to-all-start.1 = ((bf16[16,64,768]{2,1,0:T(8,128)(2,1)}), bf16[16,64,768]{2,1,0:T(8,128)(2,1)S(1)}, u32[]{:S(2)}, u32[]{:S(2)}) async-start(bf16[16,64,768]{2,1,0:T(8,128)(2,1)} %bitcast.3), calls=%async_computation.1 | async-start | bytes 3145728 | tf_op jit(solution)/shard_map/all_to_all | solution.py:75
  40.1 0.4 add_reduce_fusion.1
  40.6 0.0 copy-start.2
  40.6 1.1 %fusion.1 = f32[96,768]{1,0:T(8,128)} fusion(bf16[1024,896]{1,0:T(8,128)(2,1)S(1)} %bitcast.17, s32[1024]{0:T(1024)S(1)} %get-tuple-element.4), kind=kOutput, calls=%fused_computation.4 | convolution fusion | flops 151093248 | bytes 1871872 | tf_op jit(solution)/shard_map/dot_general | solution.py:83
  41.7 2.6 %collective-permute-start = (f32[96,768]{1,0:T(8,128)}, f32[96,768]{1,0:T(8,128)S(1)}, u32[]{:S(2)}, u32[]{:S(2)}) collective-permute-start(f32[96,768]{1,0:T(8,128)} %fusion.1), channel_id=1, source_target_pairs={{0,4},{4,0},{1,5},{5,1},{2,6},{6,2},{3,7},{7,3},{8,12},{12,8},{9,1... | collective-permute-start | bytes 884744 | tf_op jit(solution)/shard_map/ppermute | solution.py:84
  44.3 22.5 %all-to-all-done.1 = bf16[16,64,768]{2,1,0:T(8,128)(2,1)S(1)} async-done(((bf16[16,64,768]{2,1,0:T(8,128)(2,1)}), bf16[16,64,768]{2,1,0:T(8,128)(2,1)S(1)}, u32[]{:S(2)}, u32[]{:S(2)}) %all-to-all-start.1) | async-done | bytes 1572896 | tf_op jit(solution)/shard_map/all_to_all | solution.py:75
  66.8 0.0 collective-permute-done
  66.8 0.5 multiply_reduce_fusion
  67.3 0.1 multiply_convert_fusion
  67.4 0.0 copy-done.2
  67.4 0.0 copy-start
  67.4 0.2 fusion.16
  67.7 17.6 %all_to_all.20 = f32[16,16,768]{2,1,0:T(8,128)S(1)} all-to-all(f32[16,16,768]{2,1,0:T(8,128)S(1)} %bitcast.15), channel_id=1, replica_groups=mesh['y'=2,'core'=2,'zh'=2,'zl'=2,'x'=2] {'y','core','x','zl'}, dimensions={0} | all-to-all | bytes 1572864 | tf_op jit(solution)/shard_map/all_to_all | solution.py:94
  85.3 0.4 collective-permute-start.1
  85.7 5.6 %collective-permute-done.1 = f32[16,768]{1,0:T(8,128)S(1)} collective-permute-done((f32[16,768]{1,0:T(8,128)S(1)}, f32[16,768]{1,0:T(8,128)S(1)}, u32[]{:S(2)}, u32[]{:S(2)}) %collective-permute-start.1) | collective-permute-done | bytes 49184 | tf_op jit(solution)/shard_map/ppermute | solution.py:98
  91.3 0.1 multiply_reduce_fusion.1
  91.5 0.1 multiply_convert_fusion.1
  91.6 10.5 %all_to_all.21 = bf16[16,16,768]{2,1,0:T(8,128)(2,1)S(1)} all-to-all(bf16[16,16,768]{2,1,0:T(8,128)(2,1)S(1)} %broadcast_in_dim.76), channel_id=1, replica_groups=mesh['y'=2,'core'=2,'zh'=2,'zl'=2,'x'=2] {'y','core','x','zl'}, dimensions={0} | all-to-all | bytes 786432 | tf_op jit(solution)/shard_map/all_to_all | solution.py:100
  102.1 0.0 copy-done
  102.1 0.9 fusion.4
  103.0 0.7 copy.10
  (10 shorter events, 0.2 us)
Async XLA Ops:
  0.6 3.3 %copy-start.1 = (bf16[128,768]{1,0:T(8,128)(2,1)S(1)}, bf16[128,768]{1,0:T(8,128)(2,1)}, u32[]{:S(2)}) copy-start(bf16[128,768]{1,0:T(8,128)(2,1)} %param.5) | copy-start | bytes 589828
  6.1 30.3 %all-to-all-start = ((bf16[16,64,896]{2,1,0:T(8,128)(2,1)}), bf16[16,64,896]{2,1,0:T(8,128)(2,1)S(1)}, u32[]{:S(2)}, u32[]{:S(2)}) async-start(bf16[16,64,896]{2,1,0:T(8,128)(2,1)} %bitcast.18), calls=%async_computation | async-start | bytes 3670016 | tf_op jit(solution)/shard_map/all_to_all | solution.py:72
  36.4 30.4 %all-to-all-start.1 = ((bf16[16,64,768]{2,1,0:T(8,128)(2,1)}), bf16[16,64,768]{2,1,0:T(8,128)(2,1)S(1)}, u32[]{:S(2)}, u32[]{:S(2)}) async-start(bf16[16,64,768]{2,1,0:T(8,128)(2,1)} %bitcast.3), calls=%async_computation.1 | async-start | bytes 3145728 | tf_op jit(solution)/shard_map/all_to_all | solution.py:75
  40.6 26.8 %copy-start.2 = (s32[96]{0:T(128)S(1)}, s32[96]{0:T(128)}, u32[]{:S(2)}) copy-start(s32[96]{0:T(128)} %param.9) | copy-start | bytes 1156
  41.7 25.1 %collective-permute-start = (f32[96,768]{1,0:T(8,128)}, f32[96,768]{1,0:T(8,128)S(1)}, u32[]{:S(2)}, u32[]{:S(2)}) collective-permute-start(f32[96,768]{1,0:T(8,128)} %fusion.1), channel_id=1, source_target_pairs={{0,4},{4,0},{1,5},{5,1},{2,6},{6,2},{3,7},{7,3},{8,12},{12,8},{9,1... | collective-permute-start | bytes 884744 | tf_op jit(solution)/shard_map/ppermute | solution.py:84
  67.4 34.7 %copy-start = (bf16[96,768]{1,0:T(8,128)(2,1)}, bf16[96,768]{1,0:T(8,128)(2,1)S(1)}, u32[]{:S(2)}) copy-start(bf16[96,768]{1,0:T(8,128)(2,1)S(1)} %multiply_convert_fusion) | copy-start | bytes 442372
  85.3 6.0 %collective-permute-start.1 = (f32[16,768]{1,0:T(8,128)S(1)}, f32[16,768]{1,0:T(8,128)S(1)}, u32[]{:S(2)}, u32[]{:S(2)}) collective-permute-start(f32[16,768]{1,0:T(8,128)S(1)} %reduce_sum.38), channel_id=1, source_target_pairs={{0,4},{4,0},{1,5},{5,1},{2,6},{6,2},{3,7},{7,3},{8,12},{12,8},{9,1... | collective-permute-start | bytes 147464 | tf_op jit(solution)/shard_map/ppermute | solution.py:98

commit v18 on v17

--- a/solution.py
+++ b/solution.py
@@ -58,16 +58,18 @@
 
     lanes = 128
     wide = width + lanes
-    doc_part = (first_doc[:, None] == jnp.arange(docs, dtype=jnp.int32)[None, :]).astype(bf16)
-    table = jnp.concatenate([doc_embed, jnp.zeros((docs, lanes), bf16)], axis=1)
+    table = jnp.concatenate([doc_embed, jnp.zeros((1, width), bf16)], axis=0)
+    table_wide = jnp.concatenate([table, jnp.zeros((docs + 1, lanes), bf16)], axis=1)
+    first_at = jnp.where(first_doc >= 0, first_doc, docs)
+    second_at = jnp.where(second_doc >= 0, second_doc, docs)
     lane = jnp.arange(wide, dtype=jnp.int32)[None, :]
-    slot_pair = slot_plus.astype(f32).reshape(2, group * capacity)
+    slot_pair = slot_plus.astype(bf16).reshape(2, group * capacity)
+    zero = jnp.zeros((), bf16)
     slot_lanes = jnp.where(
-        lane == width, slot_pair[0][:, None], jnp.where(lane == width + 1, slot_pair[1][:, None], 0.0)
+        lane == width, slot_pair[0][:, None], jnp.where(lane == width + 1, slot_pair[1][:, None], zero)
     )
-    send_first = (jnp.dot(doc_part, table, preferred_element_type=f32) + slot_lanes).astype(bf16)
-    pick = (second_doc[:, None] == jnp.arange(docs, dtype=jnp.int32)[None, :]).astype(bf16)
-    send_second = jnp.dot(pick, doc_embed, preferred_element_type=f32).astype(bf16)
+    send_first = jnp.take(table_wide, first_at, axis=0) + slot_lanes
+    send_second = jnp.take(table, second_at, axis=0)
 
     got_first = lax.all_to_all(
         send_first.reshape(group, capacity, wide), near, split_axis=0, concat_axis=0, tiled=True

time: 104 us -> 108 us (1.038)
  local copies, waits for them, and re-layouts: 1.08 us -> 9.2 us
  waiting for transfers between devices: 50.3 us -> 44.9 us
  other arithmetic: 1.67 us -> 6.05 us
  matrix products: 8.79 us -> 5.53 us
    gather x0 -> x2, local copies, waits for them, and re-layouts: none -> 8 us  [the longest x1 4 us: local(): send_first = jnp.take(table_wide, first_at, axis=0) + slot_lanes]
    dot_general x2 -> x0, matrix products: 3.95 us -> none  [the longest x1 2.17 us: local(): jnp.dot(doc_part, table, preferred_element_type=f32) + slot_lanes]
    all_to_all x1, waiting for transfers between devices: 22.2 us -> 18.6 us  [local(): lax.all_to_all(send_first.reshape(group, capacity, wide), near, split_axi...]
    add x0 -> x1, other arithmetic: none -> 1.98 us  [local(): send_first = jnp.take(table_wide, first_at, axis=0) + slot_lanes]
    all_to_all x1, waiting for transfers between devices: 22.5 us -> 20.7 us  [local(): lax.all_to_all(send_second.reshape(group, capacity, width), near, split_a...]
    select_n x0 -> x1, other arithmetic: none -> 1.39 us  [local(): send_second = jnp.take(table, second_at, axis=0)]
  transfers between devices with their start and end apart: 4 -> 4, of which waited for: 3 -> 3; matrix products, arithmetic and copies ran while one was open for 3% -> 8% of each run, Pallas kernels for 0% -> 0%
where the time goes in v18:
time: 108 us
  waiting for transfers between devices  44.9 us (42%)
  blocking collectives  28.1 us (26%)
  starting transfers between devices  13.2 us (12%)
  local copies, waits for them, and re-layouts  9.2 us (9%)
  other arithmetic  6.05 us (6%)
  matrix products  5.53 us (5%)
    all_to_all x1, waiting for transfers between devices, local(): lax.all_to_all(send_second.reshape(group, capacity, width), near, split_a...  20.7 us
    all_to_all x1, waiting for transfers between devices, local(): lax.all_to_all(send_first.reshape(group, capacity, wide), near, split_axi...  18.6 us
    all_to_all x1, blocking collectives, local(): lax.all_to_all(partial_sums.reshape(group, share, width), near, split_axi...  17.6 us
    all_to_all x1, blocking collectives, local(): lax.all_to_all(jnp.broadcast_to(own[None], (group, share, width)), near,...  10.5 us
    all_to_all x1, starting transfers between devices, local(): lax.all_to_all(send_first.reshape(group, capacity, wide), near, split_axi...  6.36 us
    ppermute x1, waiting for transfers between devices, local(): sums = half_sums + lax.ppermute(half_sums, 'zh', [(0, 1), (1, 0)])  5.59 us
    gather x1, local copies, waits for them, and re-layouts, local(): send_first = jnp.take(table_wide, first_at, axis=0) + slot_lanes  4 us
    gather x1, local copies, waits for them, and re-layouts, local(): send_second = jnp.take(table, second_at, axis=0)  4 us
  transfers between devices with their start and end apart: 4, of which 3 were waited for; matrix products, arithmetic and copies ran while one was open for 8% of the time, Pallas kernels for 0%

profile of v18, /device:TPU:0, one launch (start us, length us, event | category | flops | bytes accessed | tf_op | source)
XLA Modules:
  0.0 107.8 jit_solution(11485100979405852899)
XLA Ops:
  0.6 0.0 copy-start.1
  0.7 1.2 %fusion.5 = f32[1024]{0:T(1024)S(1)} fusion(s32[1024]{0:T(1024)} %bitcast.16, s32[32]{0:T(128)S(1)} %fusion.23), kind=kOutput, calls=%fused_computation.12 | convolution fusion | flops 68353024 | bytes 8320 | tf_op jit(solution)/shard_map/dot_general | solution.py:41
  1.9 0.7 add_convert_fusion
  2.7 0.9 fusion.32
  3.6 0.1 slice.47
  3.7 0.1 fusion.31
  3.8 0.1 slice.49
  3.9 0.1 slice.51
  3.9 0.0 copy-done.1
  4.0 4.0 %gather_fusion = bf16[1024,768]{1,0:T(8,128)(2,1)S(1)} fusion(bf16[129,768]{1,0:T(8,128)(2,1)S(1)} %concatenate.9, s32[1024]{0:T(1024)S(1)} %fusion.20), kind=kCustom, calls=%fused_computation | custom fusion | bytes 3149824 | tf_op jit(solution)/shard_map/jit(_take)/gather | solution.py:71
  8.0 2.0 %select_add_fusion = bf16[1024,896]{1,0:T(8,128)(2,1)} fusion(bf16[1024,768]{1,0:T(8,128)(2,1)S(1)} %gather_fusion, pred[1024]{0:T(1024)(128)(4,1)S(1)} %compare_and_fusion.1, pred[896]{0:T(1024)(128)(4,1)S(1)} %get-tuple-element.19, pred[896]{0:T(1024)(128)(4,1)S(1)} %get-tuple-element.20, bf16[1024]{0:T(1024)(128)(2,1)S(1)} %slice.51, ...), kind=kLoop, calls=%fused_computation.4 | loop fusion | flops 6422528 | bytes 3414784 | tf_op jit(solution)/shard_map/add | solution.py:71
  10.0 6.4 %all-to-all-start = ((bf16[16,64,896]{2,1,0:T(8,128)(2,1)}), bf16[16,64,896]{2,1,0:T(8,128)(2,1)}, u32[]{:S(2)}, u32[]{:S(2)}) async-start(bf16[16,64,896]{2,1,0:T(8,128)(2,1)} %bitcast.1), calls=%async_computation | async-start | bytes 3670016 | tf_op jit(solution)/shard_map/all_to_all | solution.py:74
  16.3 0.1 slice.54
  16.4 4.0 %gather_fusion.1 = bf16[1024,768]{1,0:T(8,128)(2,1)S(1)} fusion(bf16[129,768]{1,0:T(8,128)(2,1)S(1)} %concatenate.9, s32[1024]{0:T(1024)S(1)} %fusion.19), kind=kCustom, calls=%fused_computation.1 | custom fusion | bytes 3149824 | tf_op jit(solution)/shard_map/jit(_take)/gather | solution.py:72
  20.4 1.4 %broadcast_select_fusion = bf16[16,64,768]{2,1,0:T(8,128)(2,1)} fusion(bf16[16,64,768]{2,1,0:T(8,128)(2,1)S(1)} %bitcast.12, pred[16,64]{1,0:T(8,128)(4,1)S(1)} %compare_and_fusion), kind=kLoop, calls=%fused_computation.7 | loop fusion | flops 786432 | bytes 3146752 | tf_op jit(solution)/shard_map/jit(_take)/select_n | solution.py:72
  21.8 18.6 %all-to-all-done = bf16[16,64,896]{2,1,0:T(8,128)(2,1)} async-done(((bf16[16,64,896]{2,1,0:T(8,128)(2,1)}), bf16[16,64,896]{2,1,0:T(8,128)(2,1)}, u32[]{:S(2)}, u32[]{:S(2)}) %all-to-all-start) | async-done | bytes 1835040 | tf_op jit(solution)/shard_map/all_to_all | solution.py:74
  40.4 3.7 %all-to-all-start.1 = ((bf16[16,64,768]{2,1,0:T(8,128)(2,1)}), bf16[16,64,768]{2,1,0:T(8,128)(2,1)S(1)}, u32[]{:S(2)}, u32[]{:S(2)}) async-start(bf16[16,64,768]{2,1,0:T(8,128)(2,1)} %broadcast_select_fusion), calls=%async_computation.1 | async-start | bytes 3145728 | tf_op jit(solution)/shard_map/all_to_all | solution.py:77
  44.1 1.5 %add_reduce_fusion.1 = (s32[1024]{0:T(1024)S(1)}, s32[1024]{0:T(1024)S(1)}) fusion(bf16[1024,896]{1,0:T(8,128)(2,1)} %bitcast.2), kind=kLoop, calls=%fused_computation.15 | loop fusion | flops 4096 | bytes 12288 | tf_op jit(solution)/shard_map/sub | solution.py:81
  45.6 0.0 copy-start.2
  45.6 1.8 %fusion.1 = f32[96,768]{1,0:T(8,128)S(1)} fusion(bf16[1024,896]{1,0:T(8,128)(2,1)} %bitcast.2, s32[1024]{0:T(1024)S(1)} %get-tuple-element.4), kind=kOutput, calls=%fused_computation.5 | convolution fusion | flops 151093248 | bytes 1871872 | tf_op jit(solution)/shard_map/dot_general | solution.py:85
  47.4 2.7 %collective-permute-start = (f32[96,768]{1,0:T(8,128)S(1)}, f32[96,768]{1,0:T(8,128)S(1)}, u32[]{:S(2)}, u32[]{:S(2)}) collective-permute-start(f32[96,768]{1,0:T(8,128)S(1)} %fusion.1), channel_id=1, source_target_pairs={{0,4},{4,0},{1,5},{5,1},{2,6},{6,2},{3,7},{7,3},{8,12},{12,8},{9,1... | collective-permute-start | bytes 884744 | tf_op jit(solution)/shard_map/ppermute | solution.py:86
  50.1 20.7 %all-to-all-done.1 = bf16[16,64,768]{2,1,0:T(8,128)(2,1)S(1)} async-done(((bf16[16,64,768]{2,1,0:T(8,128)(2,1)}), bf16[16,64,768]{2,1,0:T(8,128)(2,1)S(1)}, u32[]{:S(2)}, u32[]{:S(2)}) %all-to-all-start.1) | async-done | bytes 1572896 | tf_op jit(solution)/shard_map/all_to_all | solution.py:77
  70.8 0.0 collective-permute-done
  70.8 0.5 multiply_reduce_fusion
  71.3 0.1 multiply_convert_fusion
  71.4 0.0 copy-done.2
  71.4 0.0 copy-start
  71.4 0.2 fusion.13
  71.7 17.6 %all_to_all.20 = f32[16,16,768]{2,1,0:T(8,128)S(1)} all-to-all(f32[16,16,768]{2,1,0:T(8,128)S(1)} %bitcast.15), channel_id=1, replica_groups=mesh['y'=2,'core'=2,'zh'=2,'zl'=2,'x'=2] {'y','core','x','zl'}, dimensions={0} | all-to-all | bytes 1572864 | tf_op jit(solution)/shard_map/all_to_all | solution.py:96
  89.3 0.4 collective-permute-start.1
  89.8 5.6 %collective-permute-done.1 = f32[16,768]{1,0:T(8,128)S(1)} collective-permute-done((f32[16,768]{1,0:T(8,128)S(1)}, f32[16,768]{1,0:T(8,128)S(1)}, u32[]{:S(2)}, u32[]{:S(2)}) %collective-permute-start.1) | collective-permute-done | bytes 49184 | tf_op jit(solution)/shard_map/ppermute | solution.py:100
  95.4 0.1 multiply_reduce_fusion.1
  95.5 0.1 multiply_convert_fusion.1
  95.6 10.5 %all_to_all.21 = bf16[16,16,768]{2,1,0:T(8,128)(2,1)S(1)} all-to-all(bf16[16,16,768]{2,1,0:T(8,128)(2,1)S(1)} %broadcast_in_dim.112), channel_id=1, replica_groups=mesh['y'=2,'core'=2,'zh'=2,'zl'=2,'x'=2] {'y','core','x','zl'}, dimensions={0} | all-to-all | bytes 786432 | tf_op jit(solution)/shard_map/all_to_all | solution.py:102
  106.1 0.0 copy-done
  106.1 0.9 fusion.4
  107.0 0.7 copy.10
  (15 shorter events, 0.3 us)
Async XLA Ops:
  0.6 3.3 %copy-start.1 = (bf16[128,768]{1,0:T(8,128)(2,1)S(1)}, bf16[128,768]{1,0:T(8,128)(2,1)}, u32[]{:S(2)}) copy-start(bf16[128,768]{1,0:T(8,128)(2,1)} %param.5) | copy-start | bytes 589828
  10.0 30.5 %all-to-all-start = ((bf16[16,64,896]{2,1,0:T(8,128)(2,1)}), bf16[16,64,896]{2,1,0:T(8,128)(2,1)}, u32[]{:S(2)}, u32[]{:S(2)}) async-start(bf16[16,64,896]{2,1,0:T(8,128)(2,1)} %bitcast.1), calls=%async_computation | async-start | bytes 3670016 | tf_op jit(solution)/shard_map/all_to_all | solution.py:74
  40.4 30.4 %all-to-all-start.1 = ((bf16[16,64,768]{2,1,0:T(8,128)(2,1)}), bf16[16,64,768]{2,1,0:T(8,128)(2,1)S(1)}, u32[]{:S(2)}, u32[]{:S(2)}) async-start(bf16[16,64,768]{2,1,0:T(8,128)(2,1)} %broadcast_select_fusion), calls=%async_computation.1 | async-start | bytes 3145728 | tf_op jit(solution)/shard_map/all_to_all | solution.py:77
  45.6 25.8 %copy-start.2 = (s32[96]{0:T(128)S(1)}, s32[96]{0:T(128)}, u32[]{:S(2)}) copy-start(s32[96]{0:T(128)} %param.9) | copy-start | bytes 1156
  47.4 23.4 %collective-permute-start = (f32[96,768]{1,0:T(8,128)S(1)}, f32[96,768]{1,0:T(8,128)S(1)}, u32[]{:S(2)}, u32[]{:S(2)}) collective-permute-start(f32[96,768]{1,0:T(8,128)S(1)} %fusion.1), channel_id=1, source_target_pairs={{0,4},{4,0},{1,5},{5,1},{2,6},{6,2},{3,7},{7,3},{8,12},{12,8},{9,1... | collective-permute-start | bytes 884744 | tf_op jit(solution)/shard_map/ppermute | solution.py:86
  71.4 34.7 %copy-start = (bf16[96,768]{1,0:T(8,128)(2,1)}, bf16[96,768]{1,0:T(8,128)(2,1)S(1)}, u32[]{:S(2)}) copy-start(bf16[96,768]{1,0:T(8,128)(2,1)S(1)} %multiply_convert_fusion) | copy-start | bytes 442372
  89.3 6.0 %collective-permute-start.1 = (f32[16,768]{1,0:T(8,128)S(1)}, f32[16,768]{1,0:T(8,128)S(1)}, u32[]{:S(2)}, u32[]{:S(2)}) collective-permute-start(f32[16,768]{1,0:T(8,128)S(1)} %reduce_sum.38), channel_id=1, source_target_pairs={{0,4},{4,0},{1,5},{5,1},{2,6},{6,2},{3,7},{7,3},{8,12},{12,8},{9,1... | collective-permute-start | bytes 147464 | tf_op jit(solution)/shard_map/ppermute | solution.py:100

commit v19 on v17

--- a/solution.py
+++ b/solution.py
@@ -59,13 +59,16 @@
     lanes = 128
     wide = width + lanes
     doc_part = (first_doc[:, None] == jnp.arange(docs, dtype=jnp.int32)[None, :]).astype(bf16)
-    table = jnp.concatenate([doc_embed, jnp.zeros((docs, lanes), bf16)], axis=1)
-    lane = jnp.arange(wide, dtype=jnp.int32)[None, :]
-    slot_pair = slot_plus.astype(f32).reshape(2, group * capacity)
-    slot_lanes = jnp.where(
-        lane == width, slot_pair[0][:, None], jnp.where(lane == width + 1, slot_pair[1][:, None], 0.0)
+    slot_part = slot_plus.astype(bf16).reshape(2, group * capacity).T
+    chooser = jnp.concatenate([doc_part, slot_part], axis=1)
+    table = jnp.concatenate(
+        [
+            jnp.concatenate([doc_embed, jnp.zeros((docs, lanes), bf16)], axis=1),
+            jnp.concatenate([jnp.zeros((2, width), bf16), jnp.eye(2, lanes, dtype=bf16)], axis=1),
+        ],
+        axis=0,
     )
-    send_first = (jnp.dot(doc_part, table, preferred_element_type=f32) + slot_lanes).astype(bf16)
+    send_first = jnp.dot(chooser, table, preferred_element_type=f32).astype(bf16)
     pick = (second_doc[:, None] == jnp.arange(docs, dtype=jnp.int32)[None, :]).astype(bf16)
     send_second = jnp.dot(pick, doc_embed, preferred_element_type=f32).astype(bf16)
 
@@ -80,7 +83,7 @@
 
     label_ids = jnp.arange(owned, dtype=jnp.int32)
     first_hot = (label_ids[:, None] == first_slot[None, :]).astype(bf16)
-    mirror_part = jnp.dot(first_hot, got_first, preferred_element_type=f32)[:, :width]
+    mirror_part = jnp.dot(first_hot, got_first[:, :width], preferred_element_type=f32)
     mirrored = lax.ppermute(mirror_part, "zh", [(0, 1), (1, 0)])
     second_hot = (label_ids[:, None] == second_slot[None, :]).astype(bf16)
     own_part = jnp.dot(second_hot, got_second, preferred_element_type=f32)

time: 104 us -> 104 us (level)
  no operation moved by 1% of the time
where the time goes in v19:
time: 104 us
  waiting for transfers between devices  50.3 us (48%)
  blocking collectives  28.1 us (27%)
  starting transfers between devices  13 us (12%)
  matrix products  8.57 us (8%)
  other arithmetic  1.89 us (2%)
  local copies, waits for them, and re-layouts  1.24 us (1%)
    all_to_all x1, waiting for transfers between devices, local(): lax.all_to_all(send_second.reshape(group, capacity, width), near, split_a...  22.5 us
    all_to_all x1, waiting for transfers between devices, local(): lax.all_to_all(send_first.reshape(group, capacity, wide), near, split_axi...  22.2 us
    all_to_all x1, blocking collectives, local(): lax.all_to_all(partial_sums.reshape(group, share, width), near, split_axi...  17.6 us
    all_to_all x1, blocking collectives, local(): lax.all_to_all(jnp.broadcast_to(own[None], (group, share, width)), near,...  10.5 us
    all_to_all x1, starting transfers between devices, local(): lax.all_to_all(send_first.reshape(group, capacity, wide), near, split_axi...  6.31 us
    ppermute x1, waiting for transfers between devices, local(): sums = half_sums + lax.ppermute(half_sums, 'zh', [(0, 1), (1, 0)])  5.6 us
    all_to_all x1, starting transfers between devices, local(): lax.all_to_all(send_second.reshape(group, capacity, width), near, split_a...  3.71 us
    ppermute x1, starting transfers between devices, local(): mirrored = lax.ppermute(mirror_part, 'zh', [(0, 1), (1, 0)])  2.59 us
  transfers between devices with their start and end apart: 4, of which 3 were waited for; matrix products, arithmetic and copies ran while one was open for 3% of the time, Pallas kernels for 0%

profile of v19, /device:TPU:0, one launch (start us, length us, event | category | flops | bytes accessed | tf_op | source)
XLA Modules:
  0.0 104.0 jit_solution(3818561787320730580)
XLA Ops:
  0.6 0.0 copy-start.1
  0.7 1.2 %fusion.5 = f32[1024]{0:T(1024)S(1)} fusion(s32[1024]{0:T(1024)} %bitcast.21, s32[32]{0:T(128)S(1)} %fusion.33), kind=kOutput, calls=%fused_computation.10 | convolution fusion | flops 68353024 | bytes 8320 | tf_op jit(solution)/shard_map/dot_general | solution.py:41
  1.9 0.7 add_convert_fusion
  2.7 0.9 convolution_convert_fusion.2
  3.6 0.1 slice_add_fusion
  3.7 0.1 slice.30
  3.7 0.1 convert_element_type.76
  3.8 0.2 copy.11
  4.1 0.2 fusion.9
  4.3 0.0 copy-done.1
  4.3 2.0 %convolution_convert_fusion = bf16[1024,896]{1,0:T(8,128)(2,1)} fusion(bf16[1024,2]{1,0:T(8,128)(2,1)S(1)} %copy.11, bf16[1024,128]{1,0:T(8,128)(2,1)S(1)} %fusion.9, bf16[128,768]{1,0:T(8,128)(2,1)S(1)} %copy-done.1, bf16[2,896]{1,0:T(2,128)(2,1)S(1)} %pad_convert_fusion), kind=kOutput, calls=%fused_computation.2 | convolution fusion | flops 240699904 | bytes 2301440 | tf_op jit(solution)/shard_map/dot_general | solution.py:71
  6.2 6.3 %all-to-all-start = ((bf16[16,64,896]{2,1,0:T(8,128)(2,1)}), bf16[16,64,896]{2,1,0:T(8,128)(2,1)S(1)}, u32[]{:S(2)}, u32[]{:S(2)}) async-start(bf16[16,64,896]{2,1,0:T(8,128)(2,1)} %bitcast.19), calls=%async_computation | async-start | bytes 3670016 | tf_op jit(solution)/shard_map/all_to_all | solution.py:75
  12.6 0.1 slice.34
  12.6 1.8 %convolution_convert_fusion.1 = bf16[1024,768]{1,0:T(8,128)(2,1)} fusion(bf16[128,768]{1,0:T(8,128)(2,1)S(1)} %copy-done.1, s32[1024]{0:T(1024)S(1)} %slice.34), kind=kOutput, calls=%fused_computation.3 | convolution fusion | flops 202244096 | bytes 1773568 | tf_op jit(solution)/shard_map/dot_general | solution.py:73
  14.4 22.2 %all-to-all-done = bf16[16,64,896]{2,1,0:T(8,128)(2,1)S(1)} async-done(((bf16[16,64,896]{2,1,0:T(8,128)(2,1)}), bf16[16,64,896]{2,1,0:T(8,128)(2,1)S(1)}, u32[]{:S(2)}, u32[]{:S(2)}) %all-to-all-start) | async-done | bytes 1835040 | tf_op jit(solution)/shard_map/all_to_all | solution.py:75
  36.6 3.7 %all-to-all-start.1 = ((bf16[16,64,768]{2,1,0:T(8,128)(2,1)}), bf16[16,64,768]{2,1,0:T(8,128)(2,1)S(1)}, u32[]{:S(2)}, u32[]{:S(2)}) async-start(bf16[16,64,768]{2,1,0:T(8,128)(2,1)} %bitcast.4), calls=%async_computation.1 | async-start | bytes 3145728 | tf_op jit(solution)/shard_map/all_to_all | solution.py:78
  40.3 0.4 add_reduce_fusion.1
  40.7 0.0 copy-start.2
  40.7 1.1 %fusion.1 = f32[96,768]{1,0:T(8,128)} fusion(bf16[1024,896]{1,0:T(8,128)(2,1)S(1)} %bitcast.18, s32[1024]{0:T(1024)S(1)} %get-tuple-element.4), kind=kOutput, calls=%fused_computation.4 | convolution fusion | flops 151093248 | bytes 1871872 | tf_op jit(solution)/shard_map/dot_general | solution.py:86
  41.9 2.6 %collective-permute-start = (f32[96,768]{1,0:T(8,128)}, f32[96,768]{1,0:T(8,128)S(1)}, u32[]{:S(2)}, u32[]{:S(2)}) collective-permute-start(f32[96,768]{1,0:T(8,128)} %fusion.1), channel_id=1, source_target_pairs={{0,4},{4,0},{1,5},{5,1},{2,6},{6,2},{3,7},{7,3},{8,12},{12,8},{9,1... | collective-permute-start | bytes 884744 | tf_op jit(solution)/shard_map/ppermute | solution.py:87
  44.4 22.5 %all-to-all-done.1 = bf16[16,64,768]{2,1,0:T(8,128)(2,1)S(1)} async-done(((bf16[16,64,768]{2,1,0:T(8,128)(2,1)}), bf16[16,64,768]{2,1,0:T(8,128)(2,1)S(1)}, u32[]{:S(2)}, u32[]{:S(2)}) %all-to-all-start.1) | async-done | bytes 1572896 | tf_op jit(solution)/shard_map/all_to_all | solution.py:78
  67.0 0.0 collective-permute-done
  67.0 0.5 multiply_reduce_fusion
  67.5 0.1 multiply_convert_fusion
  67.6 0.0 copy-done.2
  67.6 0.0 copy-start
  67.6 0.2 fusion.24
  67.8 17.6 %all_to_all.20 = f32[16,16,768]{2,1,0:T(8,128)S(1)} all-to-all(f32[16,16,768]{2,1,0:T(8,128)S(1)} %bitcast.16), channel_id=1, replica_groups=mesh['y'=2,'core'=2,'zh'=2,'zl'=2,'x'=2] {'y','core','x','zl'}, dimensions={0} | all-to-all | bytes 1572864 | tf_op jit(solution)/shard_map/all_to_all | solution.py:97
  85.5 0.4 collective-permute-start.1
  85.9 5.6 %collective-permute-done.1 = f32[16,768]{1,0:T(8,128)S(1)} collective-permute-done((f32[16,768]{1,0:T(8,128)S(1)}, f32[16,768]{1,0:T(8,128)S(1)}, u32[]{:S(2)}, u32[]{:S(2)}) %collective-permute-start.1) | collective-permute-done | bytes 49184 | tf_op jit(solution)/shard_map/ppermute | solution.py:101
  91.5 0.1 multiply_reduce_fusion.1
  91.7 0.1 multiply_convert_fusion.1
  91.8 10.5 %all_to_all.21 = bf16[16,16,768]{2,1,0:T(8,128)(2,1)S(1)} all-to-all(bf16[16,16,768]{2,1,0:T(8,128)(2,1)S(1)} %broadcast_in_dim.12), channel_id=1, replica_groups=mesh['y'=2,'core'=2,'zh'=2,'zl'=2,'x'=2] {'y','core','x','zl'}, dimensions={0} | all-to-all | bytes 786432 | tf_op jit(solution)/shard_map/all_to_all | solution.py:103
  102.3 0.0 copy-done
  102.3 0.9 fusion.4
  103.2 0.7 copy.13
  (10 shorter events, 0.2 us)
Async XLA Ops:
  0.6 3.6 %copy-start.1 = (bf16[128,768]{1,0:T(8,128)(2,1)S(1)}, bf16[128,768]{1,0:T(8,128)(2,1)}, u32[]{:S(2)}) copy-start(bf16[128,768]{1,0:T(8,128)(2,1)} %param.5) | copy-start | bytes 589828
  6.2 30.3 %all-to-all-start = ((bf16[16,64,896]{2,1,0:T(8,128)(2,1)}), bf16[16,64,896]{2,1,0:T(8,128)(2,1)S(1)}, u32[]{:S(2)}, u32[]{:S(2)}) async-start(bf16[16,64,896]{2,1,0:T(8,128)(2,1)} %bitcast.19), calls=%async_computation | async-start | bytes 3670016 | tf_op jit(solution)/shard_map/all_to_all | solution.py:75
  36.6 30.4 %all-to-all-start.1 = ((bf16[16,64,768]{2,1,0:T(8,128)(2,1)}), bf16[16,64,768]{2,1,0:T(8,128)(2,1)S(1)}, u32[]{:S(2)}, u32[]{:S(2)}) async-start(bf16[16,64,768]{2,1,0:T(8,128)(2,1)} %bitcast.4), calls=%async_computation.1 | async-start | bytes 3145728 | tf_op jit(solution)/shard_map/all_to_all | solution.py:78
  40.7 26.8 %copy-start.2 = (s32[96]{0:T(128)S(1)}, s32[96]{0:T(128)}, u32[]{:S(2)}) copy-start(s32[96]{0:T(128)} %param.9) | copy-start | bytes 1156
  41.9 25.1 %collective-permute-start = (f32[96,768]{1,0:T(8,128)}, f32[96,768]{1,0:T(8,128)S(1)}, u32[]{:S(2)}, u32[]{:S(2)}) collective-permute-start(f32[96,768]{1,0:T(8,128)} %fusion.1), channel_id=1, source_target_pairs={{0,4},{4,0},{1,5},{5,1},{2,6},{6,2},{3,7},{7,3},{8,12},{12,8},{9,1... | collective-permute-start | bytes 884744 | tf_op jit(solution)/shard_map/ppermute | solution.py:87
  67.6 34.7 %copy-start = (bf16[96,768]{1,0:T(8,128)(2,1)}, bf16[96,768]{1,0:T(8,128)(2,1)S(1)}, u32[]{:S(2)}) copy-start(bf16[96,768]{1,0:T(8,128)(2,1)S(1)} %multiply_convert_fusion) | copy-start | bytes 442372
  85.5 6.0 %collective-permute-start.1 = (f32[16,768]{1,0:T(8,128)S(1)}, f32[16,768]{1,0:T(8,128)S(1)}, u32[]{:S(2)}, u32[]{:S(2)}) collective-permute-start(f32[16,768]{1,0:T(8,128)S(1)} %reduce_sum.38), channel_id=1, source_target_pairs={{0,4},{4,0},{1,5},{5,1},{2,6},{6,2},{3,7},{7,3},{8,12},{12,8},{9,1... | collective-permute-start | bytes 147464 | tf_op jit(solution)/shard_map/ppermute | solution.py:101

commit v20 on v17

--- a/solution.py
+++ b/solution.py
@@ -95,7 +95,10 @@
             partial_sums.reshape(group, share, width), near, split_axis=0, concat_axis=0, tiled=True
         )
         half_sums = jnp.sum(parts, axis=0)
-        sums = half_sums + lax.ppermute(half_sums, "zh", [(0, 1), (1, 0)])
+        both = lax.all_to_all(
+            jnp.broadcast_to(half_sums[None], (2, share, width)), "zh", split_axis=0, concat_axis=0, tiled=True
+        )
+        sums = both[0] + both[1]
         own = rms_scale(sums).astype(bf16)
         centroids = lax.all_to_all(
             jnp.broadcast_to(own[None], (group, share, width)),

time: 104 us -> 107 us (1.029)
  blocking collectives: 28.1 us -> 36.7 us
  waiting for transfers between devices: 50.3 us -> 44.7 us
    all_to_all x0 -> x1, blocking collectives: none -> 8.53 us  [local(): lax.all_to_all(jnp.broadcast_to(half_sums[None], (2, share, width)), 'zh'...]
    ppermute x1 -> x0, waiting for transfers between devices: 5.6 us -> none  [local(): sums = half_sums + lax.ppermute(half_sums, 'zh', [(0, 1), (1, 0)])]
  transfers between devices with their start and end apart: 4 -> 3, of which waited for: 3 -> 2; matrix products, arithmetic and copies ran while one was open for 3% -> 3% of each run, Pallas kernels for 0% -> 0%
where the time goes in v20:
time: 107 us; the launch traced here: 106 us
  waiting for transfers between devices  44.7 us (42%)
  blocking collectives  36.7 us (34%)
  starting transfers between devices  12.6 us (12%)
  matrix products  8.78 us (8%)
  other arithmetic  1.67 us (2%)
  local copies, waits for them, and re-layouts  1.09 us (1%)
    all_to_all x1, waiting for transfers between devices, local(): lax.all_to_all(send_second.reshape(group, capacity, width), near, split_a...  22.5 us
    all_to_all x1, waiting for transfers between devices, local(): lax.all_to_all(send_first.reshape(group, capacity, wide), near, split_axi...  22.2 us
    all_to_all x1, blocking collectives, local(): lax.all_to_all(partial_sums.reshape(group, share, width), near, split_axi...  17.6 us
    all_to_all x1, blocking collectives, local(): lax.all_to_all(jnp.broadcast_to(own[None], (group, share, width)), near,...  10.5 us
    all_to_all x1, blocking collectives, local(): lax.all_to_all(jnp.broadcast_to(half_sums[None], (2, share, width)), 'zh'...  8.53 us
    all_to_all x1, starting transfers between devices, local(): lax.all_to_all(send_first.reshape(group, capacity, wide), near, split_axi...  6.31 us
    all_to_all x1, starting transfers between devices, local(): lax.all_to_all(send_second.reshape(group, capacity, width), near, split_a...  3.71 us
    ppermute x1, starting transfers between devices, local(): mirrored = lax.ppermute(mirror_part, 'zh', [(0, 1), (1, 0)])  2.59 us
  transfers between devices with their start and end apart: 3, of which 2 were waited for; matrix products, arithmetic and copies ran while one was open for 3% of the time, Pallas kernels for 0%

profile of v20, /device:TPU:0, one launch (start us, length us, event | category | flops | bytes accessed | tf_op | source)
XLA Modules:
  0.0 106.3 jit_solution(5857008201725206781)
XLA Ops:
  0.6 0.0 copy-start.1
  0.7 1.2 %fusion.5 = f32[1024]{0:T(1024)S(1)} fusion(s32[1024]{0:T(1024)} %bitcast.21, s32[32]{0:T(128)S(1)} %fusion.25), kind=kOutput, calls=%fused_computation.10 | convolution fusion | flops 68353024 | bytes 8320 | tf_op jit(solution)/shard_map/dot_general | solution.py:41
  1.9 0.7 add_convert_fusion.1
  2.7 0.9 convolution_convert_fusion.1
  3.6 0.1 slice_add_fusion.1
  3.7 0.1 slice.49
  3.7 0.1 slice.52
  3.8 0.1 slice.54
  3.9 0.0 copy-done.1
  3.9 2.2 %add_convert_fusion = bf16[1024,896]{1,0:T(8,128)(2,1)} fusion(f32[1024]{0:T(1024)S(1)} %slice.54, f32[1024]{0:T(1024)S(1)} %slice.52, pred[896]{0:T(1024)(128)(4,1)S(1)} %get-tuple-element.17, pred[896]{0:T(1024)(128)(4,1)S(1)} %get-tuple-element.18, s32[1024]{0:T(1024)S(1)} %slice.49, bf16[128,768]{1,0:T(8,128)(2,1)S(1)} %copy-done.1), kind=kOutput, calls=%fused_computation.2 | convolution fusion | flops 238682112 | bytes 2045696 | tf_op jit(solution)/shard_map/dot_general | solution.py:68
  6.1 6.3 %all-to-all-start = ((bf16[16,64,896]{2,1,0:T(8,128)(2,1)}), bf16[16,64,896]{2,1,0:T(8,128)(2,1)S(1)}, u32[]{:S(2)}, u32[]{:S(2)}) async-start(bf16[16,64,896]{2,1,0:T(8,128)(2,1)} %bitcast.20), calls=%async_computation | async-start | bytes 3670016 | tf_op jit(solution)/shard_map/all_to_all | solution.py:72
  12.4 0.1 slice.57
  12.4 1.8 %convolution_convert_fusion = bf16[1024,768]{1,0:T(8,128)(2,1)} fusion(bf16[128,768]{1,0:T(8,128)(2,1)S(1)} %copy-done.1, s32[1024]{0:T(1024)S(1)} %slice.57), kind=kOutput, calls=%fused_computation.3 | convolution fusion | flops 202244096 | bytes 1773568 | tf_op jit(solution)/shard_map/dot_general | solution.py:70
  14.2 22.2 %all-to-all-done = bf16[16,64,896]{2,1,0:T(8,128)(2,1)S(1)} async-done(((bf16[16,64,896]{2,1,0:T(8,128)(2,1)}), bf16[16,64,896]{2,1,0:T(8,128)(2,1)S(1)}, u32[]{:S(2)}, u32[]{:S(2)}) %all-to-all-start) | async-done | bytes 1835040 | tf_op jit(solution)/shard_map/all_to_all | solution.py:72
  36.4 3.7 %all-to-all-start.1 = ((bf16[16,64,768]{2,1,0:T(8,128)(2,1)}), bf16[16,64,768]{2,1,0:T(8,128)(2,1)S(1)}, u32[]{:S(2)}, u32[]{:S(2)}) async-start(bf16[16,64,768]{2,1,0:T(8,128)(2,1)} %bitcast.3), calls=%async_computation.1 | async-start | bytes 3145728 | tf_op jit(solution)/shard_map/all_to_all | solution.py:75
  40.1 0.4 add_reduce_fusion.1
  40.6 0.0 copy-start.2
  40.6 1.1 %fusion.1 = f32[96,768]{1,0:T(8,128)} fusion(bf16[1024,896]{1,0:T(8,128)(2,1)S(1)} %bitcast.19, s32[1024]{0:T(1024)S(1)} %get-tuple-element.4), kind=kOutput, calls=%fused_computation.4 | convolution fusion | flops 151093248 | bytes 1871872 | tf_op jit(solution)/shard_map/dot_general | solution.py:83
  41.7 2.6 %collective-permute-start = (f32[96,768]{1,0:T(8,128)}, f32[96,768]{1,0:T(8,128)S(1)}, u32[]{:S(2)}, u32[]{:S(2)}) collective-permute-start(f32[96,768]{1,0:T(8,128)} %fusion.1), channel_id=1, source_target_pairs={{0,4},{4,0},{1,5},{5,1},{2,6},{6,2},{3,7},{7,3},{8,12},{12,8},{9,1... | collective-permute-start | bytes 884744 | tf_op jit(solution)/shard_map/ppermute | solution.py:84
  44.3 22.5 %all-to-all-done.1 = bf16[16,64,768]{2,1,0:T(8,128)(2,1)S(1)} async-done(((bf16[16,64,768]{2,1,0:T(8,128)(2,1)}), bf16[16,64,768]{2,1,0:T(8,128)(2,1)S(1)}, u32[]{:S(2)}, u32[]{:S(2)}) %all-to-all-start.1) | async-done | bytes 1572896 | tf_op jit(solution)/shard_map/all_to_all | solution.py:75
  66.8 0.0 collective-permute-done
  66.8 0.5 multiply_reduce_fusion
  67.3 0.1 multiply_convert_fusion
  67.4 0.0 copy-done.2
  67.4 0.0 copy-start
  67.4 0.2 fusion.16
  67.7 17.6 %all_to_all.25 = f32[16,16,768]{2,1,0:T(8,128)S(1)} all-to-all(f32[16,16,768]{2,1,0:T(8,128)S(1)} %bitcast.17), channel_id=1, replica_groups=mesh['y'=2,'core'=2,'zh'=2,'zl'=2,'x'=2] {'y','core','x','zl'}, dimensions={0} | all-to-all | bytes 1572864 | tf_op jit(solution)/shard_map/all_to_all | solution.py:94
  85.3 8.5 %all_to_all.26 = f32[2,16,768]{2,1,0:T(8,128)S(1)} all-to-all(f32[2,16,768]{2,1,0:T(8,128)S(1)} %broadcast_in_dim.84), channel_id=1, replica_groups=mesh['y'=2,'core'=2,'zh'=2,'zl'=2,'x'=2] {'zh'}, dimensions={0} | all-to-all | bytes 196608 | tf_op jit(solution)/shard_map/all_to_all | solution.py:98
  93.9 0.1 multiply_reduce_fusion.1
  94.0 0.1 fusion.22
  94.1 10.5 %all_to_all.27 = bf16[16,16,768]{2,1,0:T(8,128)(2,1)S(1)} all-to-all(bf16[16,16,768]{2,1,0:T(8,128)(2,1)S(1)} %broadcast_in_dim.86), channel_id=1, replica_groups=mesh['y'=2,'core'=2,'zh'=2,'zl'=2,'x'=2] {'y','core','x','zl'}, dimensions={0} | all-to-all | bytes 786432 | tf_op jit(solution)/shard_map/all_to_all | solution.py:103
  104.6 0.0 copy-done
  104.6 0.9 fusion.4
  105.5 0.7 copy.10
  (11 shorter events, 0.2 us)
Async XLA Ops:
  0.6 3.3 %copy-start.1 = (bf16[128,768]{1,0:T(8,128)(2,1)S(1)}, bf16[128,768]{1,0:T(8,128)(2,1)}, u32[]{:S(2)}) copy-start(bf16[128,768]{1,0:T(8,128)(2,1)} %param.5) | copy-start | bytes 589828
  6.1 30.3 %all-to-all-start = ((bf16[16,64,896]{2,1,0:T(8,128)(2,1)}), bf16[16,64,896]{2,1,0:T(8,128)(2,1)S(1)}, u32[]{:S(2)}, u32[]{:S(2)}) async-start(bf16[16,64,896]{2,1,0:T(8,128)(2,1)} %bitcast.20), calls=%async_computation | async-start | bytes 3670016 | tf_op jit(solution)/shard_map/all_to_all | solution.py:72
  36.4 30.4 %all-to-all-start.1 = ((bf16[16,64,768]{2,1,0:T(8,128)(2,1)}), bf16[16,64,768]{2,1,0:T(8,128)(2,1)S(1)}, u32[]{:S(2)}, u32[]{:S(2)}) async-start(bf16[16,64,768]{2,1,0:T(8,128)(2,1)} %bitcast.3), calls=%async_computation.1 | async-start | bytes 3145728 | tf_op jit(solution)/shard_map/all_to_all | solution.py:75
  40.6 26.8 %copy-start.2 = (s32[96]{0:T(128)S(1)}, s32[96]{0:T(128)}, u32[]{:S(2)}) copy-start(s32[96]{0:T(128)} %param.9) | copy-start | bytes 1156
  41.7 25.1 %collective-permute-start = (f32[96,768]{1,0:T(8,128)}, f32[96,768]{1,0:T(8,128)S(1)}, u32[]{:S(2)}, u32[]{:S(2)}) collective-permute-start(f32[96,768]{1,0:T(8,128)} %fusion.1), channel_id=1, source_target_pairs={{0,4},{4,0},{1,5},{5,1},{2,6},{6,2},{3,7},{7,3},{8,12},{12,8},{9,1... | collective-permute-start | bytes 884744 | tf_op jit(solution)/shard_map/ppermute | solution.py:84
  67.4 37.2 %copy-start = (bf16[96,768]{1,0:T(8,128)(2,1)}, bf16[96,768]{1,0:T(8,128)(2,1)S(1)}, u32[]{:S(2)}) copy-start(bf16[96,768]{1,0:T(8,128)(2,1)S(1)} %multiply_convert_fusion) | copy-start | bytes 442372

commit v21 on v17

--- a/solution.py
+++ b/solution.py
@@ -41,19 +41,20 @@
     before_t = jnp.dot(hits_t, earlier_t, preferred_element_type=f32)
     rank_row = jnp.sum(before_t * hits_t.astype(f32), axis=0, keepdims=True).astype(jnp.int32)
 
-    at_rank_t = (jnp.arange(capacity, dtype=jnp.int32)[:, None] == rank_row).astype(f32)
+    at_rank_t = (jnp.arange(capacity, dtype=jnp.int32)[:, None] == rank_row).astype(bf16)
+    hits_f = hits_t.astype(f32)
     tagged_t = jnp.concatenate(
         [
-            at_rank_t * (pair_doc.reshape(1, pairs) + 1).astype(f32),
-            at_rank_t * (pair_slot.reshape(1, pairs) + 1).astype(f32),
+            hits_f * (pair_doc.reshape(1, pairs) + 1).astype(f32),
+            hits_f * (pair_slot.reshape(1, pairs) + 1).astype(f32),
         ],
         axis=0,
     ).astype(bf16)
     picked = lax.dot_general(
-        hits_t, tagged_t, (((1,), (1,)), ((), ())), preferred_element_type=f32
+        tagged_t, at_rank_t, (((1,), (1,)), ((), ())), preferred_element_type=f32
     ).astype(jnp.int32)
-    send_doc = picked[:, :capacity].reshape(devices * capacity) - 1
-    slot_plus = picked[:, capacity:].reshape(devices * capacity)
+    send_doc = picked[:devices].reshape(devices * capacity) - 1
+    slot_plus = picked[devices:].reshape(devices * capacity)
     first_doc, second_doc = send_doc[: group * capacity], send_doc[group * capacity :]
 
     lanes = 128

time: 104 us -> 104 us (level)
  no operation moved by 1% of the time
where the time goes in v21:
time: 104 us
  waiting for transfers between devices  50.3 us (48%)
  blocking collectives  28.1 us (27%)
  starting transfers between devices  13 us (12%)
  matrix products  8.07 us (8%)
  other arithmetic  2.33 us (2%)
  local copies, waits for them, and re-layouts  1.08 us (1%)
    all_to_all x1, waiting for transfers between devices, local(): lax.all_to_all(send_second.reshape(group, capacity, width), near, split_a...  22.5 us
    all_to_all x1, waiting for transfers between devices, local(): lax.all_to_all(send_first.reshape(group, capacity, wide), near, split_axi...  22.2 us
    all_to_all x1, blocking collectives, local(): lax.all_to_all(partial_sums.reshape(group, share, width), near, split_axi...  17.6 us
    all_to_all x1, blocking collectives, local(): lax.all_to_all(jnp.broadcast_to(own[None], (group, share, width)), near,...  10.5 us
    all_to_all x1, starting transfers between devices, local(): lax.all_to_all(send_first.reshape(group, capacity, wide), near, split_axi...  6.32 us
    ppermute x1, waiting for transfers between devices, local(): sums = half_sums + lax.ppermute(half_sums, 'zh', [(0, 1), (1, 0)])  5.6 us
    all_to_all x1, starting transfers between devices, local(): lax.all_to_all(send_second.reshape(group, capacity, width), near, split_a...  3.71 us
    ppermute x1, starting transfers between devices, local(): mirrored = lax.ppermute(mirror_part, 'zh', [(0, 1), (1, 0)])  2.59 us
  transfers between devices with their start and end apart: 4, of which 3 were waited for; matrix products, arithmetic and copies ran while one was open for 3% of the time, Pallas kernels for 0%

profile of v21, /device:TPU:0, one launch (start us, length us, event | category | flops | bytes accessed | tf_op | source)
XLA Modules:
  0.0 103.7 jit_solution(15848143108053815367)
XLA Ops:
  0.6 0.0 copy-start.1
  0.7 1.2 %fusion.5 = f32[1024]{0:T(1024)S(1)} fusion(s32[1024]{0:T(1024)} %bitcast.19, s32[32]{0:T(128)S(1)} %fusion.24), kind=kOutput, calls=%fused_computation.10 | convolution fusion | flops 68353024 | bytes 8320 | tf_op jit(solution)/shard_map/dot_general | solution.py:41
  1.9 0.7 add_convert_fusion.1
  2.6 0.8 fusion.12
  3.4 0.2 convolution_convert_fusion.1
  3.6 0.1 slice.43
  3.7 0.1 slice.46
  3.8 0.1 slice.48
  3.8 0.0 copy-done.1
  3.8 2.2 %add_convert_fusion = bf16[1024,896]{1,0:T(8,128)(2,1)} fusion(f32[1024]{0:T(1024)S(1)} %slice.48, f32[1024]{0:T(1024)S(1)} %slice.46, pred[896]{0:T(1024)(128)(4,1)S(1)} %get-tuple-element.19, pred[896]{0:T(1024)(128)(4,1)S(1)} %get-tuple-element.20, s32[1024]{0:T(1024)S(1)} %slice.43, bf16[128,768]{1,0:T(8,128)(2,1)S(1)} %copy-done.1), kind=kOutput, calls=%fused_computation.2 | convolution fusion | flops 238682112 | bytes 2045696 | tf_op jit(solution)/shard_map/dot_general | solution.py:69
  6.0 6.3 %all-to-all-start = ((bf16[16,64,896]{2,1,0:T(8,128)(2,1)}), bf16[16,64,896]{2,1,0:T(8,128)(2,1)S(1)}, u32[]{:S(2)}, u32[]{:S(2)}) async-start(bf16[16,64,896]{2,1,0:T(8,128)(2,1)} %bitcast.18), calls=%async_computation | async-start | bytes 3670016 | tf_op jit(solution)/shard_map/all_to_all | solution.py:73
  12.3 0.1 slice.51
  12.4 1.8 %convolution_convert_fusion = bf16[1024,768]{1,0:T(8,128)(2,1)} fusion(bf16[128,768]{1,0:T(8,128)(2,1)S(1)} %copy-done.1, s32[1024]{0:T(1024)S(1)} %slice.51), kind=kOutput, calls=%fused_computation.3 | convolution fusion | flops 202244096 | bytes 1773568 | tf_op jit(solution)/shard_map/dot_general | solution.py:71
  14.2 22.2 %all-to-all-done = bf16[16,64,896]{2,1,0:T(8,128)(2,1)S(1)} async-done(((bf16[16,64,896]{2,1,0:T(8,128)(2,1)}), bf16[16,64,896]{2,1,0:T(8,128)(2,1)S(1)}, u32[]{:S(2)}, u32[]{:S(2)}) %all-to-all-start) | async-done | bytes 1835040 | tf_op jit(solution)/shard_map/all_to_all | solution.py:73
  36.3 3.7 %all-to-all-start.1 = ((bf16[16,64,768]{2,1,0:T(8,128)(2,1)}), bf16[16,64,768]{2,1,0:T(8,128)(2,1)S(1)}, u32[]{:S(2)}, u32[]{:S(2)}) async-start(bf16[16,64,768]{2,1,0:T(8,128)(2,1)} %bitcast.3), calls=%async_computation.1 | async-start | bytes 3145728 | tf_op jit(solution)/shard_map/all_to_all | solution.py:76
  40.1 0.4 add_reduce_fusion.1
  40.5 0.0 copy-start.2
  40.5 1.1 %fusion.1 = f32[96,768]{1,0:T(8,128)} fusion(bf16[1024,896]{1,0:T(8,128)(2,1)S(1)} %bitcast.17, s32[1024]{0:T(1024)S(1)} %get-tuple-element.4), kind=kOutput, calls=%fused_computation.4 | convolution fusion | flops 151093248 | bytes 1871872 | tf_op jit(solution)/shard_map/dot_general | solution.py:84
  41.6 2.6 %collective-permute-start = (f32[96,768]{1,0:T(8,128)}, f32[96,768]{1,0:T(8,128)S(1)}, u32[]{:S(2)}, u32[]{:S(2)}) collective-permute-start(f32[96,768]{1,0:T(8,128)} %fusion.1), channel_id=1, source_target_pairs={{0,4},{4,0},{1,5},{5,1},{2,6},{6,2},{3,7},{7,3},{8,12},{12,8},{9,1... | collective-permute-start | bytes 884744 | tf_op jit(solution)/shard_map/ppermute | solution.py:85
  44.2 22.5 %all-to-all-done.1 = bf16[16,64,768]{2,1,0:T(8,128)(2,1)S(1)} async-done(((bf16[16,64,768]{2,1,0:T(8,128)(2,1)}), bf16[16,64,768]{2,1,0:T(8,128)(2,1)S(1)}, u32[]{:S(2)}, u32[]{:S(2)}) %all-to-all-start.1) | async-done | bytes 1572896 | tf_op jit(solution)/shard_map/all_to_all | solution.py:76
  66.7 0.0 collective-permute-done
  66.7 0.5 multiply_reduce_fusion
  67.2 0.1 multiply_convert_fusion
  67.3 0.0 copy-done.2
  67.3 0.0 copy-start
  67.4 0.2 fusion.18
  67.6 17.6 %all_to_all.20 = f32[16,16,768]{2,1,0:T(8,128)S(1)} all-to-all(f32[16,16,768]{2,1,0:T(8,128)S(1)} %bitcast.15), channel_id=1, replica_groups=mesh['y'=2,'core'=2,'zh'=2,'zl'=2,'x'=2] {'y','core','x','zl'}, dimensions={0} | all-to-all | bytes 1572864 | tf_op jit(solution)/shard_map/all_to_all | solution.py:95
  85.3 0.4 collective-permute-start.1
  85.7 5.6 %collective-permute-done.1 = f32[16,768]{1,0:T(8,128)S(1)} collective-permute-done((f32[16,768]{1,0:T(8,128)S(1)}, f32[16,768]{1,0:T(8,128)S(1)}, u32[]{:S(2)}, u32[]{:S(2)}) %collective-permute-start.1) | collective-permute-done | bytes 49184 | tf_op jit(solution)/shard_map/ppermute | solution.py:99
  91.3 0.1 multiply_reduce_fusion.1
  91.4 0.1 multiply_convert_fusion.1
  91.5 10.5 %all_to_all.21 = bf16[16,16,768]{2,1,0:T(8,128)(2,1)S(1)} all-to-all(bf16[16,16,768]{2,1,0:T(8,128)(2,1)S(1)} %broadcast_in_dim.76), channel_id=1, replica_groups=mesh['y'=2,'core'=2,'zh'=2,'zl'=2,'x'=2] {'y','core','x','zl'}, dimensions={0} | all-to-all | bytes 786432 | tf_op jit(solution)/shard_map/all_to_all | solution.py:101
  102.1 0.0 copy-done
  102.1 0.9 fusion.4
  103.0 0.7 copy.10
  (10 shorter events, 0.2 us)
Async XLA Ops:
  0.6 3.2 %copy-start.1 = (bf16[128,768]{1,0:T(8,128)(2,1)S(1)}, bf16[128,768]{1,0:T(8,128)(2,1)}, u32[]{:S(2)}) copy-start(bf16[128,768]{1,0:T(8,128)(2,1)} %param.5) | copy-start | bytes 589828
  6.0 30.3 %all-to-all-start = ((bf16[16,64,896]{2,1,0:T(8,128)(2,1)}), bf16[16,64,896]{2,1,0:T(8,128)(2,1)S(1)}, u32[]{:S(2)}, u32[]{:S(2)}) async-start(bf16[16,64,896]{2,1,0:T(8,128)(2,1)} %bitcast.18), calls=%async_computation | async-start | bytes 3670016 | tf_op jit(solution)/shard_map/all_to_all | solution.py:73
  36.3 30.4 %all-to-all-start.1 = ((bf16[16,64,768]{2,1,0:T(8,128)(2,1)}), bf16[16,64,768]{2,1,0:T(8,128)(2,1)S(1)}, u32[]{:S(2)}, u32[]{:S(2)}) async-start(bf16[16,64,768]{2,1,0:T(8,128)(2,1)} %bitcast.3), calls=%async_computation.1 | async-start | bytes 3145728 | tf_op jit(solution)/shard_map/all_to_all | solution.py:76
  40.5 26.8 %copy-start.2 = (s32[96]{0:T(128)S(1)}, s32[96]{0:T(128)}, u32[]{:S(2)}) copy-start(s32[96]{0:T(128)} %param.9) | copy-start | bytes 1156
  41.6 25.1 %collective-permute-start = (f32[96,768]{1,0:T(8,128)}, f32[96,768]{1,0:T(8,128)S(1)}, u32[]{:S(2)}, u32[]{:S(2)}) collective-permute-start(f32[96,768]{1,0:T(8,128)} %fusion.1), channel_id=1, source_target_pairs={{0,4},{4,0},{1,5},{5,1},{2,6},{6,2},{3,7},{7,3},{8,12},{12,8},{9,1... | collective-permute-start | bytes 884744 | tf_op jit(solution)/shard_map/ppermute | solution.py:85
  67.3 34.7 %copy-start = (bf16[96,768]{1,0:T(8,128)(2,1)}, bf16[96,768]{1,0:T(8,128)(2,1)S(1)}, u32[]{:S(2)}) copy-start(bf16[96,768]{1,0:T(8,128)(2,1)S(1)} %multiply_convert_fusion) | copy-start | bytes 442372
  85.3 6.0 %collective-permute-start.1 = (f32[16,768]{1,0:T(8,128)S(1)}, f32[16,768]{1,0:T(8,128)S(1)}, u32[]{:S(2)}, u32[]{:S(2)}) collective-permute-start(f32[16,768]{1,0:T(8,128)S(1)} %reduce_sum.38), channel_id=1, source_target_pairs={{0,4},{4,0},{1,5},{5,1},{2,6},{6,2},{3,7},{7,3},{8,12},{12,8},{9,1... | collective-permute-start | bytes 147464 | tf_op jit(solution)/shard_map/ppermute | solution.py:99

commit v22 on v21

--- a/solution.py
+++ b/solution.py
@@ -81,7 +81,7 @@
 
     label_ids = jnp.arange(owned, dtype=jnp.int32)
     first_hot = (label_ids[:, None] == first_slot[None, :]).astype(bf16)
-    mirror_part = jnp.dot(first_hot, got_first, preferred_element_type=f32)[:, :width]
+    mirror_part = jnp.dot(first_hot, got_first[:, :width], preferred_element_type=f32)
     mirrored = lax.ppermute(mirror_part, "zh", [(0, 1), (1, 0)])
     second_hot = (label_ids[:, None] == second_slot[None, :]).astype(bf16)
     own_part = jnp.dot(second_hot, got_second, preferred_element_type=f32)

time: 104 us -> 104 us (level)
  no operation moved by 1% of the time
where the time goes in v22:
time: 104 us
  waiting for transfers between devices  50.3 us (48%)
  blocking collectives  28.1 us (27%)
  starting transfers between devices  13 us (12%)
  matrix products  8.07 us (8%)
  other arithmetic  2.33 us (2%)
  local copies, waits for them, and re-layouts  1.08 us (1%)
    all_to_all x1, waiting for transfers between devices, local(): lax.all_to_all(send_second.reshape(group, capacity, width), near, split_a...  22.5 us
    all_to_all x1, waiting for transfers between devices, local(): lax.all_to_all(send_first.reshape(group, capacity, wide), near, split_axi...  22.2 us
    all_to_all x1, blocking collectives, local(): lax.all_to_all(partial_sums.reshape(group, share, width), near, split_axi...  17.6 us
    all_to_all x1, blocking collectives, local(): lax.all_to_all(jnp.broadcast_to(own[None], (group, share, width)), near,...  10.5 us
    all_to_all x1, starting transfers between devices, local(): lax.all_to_all(send_first.reshape(group, capacity, wide), near, split_axi...  6.32 us
    ppermute x1, waiting for transfers between devices, local(): sums = half_sums + lax.ppermute(half_sums, 'zh', [(0, 1), (1, 0)])  5.6 us
    all_to_all x1, starting transfers between devices, local(): lax.all_to_all(send_second.reshape(group, capacity, width), near, split_a...  3.71 us
    ppermute x1, starting transfers between devices, local(): mirrored = lax.ppermute(mirror_part, 'zh', [(0, 1), (1, 0)])  2.59 us
  transfers between devices with their start and end apart: 4, of which 3 were waited for; matrix products, arithmetic and copies ran while one was open for 3% of the time, Pallas kernels for 0%

profile of v22, /device:TPU:0, one launch (start us, length us, event | category | flops | bytes accessed | tf_op | source)
XLA Modules:
  0.0 103.7 jit_solution(15848143108053815367)
XLA Ops:
  0.6 0.0 copy-start.1
  0.7 1.2 %fusion.5 = f32[1024]{0:T(1024)S(1)} fusion(s32[1024]{0:T(1024)} %bitcast.19, s32[32]{0:T(128)S(1)} %fusion.24), kind=kOutput, calls=%fused_computation.10 | convolution fusion | flops 68353024 | bytes 8320 | tf_op jit(solution)/shard_map/dot_general | solution.py:41
  1.9 0.7 add_convert_fusion.1
  2.6 0.8 fusion.12
  3.4 0.2 convolution_convert_fusion.1
  3.6 0.1 slice.43
  3.7 0.1 slice.46
  3.8 0.1 slice.48
  3.8 0.0 copy-done.1
  3.8 2.2 %add_convert_fusion = bf16[1024,896]{1,0:T(8,128)(2,1)} fusion(f32[1024]{0:T(1024)S(1)} %slice.48, f32[1024]{0:T(1024)S(1)} %slice.46, pred[896]{0:T(1024)(128)(4,1)S(1)} %get-tuple-element.19, pred[896]{0:T(1024)(128)(4,1)S(1)} %get-tuple-element.20, s32[1024]{0:T(1024)S(1)} %slice.43, bf16[128,768]{1,0:T(8,128)(2,1)S(1)} %copy-done.1), kind=kOutput, calls=%fused_computation.2 | convolution fusion | flops 238682112 | bytes 2045696 | tf_op jit(solution)/shard_map/dot_general | solution.py:69
  6.0 6.3 %all-to-all-start = ((bf16[16,64,896]{2,1,0:T(8,128)(2,1)}), bf16[16,64,896]{2,1,0:T(8,128)(2,1)S(1)}, u32[]{:S(2)}, u32[]{:S(2)}) async-start(bf16[16,64,896]{2,1,0:T(8,128)(2,1)} %bitcast.18), calls=%async_computation | async-start | bytes 3670016 | tf_op jit(solution)/shard_map/all_to_all | solution.py:73
  12.3 0.1 slice.51
  12.4 1.8 %convolution_convert_fusion = bf16[1024,768]{1,0:T(8,128)(2,1)} fusion(bf16[128,768]{1,0:T(8,128)(2,1)S(1)} %copy-done.1, s32[1024]{0:T(1024)S(1)} %slice.51), kind=kOutput, calls=%fused_computation.3 | convolution fusion | flops 202244096 | bytes 1773568 | tf_op jit(solution)/shard_map/dot_general | solution.py:71
  14.2 22.2 %all-to-all-done = bf16[16,64,896]{2,1,0:T(8,128)(2,1)S(1)} async-done(((bf16[16,64,896]{2,1,0:T(8,128)(2,1)}), bf16[16,64,896]{2,1,0:T(8,128)(2,1)S(1)}, u32[]{:S(2)}, u32[]{:S(2)}) %all-to-all-start) | async-done | bytes 1835040 | tf_op jit(solution)/shard_map/all_to_all | solution.py:73
  36.3 3.7 %all-to-all-start.1 = ((bf16[16,64,768]{2,1,0:T(8,128)(2,1)}), bf16[16,64,768]{2,1,0:T(8,128)(2,1)S(1)}, u32[]{:S(2)}, u32[]{:S(2)}) async-start(bf16[16,64,768]{2,1,0:T(8,128)(2,1)} %bitcast.3), calls=%async_computation.1 | async-start | bytes 3145728 | tf_op jit(solution)/shard_map/all_to_all | solution.py:76
  40.1 0.4 add_reduce_fusion.1
  40.5 0.0 copy-start.2
  40.5 1.1 %fusion.1 = f32[96,768]{1,0:T(8,128)} fusion(bf16[1024,896]{1,0:T(8,128)(2,1)S(1)} %bitcast.17, s32[1024]{0:T(1024)S(1)} %get-tuple-element.4), kind=kOutput, calls=%fused_computation.4 | convolution fusion | flops 151093248 | bytes 1871872 | tf_op jit(solution)/shard_map/dot_general | solution.py:84
  41.6 2.6 %collective-permute-start = (f32[96,768]{1,0:T(8,128)}, f32[96,768]{1,0:T(8,128)S(1)}, u32[]{:S(2)}, u32[]{:S(2)}) collective-permute-start(f32[96,768]{1,0:T(8,128)} %fusion.1), channel_id=1, source_target_pairs={{0,4},{4,0},{1,5},{5,1},{2,6},{6,2},{3,7},{7,3},{8,12},{12,8},{9,1... | collective-permute-start | bytes 884744 | tf_op jit(solution)/shard_map/ppermute | solution.py:85
  44.2 22.5 %all-to-all-done.1 = bf16[16,64,768]{2,1,0:T(8,128)(2,1)S(1)} async-done(((bf16[16,64,768]{2,1,0:T(8,128)(2,1)}), bf16[16,64,768]{2,1,0:T(8,128)(2,1)S(1)}, u32[]{:S(2)}, u32[]{:S(2)}) %all-to-all-start.1) | async-done | bytes 1572896 | tf_op jit(solution)/shard_map/all_to_all | solution.py:76
  66.7 0.0 collective-permute-done
  66.7 0.5 multiply_reduce_fusion
  67.2 0.1 multiply_convert_fusion
  67.3 0.0 copy-done.2
  67.3 0.0 copy-start
  67.4 0.2 fusion.18
  67.6 17.6 %all_to_all.20 = f32[16,16,768]{2,1,0:T(8,128)S(1)} all-to-all(f32[16,16,768]{2,1,0:T(8,128)S(1)} %bitcast.15), channel_id=1, replica_groups=mesh['y'=2,'core'=2,'zh'=2,'zl'=2,'x'=2] {'y','core','x','zl'}, dimensions={0} | all-to-all | bytes 1572864 | tf_op jit(solution)/shard_map/all_to_all | solution.py:95
  85.3 0.4 collective-permute-start.1
  85.7 5.6 %collective-permute-done.1 = f32[16,768]{1,0:T(8,128)S(1)} collective-permute-done((f32[16,768]{1,0:T(8,128)S(1)}, f32[16,768]{1,0:T(8,128)S(1)}, u32[]{:S(2)}, u32[]{:S(2)}) %collective-permute-start.1) | collective-permute-done | bytes 49184 | tf_op jit(solution)/shard_map/ppermute | solution.py:99
  91.3 0.1 multiply_reduce_fusion.1
  91.4 0.1 multiply_convert_fusion.1
  91.5 10.5 %all_to_all.21 = bf16[16,16,768]{2,1,0:T(8,128)(2,1)S(1)} all-to-all(bf16[16,16,768]{2,1,0:T(8,128)(2,1)S(1)} %broadcast_in_dim.76), channel_id=1, replica_groups=mesh['y'=2,'core'=2,'zh'=2,'zl'=2,'x'=2] {'y','core','x','zl'}, dimensions={0} | all-to-all | bytes 786432 | tf_op jit(solution)/shard_map/all_to_all | solution.py:101
  102.1 0.0 copy-done
  102.1 0.9 fusion.4
  103.0 0.7 copy.10
  (10 shorter events, 0.2 us)
Async XLA Ops:
  0.6 3.2 %copy-start.1 = (bf16[128,768]{1,0:T(8,128)(2,1)S(1)}, bf16[128,768]{1,0:T(8,128)(2,1)}, u32[]{:S(2)}) copy-start(bf16[128,768]{1,0:T(8,128)(2,1)} %param.5) | copy-start | bytes 589828
  6.0 30.3 %all-to-all-start = ((bf16[16,64,896]{2,1,0:T(8,128)(2,1)}), bf16[16,64,896]{2,1,0:T(8,128)(2,1)S(1)}, u32[]{:S(2)}, u32[]{:S(2)}) async-start(bf16[16,64,896]{2,1,0:T(8,128)(2,1)} %bitcast.18), calls=%async_computation | async-start | bytes 3670016 | tf_op jit(solution)/shard_map/all_to_all | solution.py:73
  36.3 30.4 %all-to-all-start.1 = ((bf16[16,64,768]{2,1,0:T(8,128)(2,1)}), bf16[16,64,768]{2,1,0:T(8,128)(2,1)S(1)}, u32[]{:S(2)}, u32[]{:S(2)}) async-start(bf16[16,64,768]{2,1,0:T(8,128)(2,1)} %bitcast.3), calls=%async_computation.1 | async-start | bytes 3145728 | tf_op jit(solution)/shard_map/all_to_all | solution.py:76
  40.5 26.8 %copy-start.2 = (s32[96]{0:T(128)S(1)}, s32[96]{0:T(128)}, u32[]{:S(2)}) copy-start(s32[96]{0:T(128)} %param.9) | copy-start | bytes 1156
  41.6 25.1 %collective-permute-start = (f32[96,768]{1,0:T(8,128)}, f32[96,768]{1,0:T(8,128)S(1)}, u32[]{:S(2)}, u32[]{:S(2)}) collective-permute-start(f32[96,768]{1,0:T(8,128)} %fusion.1), channel_id=1, source_target_pairs={{0,4},{4,0},{1,5},{5,1},{2,6},{6,2},{3,7},{7,3},{8,12},{12,8},{9,1... | collective-permute-start | bytes 884744 | tf_op jit(solution)/shard_map/ppermute | solution.py:85
  67.3 34.7 %copy-start = (bf16[96,768]{1,0:T(8,128)(2,1)}, bf16[96,768]{1,0:T(8,128)(2,1)S(1)}, u32[]{:S(2)}) copy-start(bf16[96,768]{1,0:T(8,128)(2,1)S(1)} %multiply_convert_fusion) | copy-start | bytes 442372
  85.3 6.0 %collective-permute-start.1 = (f32[16,768]{1,0:T(8,128)S(1)}, f32[16,768]{1,0:T(8,128)S(1)}, u32[]{:S(2)}, u32[]{:S(2)}) collective-permute-start(f32[16,768]{1,0:T(8,128)S(1)} %reduce_sum.38), channel_id=1, source_target_pairs={{0,4},{4,0},{1,5},{5,1},{2,6},{6,2},{3,7},{7,3},{8,12},{12,8},{9,1... | collective-permute-start | bytes 147464 | tf_op jit(solution)/shard_map/ppermute | solution.py:99

commit v23 on v17

--- a/solution.py
+++ b/solution.py
@@ -91,15 +91,16 @@
 
     if CLUSTERS % group == 0:
         share = CLUSTERS // group
+        spread_c = ("y", "zl", "x", "core")
         parts = lax.all_to_all(
-            partial_sums.reshape(group, share, width), near, split_axis=0, concat_axis=0, tiled=True
+            partial_sums.reshape(group, share, width), spread_c, split_axis=0, concat_axis=0, tiled=True
         )
         half_sums = jnp.sum(parts, axis=0)
         sums = half_sums + lax.ppermute(half_sums, "zh", [(0, 1), (1, 0)])
         own = rms_scale(sums).astype(bf16)
         centroids = lax.all_to_all(
             jnp.broadcast_to(own[None], (group, share, width)),
-            near,
+            spread_c,
             split_axis=0,
             concat_axis=0,
             tiled=True,

time: 104 us -> 105 us (level)
  blocking collectives: 28.1 us -> 30.4 us
    all_to_all x2, blocking collectives: 28.1 us -> 30.4 us  [the longest x1 18.7 us: local(): lax.all_to_all(partial_sums.reshape(group, share, width), spread_c, split...]
where the time goes in v23:
time: 105 us
  waiting for transfers between devices  49.3 us (47%)
  blocking collectives  30.4 us (29%)
  starting transfers between devices  13 us (12%)
  matrix products  8.79 us (8%)
  other arithmetic  1.67 us (2%)
  local copies, waits for them, and re-layouts  1.08 us (1%)
    all_to_all x1, waiting for transfers between devices, local(): lax.all_to_all(send_second.reshape(group, capacity, width), near, split_a...  22.5 us
    all_to_all x1, waiting for transfers between devices, local(): lax.all_to_all(send_first.reshape(group, capacity, wide), near, split_axi...  22.2 us
    all_to_all x1, blocking collectives, local(): lax.all_to_all(partial_sums.reshape(group, share, width), spread_c, split...  18.7 us
    all_to_all x1, blocking collectives, local(): lax.all_to_all(jnp.broadcast_to(own[None], (group, share, width)), spread...  11.7 us
    all_to_all x1, starting transfers between devices, local(): lax.all_to_all(send_first.reshape(group, capacity, wide), near, split_axi...  6.31 us
    ppermute x1, waiting for transfers between devices, local(): sums = half_sums + lax.ppermute(half_sums, 'zh', [(0, 1), (1, 0)])  4.62 us
    all_to_all x1, starting transfers between devices, local(): lax.all_to_all(send_second.reshape(group, capacity, width), near, split_a...  3.71 us
    ppermute x1, starting transfers between devices, local(): mirrored = lax.ppermute(mirror_part, 'zh', [(0, 1), (1, 0)])  2.59 us
  transfers between devices with their start and end apart: 4, of which 3 were waited for; matrix products, arithmetic and copies ran while one was open for 3% of the time, Pallas kernels for 0%

profile of v23, /device:TPU:0, one launch (start us, length us, event | category | flops | bytes accessed | tf_op | source)
XLA Modules:
  0.0 105.1 jit_solution(3112423886823331666)
XLA Ops:
  0.6 0.0 copy-start.1
  0.7 1.2 %fusion.5 = f32[1024]{0:T(1024)S(1)} fusion(s32[1024]{0:T(1024)} %bitcast.19, s32[32]{0:T(128)S(1)} %fusion.24), kind=kOutput, calls=%fused_computation.10 | convolution fusion | flops 68353024 | bytes 8320 | tf_op jit(solution)/shard_map/dot_general | solution.py:41
  1.9 0.7 add_convert_fusion.1
  2.7 0.9 convolution_convert_fusion.1
  3.6 0.1 slice_add_fusion
  3.7 0.1 slice.43
  3.7 0.1 slice.46
  3.8 0.1 slice.48
  3.9 0.0 copy-done.1
  3.9 2.2 %add_convert_fusion = bf16[1024,896]{1,0:T(8,128)(2,1)} fusion(f32[1024]{0:T(1024)S(1)} %slice.48, f32[1024]{0:T(1024)S(1)} %slice.46, pred[896]{0:T(1024)(128)(4,1)S(1)} %get-tuple-element.19, pred[896]{0:T(1024)(128)(4,1)S(1)} %get-tuple-element.20, s32[1024]{0:T(1024)S(1)} %slice.43, bf16[128,768]{1,0:T(8,128)(2,1)S(1)} %copy-done.1), kind=kOutput, calls=%fused_computation.2 | convolution fusion | flops 238682112 | bytes 2045696 | tf_op jit(solution)/shard_map/dot_general | solution.py:68
  6.1 6.3 %all-to-all-start = ((bf16[16,64,896]{2,1,0:T(8,128)(2,1)}), bf16[16,64,896]{2,1,0:T(8,128)(2,1)S(1)}, u32[]{:S(2)}, u32[]{:S(2)}) async-start(bf16[16,64,896]{2,1,0:T(8,128)(2,1)} %bitcast.18), calls=%async_computation | async-start | bytes 3670016 | tf_op jit(solution)/shard_map/all_to_all | solution.py:72
  12.4 0.1 slice.51
  12.4 1.8 %convolution_convert_fusion = bf16[1024,768]{1,0:T(8,128)(2,1)} fusion(bf16[128,768]{1,0:T(8,128)(2,1)S(1)} %copy-done.1, s32[1024]{0:T(1024)S(1)} %slice.51), kind=kOutput, calls=%fused_computation.3 | convolution fusion | flops 202244096 | bytes 1773568 | tf_op jit(solution)/shard_map/dot_general | solution.py:70
  14.2 22.2 %all-to-all-done = bf16[16,64,896]{2,1,0:T(8,128)(2,1)S(1)} async-done(((bf16[16,64,896]{2,1,0:T(8,128)(2,1)}), bf16[16,64,896]{2,1,0:T(8,128)(2,1)S(1)}, u32[]{:S(2)}, u32[]{:S(2)}) %all-to-all-start) | async-done | bytes 1835040 | tf_op jit(solution)/shard_map/all_to_all | solution.py:72
  36.4 3.7 %all-to-all-start.1 = ((bf16[16,64,768]{2,1,0:T(8,128)(2,1)}), bf16[16,64,768]{2,1,0:T(8,128)(2,1)S(1)}, u32[]{:S(2)}, u32[]{:S(2)}) async-start(bf16[16,64,768]{2,1,0:T(8,128)(2,1)} %bitcast.3), calls=%async_computation.1 | async-start | bytes 3145728 | tf_op jit(solution)/shard_map/all_to_all | solution.py:75
  40.1 0.4 add_reduce_fusion.1
  40.6 0.0 copy-start.2
  40.6 1.1 %fusion.1 = f32[96,768]{1,0:T(8,128)} fusion(bf16[1024,896]{1,0:T(8,128)(2,1)S(1)} %bitcast.17, s32[1024]{0:T(1024)S(1)} %get-tuple-element.4), kind=kOutput, calls=%fused_computation.4 | convolution fusion | flops 151093248 | bytes 1871872 | tf_op jit(solution)/shard_map/dot_general | solution.py:83
  41.7 2.6 %collective-permute-start = (f32[96,768]{1,0:T(8,128)}, f32[96,768]{1,0:T(8,128)S(1)}, u32[]{:S(2)}, u32[]{:S(2)}) collective-permute-start(f32[96,768]{1,0:T(8,128)} %fusion.1), channel_id=1, source_target_pairs={{0,4},{4,0},{1,5},{5,1},{2,6},{6,2},{3,7},{7,3},{8,12},{12,8},{9,1... | collective-permute-start | bytes 884744 | tf_op jit(solution)/shard_map/ppermute | solution.py:84
  44.3 22.5 %all-to-all-done.1 = bf16[16,64,768]{2,1,0:T(8,128)(2,1)S(1)} async-done(((bf16[16,64,768]{2,1,0:T(8,128)(2,1)}), bf16[16,64,768]{2,1,0:T(8,128)(2,1)S(1)}, u32[]{:S(2)}, u32[]{:S(2)}) %all-to-all-start.1) | async-done | bytes 1572896 | tf_op jit(solution)/shard_map/all_to_all | solution.py:75
  66.8 0.0 collective-permute-done
  66.8 0.5 multiply_reduce_fusion
  67.3 0.1 multiply_convert_fusion
  67.4 0.0 copy-done.2
  67.4 0.0 copy-start
  67.4 0.2 fusion.16
  67.7 18.7 %all_to_all.20 = f32[16,16,768]{2,1,0:T(8,128)S(1)} all-to-all(f32[16,16,768]{2,1,0:T(8,128)S(1)} %bitcast.15), channel_id=1, replica_groups=mesh['y'=2,'core'=2,'zh'=2,'zl'=2,'x'=2] {'y','zl','x','core'}, dimensions={0} | all-to-all | bytes 1572864 | tf_op jit(solution)/shard_map/all_to_all | solution.py:95
  86.4 0.4 collective-permute-start.1
  86.8 4.6 %collective-permute-done.1 = f32[16,768]{1,0:T(8,128)S(1)} collective-permute-done((f32[16,768]{1,0:T(8,128)S(1)}, f32[16,768]{1,0:T(8,128)S(1)}, u32[]{:S(2)}, u32[]{:S(2)}) %collective-permute-start.1) | collective-permute-done | bytes 49184 | tf_op jit(solution)/shard_map/ppermute | solution.py:99
  91.4 0.1 multiply_reduce_fusion.1
  91.6 0.1 multiply_convert_fusion.1
  91.7 11.7 %all_to_all.21 = bf16[16,16,768]{2,1,0:T(8,128)(2,1)S(1)} all-to-all(bf16[16,16,768]{2,1,0:T(8,128)(2,1)S(1)} %broadcast_in_dim.76), channel_id=1, replica_groups=mesh['y'=2,'core'=2,'zh'=2,'zl'=2,'x'=2] {'y','zl','x','core'}, dimensions={0} | all-to-all | bytes 786432 | tf_op jit(solution)/shard_map/all_to_all | solution.py:101
  103.4 0.0 copy-done
  103.4 0.9 fusion.4
  104.3 0.7 copy.10
  (10 shorter events, 0.2 us)
Async XLA Ops:
  0.6 3.3 %copy-start.1 = (bf16[128,768]{1,0:T(8,128)(2,1)S(1)}, bf16[128,768]{1,0:T(8,128)(2,1)}, u32[]{:S(2)}) copy-start(bf16[128,768]{1,0:T(8,128)(2,1)} %param.5) | copy-start | bytes 589828
  6.1 30.3 %all-to-all-start = ((bf16[16,64,896]{2,1,0:T(8,128)(2,1)}), bf16[16,64,896]{2,1,0:T(8,128)(2,1)S(1)}, u32[]{:S(2)}, u32[]{:S(2)}) async-start(bf16[16,64,896]{2,1,0:T(8,128)(2,1)} %bitcast.18), calls=%async_computation | async-start | bytes 3670016 | tf_op jit(solution)/shard_map/all_to_all | solution.py:72
  36.4 30.4 %all-to-all-start.1 = ((bf16[16,64,768]{2,1,0:T(8,128)(2,1)}), bf16[16,64,768]{2,1,0:T(8,128)(2,1)S(1)}, u32[]{:S(2)}, u32[]{:S(2)}) async-start(bf16[16,64,768]{2,1,0:T(8,128)(2,1)} %bitcast.3), calls=%async_computation.1 | async-start | bytes 3145728 | tf_op jit(solution)/shard_map/all_to_all | solution.py:75
  40.6 26.8 %copy-start.2 = (s32[96]{0:T(128)S(1)}, s32[96]{0:T(128)}, u32[]{:S(2)}) copy-start(s32[96]{0:T(128)} %param.9) | copy-start | bytes 1156
  41.7 25.1 %collective-permute-start = (f32[96,768]{1,0:T(8,128)}, f32[96,768]{1,0:T(8,128)S(1)}, u32[]{:S(2)}, u32[]{:S(2)}) collective-permute-start(f32[96,768]{1,0:T(8,128)} %fusion.1), channel_id=1, source_target_pairs={{0,4},{4,0},{1,5},{5,1},{2,6},{6,2},{3,7},{7,3},{8,12},{12,8},{9,1... | collective-permute-start | bytes 884744 | tf_op jit(solution)/shard_map/ppermute | solution.py:84
  67.4 36.0 %copy-start = (bf16[96,768]{1,0:T(8,128)(2,1)}, bf16[96,768]{1,0:T(8,128)(2,1)S(1)}, u32[]{:S(2)}) copy-start(bf16[96,768]{1,0:T(8,128)(2,1)S(1)} %multiply_convert_fusion) | copy-start | bytes 442372
  86.4 5.1 %collective-permute-start.1 = (f32[16,768]{1,0:T(8,128)S(1)}, f32[16,768]{1,0:T(8,128)S(1)}, u32[]{:S(2)}, u32[]{:S(2)}) collective-permute-start(f32[16,768]{1,0:T(8,128)S(1)} %reduce_sum.38), channel_id=1, source_target_pairs={{0,4},{4,0},{1,5},{5,1},{2,6},{6,2},{3,7},{7,3},{8,12},{12,8},{9,1... | collective-permute-start | bytes 147464 | tf_op jit(solution)/shard_map/ppermute | solution.py:99

commit v24 on v17

--- a/solution.py
+++ b/solution.py
@@ -61,13 +61,14 @@
     doc_part = (first_doc[:, None] == jnp.arange(docs, dtype=jnp.int32)[None, :]).astype(bf16)
     table = jnp.concatenate([doc_embed, jnp.zeros((docs, lanes), bf16)], axis=1)
     lane = jnp.arange(wide, dtype=jnp.int32)[None, :]
-    slot_pair = slot_plus.astype(f32).reshape(2, group * capacity)
+    slot_pair = slot_plus.astype(bf16).reshape(2, group * capacity)
+    zero = jnp.zeros((), bf16)
     slot_lanes = jnp.where(
-        lane == width, slot_pair[0][:, None], jnp.where(lane == width + 1, slot_pair[1][:, None], 0.0)
+        lane == width, slot_pair[0][:, None], jnp.where(lane == width + 1, slot_pair[1][:, None], zero)
     )
-    send_first = (jnp.dot(doc_part, table, preferred_element_type=f32) + slot_lanes).astype(bf16)
+    send_first = jnp.dot(doc_part, table, preferred_element_type=bf16) + slot_lanes
     pick = (second_doc[:, None] == jnp.arange(docs, dtype=jnp.int32)[None, :]).astype(bf16)
-    send_second = jnp.dot(pick, doc_embed, preferred_element_type=f32).astype(bf16)
+    send_second = jnp.dot(pick, doc_embed, preferred_element_type=bf16)
 
     got_first = lax.all_to_all(
         send_first.reshape(group, capacity, wide), near, split_axis=0, concat_axis=0, tiled=True

time: 104 us -> 105 us (level)
  no operation moved by 1% of the time
where the time goes in v24:
time: 105 us; the launch traced here: 104 us
  waiting for transfers between devices  50.3 us (48%)
  blocking collectives  28.1 us (27%)
  starting transfers between devices  13 us (12%)
  matrix products  9.12 us (9%)
  other arithmetic  1.6 us (2%)
  local copies, waits for them, and re-layouts  1.18 us (1%)
    all_to_all x1, waiting for transfers between devices, local(): lax.all_to_all(send_second.reshape(group, capacity, width), near, split_a...  22.5 us
    all_to_all x1, waiting for transfers between devices, local(): lax.all_to_all(send_first.reshape(group, capacity, wide), near, split_axi...  22.2 us
    all_to_all x1, blocking collectives, local(): lax.all_to_all(partial_sums.reshape(group, share, width), near, split_axi...  17.6 us
    all_to_all x1, blocking collectives, local(): lax.all_to_all(jnp.broadcast_to(own[None], (group, share, width)), near,...  10.5 us
    all_to_all x1, starting transfers between devices, local(): lax.all_to_all(send_first.reshape(group, capacity, wide), near, split_axi...  6.31 us
    ppermute x1, waiting for transfers between devices, local(): sums = half_sums + lax.ppermute(half_sums, 'zh', [(0, 1), (1, 0)])  5.6 us
    all_to_all x1, starting transfers between devices, local(): lax.all_to_all(send_second.reshape(group, capacity, width), near, split_a...  3.71 us
    ppermute x1, starting transfers between devices, local(): mirrored = lax.ppermute(mirror_part, 'zh', [(0, 1), (1, 0)])  2.59 us
  transfers between devices with their start and end apart: 4, of which 3 were waited for; matrix products, arithmetic and copies ran while one was open for 3% of the time, Pallas kernels for 0%

profile of v24, /device:TPU:0, one launch (start us, length us, event | category | flops | bytes accessed | tf_op | source)
XLA Modules:
  0.0 104.1 jit_solution(12569539965376465391)
XLA Ops:
  0.6 0.0 copy-start.1
  0.7 1.2 %fusion.5 = f32[1024]{0:T(1024)S(1)} fusion(s32[1024]{0:T(1024)} %bitcast.19, s32[32]{0:T(128)S(1)} %fusion.25), kind=kOutput, calls=%fused_computation.9 | convolution fusion | flops 68353024 | bytes 8320 | tf_op jit(solution)/shard_map/dot_general | solution.py:41
  1.9 0.7 add_convert_fusion
  2.7 0.9 fusion.35
  3.6 0.1 slice.44
  3.7 0.1 fusion.34
  3.8 0.1 slice.46
  3.8 0.1 slice.48
  3.9 0.0 copy-done.1
  3.9 2.5 %select_add_fusion = bf16[1024,896]{1,0:T(8,128)(2,1)} fusion(pred[896]{0:T(1024)(128)(4,1)S(1)} %get-tuple-element.19, pred[896]{0:T(1024)(128)(4,1)S(1)} %get-tuple-element.20, bf16[1024]{0:T(1024)(128)(2,1)S(1)} %slice.48, bf16[1024]{0:T(1024)(128)(2,1)S(1)} %slice.46, s32[1024]{0:T(1024)S(1)} %slice.44, bf16[128,768]{1,0:T(8,128)(2,1)S(1)} %copy-done.1), kind=kOutput, calls=%fused_computation.2 | convolution fusion | flops 237764608 | bytes 2041600 | tf_op jit(solution)/shard_map/dot_general | solution.py:69
  6.4 6.3 %all-to-all-start = ((bf16[16,64,896]{2,1,0:T(8,128)(2,1)}), bf16[16,64,896]{2,1,0:T(8,128)(2,1)S(1)}, u32[]{:S(2)}, u32[]{:S(2)}) async-start(bf16[16,64,896]{2,1,0:T(8,128)(2,1)} %bitcast.18), calls=%async_computation | async-start | bytes 3670016 | tf_op jit(solution)/shard_map/all_to_all | solution.py:73
  12.7 0.1 slice.51
  12.8 1.8 %fusion.6 = bf16[1024,768]{1,0:T(8,128)(2,1)} fusion(bf16[128,768]{1,0:T(8,128)(2,1)S(1)} %copy-done.1, s32[1024]{0:T(1024)S(1)} %slice.51), kind=kOutput, calls=%fused_computation.15 | convolution fusion | flops 201457664 | bytes 1773568 | tf_op jit(solution)/shard_map/dot_general | solution.py:71
  14.6 22.2 %all-to-all-done = bf16[16,64,896]{2,1,0:T(8,128)(2,1)S(1)} async-done(((bf16[16,64,896]{2,1,0:T(8,128)(2,1)}), bf16[16,64,896]{2,1,0:T(8,128)(2,1)S(1)}, u32[]{:S(2)}, u32[]{:S(2)}) %all-to-all-start) | async-done | bytes 1835040 | tf_op jit(solution)/shard_map/all_to_all | solution.py:73
  36.8 3.7 %all-to-all-start.1 = ((bf16[16,64,768]{2,1,0:T(8,128)(2,1)}), bf16[16,64,768]{2,1,0:T(8,128)(2,1)S(1)}, u32[]{:S(2)}, u32[]{:S(2)}) async-start(bf16[16,64,768]{2,1,0:T(8,128)(2,1)} %bitcast.3), calls=%async_computation.1 | async-start | bytes 3145728 | tf_op jit(solution)/shard_map/all_to_all | solution.py:76
  40.5 0.4 add_reduce_fusion.1
  40.9 0.0 copy-start.2
  40.9 1.1 %fusion.1 = f32[96,768]{1,0:T(8,128)} fusion(bf16[1024,896]{1,0:T(8,128)(2,1)S(1)} %bitcast.17, s32[1024]{0:T(1024)S(1)} %get-tuple-element.4), kind=kOutput, calls=%fused_computation.3 | convolution fusion | flops 151093248 | bytes 1871872 | tf_op jit(solution)/shard_map/dot_general | solution.py:84
  42.0 2.6 %collective-permute-start = (f32[96,768]{1,0:T(8,128)}, f32[96,768]{1,0:T(8,128)S(1)}, u32[]{:S(2)}, u32[]{:S(2)}) collective-permute-start(f32[96,768]{1,0:T(8,128)} %fusion.1), channel_id=1, source_target_pairs={{0,4},{4,0},{1,5},{5,1},{2,6},{6,2},{3,7},{7,3},{8,12},{12,8},{9,1... | collective-permute-start | bytes 884744 | tf_op jit(solution)/shard_map/ppermute | solution.py:85
  44.6 22.5 %all-to-all-done.1 = bf16[16,64,768]{2,1,0:T(8,128)(2,1)S(1)} async-done(((bf16[16,64,768]{2,1,0:T(8,128)(2,1)}), bf16[16,64,768]{2,1,0:T(8,128)(2,1)S(1)}, u32[]{:S(2)}, u32[]{:S(2)}) %all-to-all-start.1) | async-done | bytes 1572896 | tf_op jit(solution)/shard_map/all_to_all | solution.py:76
  67.2 0.0 collective-permute-done
  67.2 0.5 multiply_reduce_fusion
  67.7 0.1 multiply_convert_fusion
  67.8 0.0 copy-done.2
  67.8 0.0 copy-start
  67.8 0.2 fusion.17
  68.0 17.6 %all_to_all.20 = f32[16,16,768]{2,1,0:T(8,128)S(1)} all-to-all(f32[16,16,768]{2,1,0:T(8,128)S(1)} %bitcast.15), channel_id=1, replica_groups=mesh['y'=2,'core'=2,'zh'=2,'zl'=2,'x'=2] {'y','core','x','zl'}, dimensions={0} | all-to-all | bytes 1572864 | tf_op jit(solution)/shard_map/all_to_all | solution.py:95
  85.7 0.4 collective-permute-start.1
  86.1 5.6 %collective-permute-done.1 = f32[16,768]{1,0:T(8,128)S(1)} collective-permute-done((f32[16,768]{1,0:T(8,128)S(1)}, f32[16,768]{1,0:T(8,128)S(1)}, u32[]{:S(2)}, u32[]{:S(2)}) %collective-permute-start.1) | collective-permute-done | bytes 49184 | tf_op jit(solution)/shard_map/ppermute | solution.py:99
  91.7 0.1 multiply_reduce_fusion.1
  91.9 0.1 multiply_convert_fusion.1
  92.0 10.5 %all_to_all.21 = bf16[16,16,768]{2,1,0:T(8,128)(2,1)S(1)} all-to-all(bf16[16,16,768]{2,1,0:T(8,128)(2,1)S(1)} %broadcast_in_dim.76), channel_id=1, replica_groups=mesh['y'=2,'core'=2,'zh'=2,'zl'=2,'x'=2] {'y','core','x','zl'}, dimensions={0} | all-to-all | bytes 786432 | tf_op jit(solution)/shard_map/all_to_all | solution.py:101
  102.5 0.0 copy-done
  102.5 0.9 fusion.4
  103.4 0.7 copy.10
  (10 shorter events, 0.2 us)
Async XLA Ops:
  0.6 3.3 %copy-start.1 = (bf16[128,768]{1,0:T(8,128)(2,1)S(1)}, bf16[128,768]{1,0:T(8,128)(2,1)}, u32[]{:S(2)}) copy-start(bf16[128,768]{1,0:T(8,128)(2,1)} %param.5) | copy-start | bytes 589828
  6.4 30.3 %all-to-all-start = ((bf16[16,64,896]{2,1,0:T(8,128)(2,1)}), bf16[16,64,896]{2,1,0:T(8,128)(2,1)S(1)}, u32[]{:S(2)}, u32[]{:S(2)}) async-start(bf16[16,64,896]{2,1,0:T(8,128)(2,1)} %bitcast.18), calls=%async_computation | async-start | bytes 3670016 | tf_op jit(solution)/shard_map/all_to_all | solution.py:73
  36.8 30.4 %all-to-all-start.1 = ((bf16[16,64,768]{2,1,0:T(8,128)(2,1)}), bf16[16,64,768]{2,1,0:T(8,128)(2,1)S(1)}, u32[]{:S(2)}, u32[]{:S(2)}) async-start(bf16[16,64,768]{2,1,0:T(8,128)(2,1)} %bitcast.3), calls=%async_computation.1 | async-start | bytes 3145728 | tf_op jit(solution)/shard_map/all_to_all | solution.py:76
  40.9 26.8 %copy-start.2 = (s32[96]{0:T(128)S(1)}, s32[96]{0:T(128)}, u32[]{:S(2)}) copy-start(s32[96]{0:T(128)} %param.9) | copy-start | bytes 1156
  42.0 25.1 %collective-permute-start = (f32[96,768]{1,0:T(8,128)}, f32[96,768]{1,0:T(8,128)S(1)}, u32[]{:S(2)}, u32[]{:S(2)}) collective-permute-start(f32[96,768]{1,0:T(8,128)} %fusion.1), channel_id=1, source_target_pairs={{0,4},{4,0},{1,5},{5,1},{2,6},{6,2},{3,7},{7,3},{8,12},{12,8},{9,1... | collective-permute-start | bytes 884744 | tf_op jit(solution)/shard_map/ppermute | solution.py:85
  67.8 34.7 %copy-start = (bf16[96,768]{1,0:T(8,128)(2,1)}, bf16[96,768]{1,0:T(8,128)(2,1)S(1)}, u32[]{:S(2)}) copy-start(bf16[96,768]{1,0:T(8,128)(2,1)S(1)} %multiply_convert_fusion) | copy-start | bytes 442372
  85.7 6.0 %collective-permute-start.1 = (f32[16,768]{1,0:T(8,128)S(1)}, f32[16,768]{1,0:T(8,128)S(1)}, u32[]{:S(2)}, u32[]{:S(2)}) collective-permute-start(f32[16,768]{1,0:T(8,128)S(1)} %reduce_sum.38), channel_id=1, source_target_pairs={{0,4},{4,0},{1,5},{5,1},{2,6},{6,2},{3,7},{7,3},{8,12},{12,8},{9,1... | collective-permute-start | bytes 147464 | tf_op jit(solution)/shard_map/ppermute | solution.py:99

commit v25 on v22

--- a/solution.py
+++ b/solution.py
@@ -62,13 +62,14 @@
     doc_part = (first_doc[:, None] == jnp.arange(docs, dtype=jnp.int32)[None, :]).astype(bf16)
     table = jnp.concatenate([doc_embed, jnp.zeros((docs, lanes), bf16)], axis=1)
     lane = jnp.arange(wide, dtype=jnp.int32)[None, :]
-    slot_pair = slot_plus.astype(f32).reshape(2, group * capacity)
+    slot_pair = slot_plus.astype(bf16).reshape(2, group * capacity)
+    zero = jnp.zeros((), bf16)
     slot_lanes = jnp.where(
-        lane == width, slot_pair[0][:, None], jnp.where(lane == width + 1, slot_pair[1][:, None], 0.0)
+        lane == width, slot_pair[0][:, None], jnp.where(lane == width + 1, slot_pair[1][:, None], zero)
     )
-    send_first = (jnp.dot(doc_part, table, preferred_element_type=f32) + slot_lanes).astype(bf16)
+    send_first = jnp.dot(doc_part, table, preferred_element_type=bf16) + slot_lanes
     pick = (second_doc[:, None] == jnp.arange(docs, dtype=jnp.int32)[None, :]).astype(bf16)
-    send_second = jnp.dot(pick, doc_embed, preferred_element_type=f32).astype(bf16)
+    send_second = jnp.dot(pick, doc_embed, preferred_element_type=bf16)
 
     got_first = lax.all_to_all(
         send_first.reshape(group, capacity, wide), near, split_axis=0, concat_axis=0, tiled=True

time: 104 us -> 104 us (level)
  no operation moved by 1% of the time
where the time goes in v25:
time: 104 us
  waiting for transfers between devices  50.3 us (48%)
  blocking collectives  28.1 us (27%)
  starting transfers between devices  13 us (12%)
  matrix products  8.4 us (8%)
  other arithmetic  2.33 us (2%)
  local copies, waits for them, and re-layouts  1.11 us (1%)
    all_to_all x1, waiting for transfers between devices, local(): lax.all_to_all(send_second.reshape(group, capacity, width), near, split_a...  22.5 us
    all_to_all x1, waiting for transfers between devices, local(): lax.all_to_all(send_first.reshape(group, capacity, wide), near, split_axi...  22.2 us
    all_to_all x1, blocking collectives, local(): lax.all_to_all(partial_sums.reshape(group, share, width), near, split_axi...  17.6 us
    all_to_all x1, blocking collectives, local(): lax.all_to_all(jnp.broadcast_to(own[None], (group, share, width)), near,...  10.5 us
    all_to_all x1, starting transfers between devices, local(): lax.all_to_all(send_first.reshape(group, capacity, wide), near, split_axi...  6.32 us
    ppermute x1, waiting for transfers between devices, local(): sums = half_sums + lax.ppermute(half_sums, 'zh', [(0, 1), (1, 0)])  5.6 us
    all_to_all x1, starting transfers between devices, local(): lax.all_to_all(send_second.reshape(group, capacity, width), near, split_a...  3.71 us
    ppermute x1, starting transfers between devices, local(): mirrored = lax.ppermute(mirror_part, 'zh', [(0, 1), (1, 0)])  2.59 us
  transfers between devices with their start and end apart: 4, of which 3 were waited for; matrix products, arithmetic and copies ran while one was open for 3% of the time, Pallas kernels for 0%

profile of v25, /device:TPU:0, one launch (start us, length us, event | category | flops | bytes accessed | tf_op | source)
XLA Modules:
  0.0 104.1 jit_solution(10302395932114330939)
XLA Ops:
  0.6 0.0 copy-start.1
  0.7 1.2 %fusion.5 = f32[1024]{0:T(1024)S(1)} fusion(s32[1024]{0:T(1024)} %bitcast.19, s32[32]{0:T(128)S(1)} %fusion.25), kind=kOutput, calls=%fused_computation.9 | convolution fusion | flops 68353024 | bytes 8320 | tf_op jit(solution)/shard_map/dot_general | solution.py:41
  1.9 0.7 add_convert_fusion
  2.6 0.8 fusion.13
  3.4 0.2 fusion.35
  3.6 0.1 slice.44
  3.7 0.1 slice.46
  3.8 0.1 slice.48
  3.9 0.0 copy-done.1
  3.9 2.5 %select_add_fusion = bf16[1024,896]{1,0:T(8,128)(2,1)} fusion(pred[896]{0:T(1024)(128)(4,1)S(1)} %get-tuple-element.19, pred[896]{0:T(1024)(128)(4,1)S(1)} %get-tuple-element.20, bf16[1024]{0:T(1024)(128)(2,1)S(1)} %slice.48, bf16[1024]{0:T(1024)(128)(2,1)S(1)} %slice.46, s32[1024]{0:T(1024)S(1)} %slice.44, bf16[128,768]{1,0:T(8,128)(2,1)S(1)} %copy-done.1), kind=kOutput, calls=%fused_computation.2 | convolution fusion | flops 237764608 | bytes 2041600 | tf_op jit(solution)/shard_map/dot_general | solution.py:70
  6.4 6.3 %all-to-all-start = ((bf16[16,64,896]{2,1,0:T(8,128)(2,1)}), bf16[16,64,896]{2,1,0:T(8,128)(2,1)S(1)}, u32[]{:S(2)}, u32[]{:S(2)}) async-start(bf16[16,64,896]{2,1,0:T(8,128)(2,1)} %bitcast.18), calls=%async_computation | async-start | bytes 3670016 | tf_op jit(solution)/shard_map/all_to_all | solution.py:74
  12.7 0.1 slice.51
  12.8 1.8 %fusion.6 = bf16[1024,768]{1,0:T(8,128)(2,1)} fusion(bf16[128,768]{1,0:T(8,128)(2,1)S(1)} %copy-done.1, s32[1024]{0:T(1024)S(1)} %slice.51), kind=kOutput, calls=%fused_computation.15 | convolution fusion | flops 201457664 | bytes 1773568 | tf_op jit(solution)/shard_map/dot_general | solution.py:72
  14.5 22.2 %all-to-all-done = bf16[16,64,896]{2,1,0:T(8,128)(2,1)S(1)} async-done(((bf16[16,64,896]{2,1,0:T(8,128)(2,1)}), bf16[16,64,896]{2,1,0:T(8,128)(2,1)S(1)}, u32[]{:S(2)}, u32[]{:S(2)}) %all-to-all-start) | async-done | bytes 1835040 | tf_op jit(solution)/shard_map/all_to_all | solution.py:74
  36.7 3.7 %all-to-all-start.1 = ((bf16[16,64,768]{2,1,0:T(8,128)(2,1)}), bf16[16,64,768]{2,1,0:T(8,128)(2,1)S(1)}, u32[]{:S(2)}, u32[]{:S(2)}) async-start(bf16[16,64,768]{2,1,0:T(8,128)(2,1)} %bitcast.3), calls=%async_computation.1 | async-start | bytes 3145728 | tf_op jit(solution)/shard_map/all_to_all | solution.py:77
  40.4 0.4 add_reduce_fusion.1
  40.9 0.0 copy-start.2
  40.9 1.1 %fusion.1 = f32[96,768]{1,0:T(8,128)} fusion(bf16[1024,896]{1,0:T(8,128)(2,1)S(1)} %bitcast.17, s32[1024]{0:T(1024)S(1)} %get-tuple-element.4), kind=kOutput, calls=%fused_computation.3 | convolution fusion | flops 151093248 | bytes 1871872 | tf_op jit(solution)/shard_map/dot_general | solution.py:85
  42.0 2.6 %collective-permute-start = (f32[96,768]{1,0:T(8,128)}, f32[96,768]{1,0:T(8,128)S(1)}, u32[]{:S(2)}, u32[]{:S(2)}) collective-permute-start(f32[96,768]{1,0:T(8,128)} %fusion.1), channel_id=1, source_target_pairs={{0,4},{4,0},{1,5},{5,1},{2,6},{6,2},{3,7},{7,3},{8,12},{12,8},{9,1... | collective-permute-start | bytes 884744 | tf_op jit(solution)/shard_map/ppermute | solution.py:86
  44.6 22.5 %all-to-all-done.1 = bf16[16,64,768]{2,1,0:T(8,128)(2,1)S(1)} async-done(((bf16[16,64,768]{2,1,0:T(8,128)(2,1)}), bf16[16,64,768]{2,1,0:T(8,128)(2,1)S(1)}, u32[]{:S(2)}, u32[]{:S(2)}) %all-to-all-start.1) | async-done | bytes 1572896 | tf_op jit(solution)/shard_map/all_to_all | solution.py:77
  67.1 0.0 collective-permute-done
  67.1 0.5 multiply_reduce_fusion
  67.6 0.1 multiply_convert_fusion
  67.7 0.0 copy-done.2
  67.7 0.0 copy-start
  67.7 0.2 fusion.19
  68.0 17.6 %all_to_all.20 = f32[16,16,768]{2,1,0:T(8,128)S(1)} all-to-all(f32[16,16,768]{2,1,0:T(8,128)S(1)} %bitcast.15), channel_id=1, replica_groups=mesh['y'=2,'core'=2,'zh'=2,'zl'=2,'x'=2] {'y','core','x','zl'}, dimensions={0} | all-to-all | bytes 1572864 | tf_op jit(solution)/shard_map/all_to_all | solution.py:96
  85.6 0.4 collective-permute-start.1
  86.1 5.6 %collective-permute-done.1 = f32[16,768]{1,0:T(8,128)S(1)} collective-permute-done((f32[16,768]{1,0:T(8,128)S(1)}, f32[16,768]{1,0:T(8,128)S(1)}, u32[]{:S(2)}, u32[]{:S(2)}) %collective-permute-start.1) | collective-permute-done | bytes 49184 | tf_op jit(solution)/shard_map/ppermute | solution.py:100
  91.7 0.1 multiply_reduce_fusion.1
  91.8 0.1 multiply_convert_fusion.1
  91.9 10.5 %all_to_all.21 = bf16[16,16,768]{2,1,0:T(8,128)(2,1)S(1)} all-to-all(bf16[16,16,768]{2,1,0:T(8,128)(2,1)S(1)} %broadcast_in_dim.76), channel_id=1, replica_groups=mesh['y'=2,'core'=2,'zh'=2,'zl'=2,'x'=2] {'y','core','x','zl'}, dimensions={0} | all-to-all | bytes 786432 | tf_op jit(solution)/shard_map/all_to_all | solution.py:102
  102.4 0.0 copy-done
  102.4 0.9 fusion.4
  103.3 0.7 copy.10
  (10 shorter events, 0.1 us)
Async XLA Ops:
  0.6 3.2 %copy-start.1 = (bf16[128,768]{1,0:T(8,128)(2,1)S(1)}, bf16[128,768]{1,0:T(8,128)(2,1)}, u32[]{:S(2)}) copy-start(bf16[128,768]{1,0:T(8,128)(2,1)} %param.5) | copy-start | bytes 589828
  6.4 30.3 %all-to-all-start = ((bf16[16,64,896]{2,1,0:T(8,128)(2,1)}), bf16[16,64,896]{2,1,0:T(8,128)(2,1)S(1)}, u32[]{:S(2)}, u32[]{:S(2)}) async-start(bf16[16,64,896]{2,1,0:T(8,128)(2,1)} %bitcast.18), calls=%async_computation | async-start | bytes 3670016 | tf_op jit(solution)/shard_map/all_to_all | solution.py:74
  36.7 30.4 %all-to-all-start.1 = ((bf16[16,64,768]{2,1,0:T(8,128)(2,1)}), bf16[16,64,768]{2,1,0:T(8,128)(2,1)S(1)}, u32[]{:S(2)}, u32[]{:S(2)}) async-start(bf16[16,64,768]{2,1,0:T(8,128)(2,1)} %bitcast.3), calls=%async_computation.1 | async-start | bytes 3145728 | tf_op jit(solution)/shard_map/all_to_all | solution.py:77
  40.9 26.8 %copy-start.2 = (s32[96]{0:T(128)S(1)}, s32[96]{0:T(128)}, u32[]{:S(2)}) copy-start(s32[96]{0:T(128)} %param.9) | copy-start | bytes 1156
  42.0 25.1 %collective-permute-start = (f32[96,768]{1,0:T(8,128)}, f32[96,768]{1,0:T(8,128)S(1)}, u32[]{:S(2)}, u32[]{:S(2)}) collective-permute-start(f32[96,768]{1,0:T(8,128)} %fusion.1), channel_id=1, source_target_pairs={{0,4},{4,0},{1,5},{5,1},{2,6},{6,2},{3,7},{7,3},{8,12},{12,8},{9,1... | collective-permute-start | bytes 884744 | tf_op jit(solution)/shard_map/ppermute | solution.py:86
  67.7 34.7 %copy-start = (bf16[96,768]{1,0:T(8,128)(2,1)}, bf16[96,768]{1,0:T(8,128)(2,1)S(1)}, u32[]{:S(2)}) copy-start(bf16[96,768]{1,0:T(8,128)(2,1)S(1)} %multiply_convert_fusion) | copy-start | bytes 442372
  85.6 6.0 %collective-permute-start.1 = (f32[16,768]{1,0:T(8,128)S(1)}, f32[16,768]{1,0:T(8,128)S(1)}, u32[]{:S(2)}, u32[]{:S(2)}) collective-permute-start(f32[16,768]{1,0:T(8,128)S(1)} %reduce_sum.38), channel_id=1, source_target_pairs={{0,4},{4,0},{1,5},{5,1},{2,6},{6,2},{3,7},{7,3},{8,12},{12,8},{9,1... | collective-permute-start | bytes 147464 | tf_op jit(solution)/shard_map/ppermute | solution.py:100

commit v26 on v19

--- a/solution.py
+++ b/solution.py
@@ -68,7 +68,7 @@
         ],
         axis=0,
     )
-    send_first = jnp.dot(chooser, table, preferred_element_type=f32).astype(bf16)
+    send_first = jnp.dot(chooser, table, preferred_element_type=bf16)
     pick = (second_doc[:, None] == jnp.arange(docs, dtype=jnp.int32)[None, :]).astype(bf16)
     send_second = jnp.dot(pick, doc_embed, preferred_element_type=f32).astype(bf16)
 
@@ -83,7 +83,7 @@
 
     label_ids = jnp.arange(owned, dtype=jnp.int32)
     first_hot = (label_ids[:, None] == first_slot[None, :]).astype(bf16)
-    mirror_part = jnp.dot(first_hot, got_first[:, :width], preferred_element_type=f32)
+    mirror_part = jnp.dot(first_hot, got_first, preferred_element_type=f32)[:, :width]
     mirrored = lax.ppermute(mirror_part, "zh", [(0, 1), (1, 0)])
     second_hot = (label_ids[:, None] == second_slot[None, :]).astype(bf16)
     own_part = jnp.dot(second_hot, got_second, preferred_element_type=f32)

time: 104 us -> 104 us (level)
  no operation moved by 1% of the time
where the time goes in v26:
time: 104 us
  waiting for transfers between devices  50.3 us (48%)
  blocking collectives  28.1 us (27%)
  starting transfers between devices  13 us (12%)
  matrix products  8.57 us (8%)
  other arithmetic  1.89 us (2%)
  local copies, waits for them, and re-layouts  1.24 us (1%)
    all_to_all x1, waiting for transfers between devices, local(): lax.all_to_all(send_second.reshape(group, capacity, width), near, split_a...  22.5 us
    all_to_all x1, waiting for transfers between devices, local(): lax.all_to_all(send_first.reshape(group, capacity, wide), near, split_axi...  22.2 us
    all_to_all x1, blocking collectives, local(): lax.all_to_all(partial_sums.reshape(group, share, width), near, split_axi...  17.6 us
    all_to_all x1, blocking collectives, local(): lax.all_to_all(jnp.broadcast_to(own[None], (group, share, width)), near,...  10.5 us
    all_to_all x1, starting transfers between devices, local(): lax.all_to_all(send_first.reshape(group, capacity, wide), near, split_axi...  6.31 us
    ppermute x1, waiting for transfers between devices, local(): sums = half_sums + lax.ppermute(half_sums, 'zh', [(0, 1), (1, 0)])  5.6 us
    all_to_all x1, starting transfers between devices, local(): lax.all_to_all(send_second.reshape(group, capacity, width), near, split_a...  3.71 us
    ppermute x1, starting transfers between devices, local(): mirrored = lax.ppermute(mirror_part, 'zh', [(0, 1), (1, 0)])  2.59 us
  transfers between devices with their start and end apart: 4, of which 3 were waited for; matrix products, arithmetic and copies ran while one was open for 3% of the time, Pallas kernels for 0%

profile of v26, /device:TPU:0, one launch (start us, length us, event | category | flops | bytes accessed | tf_op | source)
XLA Modules:
  0.0 104.0 jit_solution(3818561787320730580)
XLA Ops:
  0.6 0.0 copy-start.1
  0.7 1.2 %fusion.5 = f32[1024]{0:T(1024)S(1)} fusion(s32[1024]{0:T(1024)} %bitcast.21, s32[32]{0:T(128)S(1)} %fusion.34), kind=kOutput, calls=%fused_computation.9 | convolution fusion | flops 68353024 | bytes 8320 | tf_op jit(solution)/shard_map/dot_general | solution.py:41
  1.9 0.7 add_convert_fusion
  2.7 0.9 convolution_convert_fusion.1
  3.6 0.1 slice_add_fusion
  3.7 0.1 slice.30
  3.7 0.1 convert_element_type.73
  3.8 0.2 copy.11
  4.1 0.2 fusion.10
  4.3 0.0 copy-done.1
  4.3 2.0 %fusion.6 = bf16[1024,896]{1,0:T(8,128)(2,1)} fusion(bf16[1024,2]{1,0:T(8,128)(2,1)S(1)} %copy.11, bf16[1024,128]{1,0:T(8,128)(2,1)S(1)} %fusion.10, bf16[128,768]{1,0:T(8,128)(2,1)S(1)} %copy-done.1, bf16[2,896]{1,0:T(2,128)(2,1)S(1)} %pad_convert_fusion), kind=kOutput, calls=%fused_computation.11 | convolution fusion | flops 239782400 | bytes 2301440 | tf_op jit(solution)/shard_map/dot_general | solution.py:71
  6.2 6.3 %all-to-all-start = ((bf16[16,64,896]{2,1,0:T(8,128)(2,1)}), bf16[16,64,896]{2,1,0:T(8,128)(2,1)S(1)}, u32[]{:S(2)}, u32[]{:S(2)}) async-start(bf16[16,64,896]{2,1,0:T(8,128)(2,1)} %bitcast.19), calls=%async_computation | async-start | bytes 3670016 | tf_op jit(solution)/shard_map/all_to_all | solution.py:75
  12.6 0.1 slice.34
  12.6 1.8 %convolution_convert_fusion = bf16[1024,768]{1,0:T(8,128)(2,1)} fusion(bf16[128,768]{1,0:T(8,128)(2,1)S(1)} %copy-done.1, s32[1024]{0:T(1024)S(1)} %slice.34), kind=kOutput, calls=%fused_computation.2 | convolution fusion | flops 202244096 | bytes 1773568 | tf_op jit(solution)/shard_map/dot_general | solution.py:73
  14.4 22.2 %all-to-all-done = bf16[16,64,896]{2,1,0:T(8,128)(2,1)S(1)} async-done(((bf16[16,64,896]{2,1,0:T(8,128)(2,1)}), bf16[16,64,896]{2,1,0:T(8,128)(2,1)S(1)}, u32[]{:S(2)}, u32[]{:S(2)}) %all-to-all-start) | async-done | bytes 1835040 | tf_op jit(solution)/shard_map/all_to_all | solution.py:75
  36.6 3.7 %all-to-all-start.1 = ((bf16[16,64,768]{2,1,0:T(8,128)(2,1)}), bf16[16,64,768]{2,1,0:T(8,128)(2,1)S(1)}, u32[]{:S(2)}, u32[]{:S(2)}) async-start(bf16[16,64,768]{2,1,0:T(8,128)(2,1)} %bitcast.4), calls=%async_computation.1 | async-start | bytes 3145728 | tf_op jit(solution)/shard_map/all_to_all | solution.py:78
  40.3 0.4 add_reduce_fusion.1
  40.7 0.0 copy-start.2
  40.7 1.1 %fusion.1 = f32[96,768]{1,0:T(8,128)} fusion(bf16[1024,896]{1,0:T(8,128)(2,1)S(1)} %bitcast.18, s32[1024]{0:T(1024)S(1)} %get-tuple-element.4), kind=kOutput, calls=%fused_computation.3 | convolution fusion | flops 151093248 | bytes 1871872 | tf_op jit(solution)/shard_map/dot_general | solution.py:86
  41.9 2.6 %collective-permute-start = (f32[96,768]{1,0:T(8,128)}, f32[96,768]{1,0:T(8,128)S(1)}, u32[]{:S(2)}, u32[]{:S(2)}) collective-permute-start(f32[96,768]{1,0:T(8,128)} %fusion.1), channel_id=1, source_target_pairs={{0,4},{4,0},{1,5},{5,1},{2,6},{6,2},{3,7},{7,3},{8,12},{12,8},{9,1... | collective-permute-start | bytes 884744 | tf_op jit(solution)/shard_map/ppermute | solution.py:87
  44.4 22.5 %all-to-all-done.1 = bf16[16,64,768]{2,1,0:T(8,128)(2,1)S(1)} async-done(((bf16[16,64,768]{2,1,0:T(8,128)(2,1)}), bf16[16,64,768]{2,1,0:T(8,128)(2,1)S(1)}, u32[]{:S(2)}, u32[]{:S(2)}) %all-to-all-start.1) | async-done | bytes 1572896 | tf_op jit(solution)/shard_map/all_to_all | solution.py:78
  67.0 0.0 collective-permute-done
  67.0 0.5 multiply_reduce_fusion
  67.5 0.1 multiply_convert_fusion
  67.6 0.0 copy-done.2
  67.6 0.0 copy-start
  67.6 0.2 fusion.25
  67.8 17.6 %all_to_all.20 = f32[16,16,768]{2,1,0:T(8,128)S(1)} all-to-all(f32[16,16,768]{2,1,0:T(8,128)S(1)} %bitcast.16), channel_id=1, replica_groups=mesh['y'=2,'core'=2,'zh'=2,'zl'=2,'x'=2] {'y','core','x','zl'}, dimensions={0} | all-to-all | bytes 1572864 | tf_op jit(solution)/shard_map/all_to_all | solution.py:97
  85.5 0.4 collective-permute-start.1
  85.9 5.6 %collective-permute-done.1 = f32[16,768]{1,0:T(8,128)S(1)} collective-permute-done((f32[16,768]{1,0:T(8,128)S(1)}, f32[16,768]{1,0:T(8,128)S(1)}, u32[]{:S(2)}, u32[]{:S(2)}) %collective-permute-start.1) | collective-permute-done | bytes 49184 | tf_op jit(solution)/shard_map/ppermute | solution.py:101
  91.5 0.1 multiply_reduce_fusion.1
  91.7 0.1 multiply_convert_fusion.1
  91.8 10.5 %all_to_all.21 = bf16[16,16,768]{2,1,0:T(8,128)(2,1)S(1)} all-to-all(bf16[16,16,768]{2,1,0:T(8,128)(2,1)S(1)} %broadcast_in_dim.12), channel_id=1, replica_groups=mesh['y'=2,'core'=2,'zh'=2,'zl'=2,'x'=2] {'y','core','x','zl'}, dimensions={0} | all-to-all | bytes 786432 | tf_op jit(solution)/shard_map/all_to_all | solution.py:103
  102.3 0.0 copy-done
  102.3 0.9 fusion.4
  103.2 0.7 copy.13
  (10 shorter events, 0.2 us)
Async XLA Ops:
  0.6 3.6 %copy-start.1 = (bf16[128,768]{1,0:T(8,128)(2,1)S(1)}, bf16[128,768]{1,0:T(8,128)(2,1)}, u32[]{:S(2)}) copy-start(bf16[128,768]{1,0:T(8,128)(2,1)} %param.5) | copy-start | bytes 589828
  6.2 30.3 %all-to-all-start = ((bf16[16,64,896]{2,1,0:T(8,128)(2,1)}), bf16[16,64,896]{2,1,0:T(8,128)(2,1)S(1)}, u32[]{:S(2)}, u32[]{:S(2)}) async-start(bf16[16,64,896]{2,1,0:T(8,128)(2,1)} %bitcast.19), calls=%async_computation | async-start | bytes 3670016 | tf_op jit(solution)/shard_map/all_to_all | solution.py:75
  36.6 30.4 %all-to-all-start.1 = ((bf16[16,64,768]{2,1,0:T(8,128)(2,1)}), bf16[16,64,768]{2,1,0:T(8,128)(2,1)S(1)}, u32[]{:S(2)}, u32[]{:S(2)}) async-start(bf16[16,64,768]{2,1,0:T(8,128)(2,1)} %bitcast.4), calls=%async_computation.1 | async-start | bytes 3145728 | tf_op jit(solution)/shard_map/all_to_all | solution.py:78
  40.7 26.8 %copy-start.2 = (s32[96]{0:T(128)S(1)}, s32[96]{0:T(128)}, u32[]{:S(2)}) copy-start(s32[96]{0:T(128)} %param.9) | copy-start | bytes 1156
  41.9 25.1 %collective-permute-start = (f32[96,768]{1,0:T(8,128)}, f32[96,768]{1,0:T(8,128)S(1)}, u32[]{:S(2)}, u32[]{:S(2)}) collective-permute-start(f32[96,768]{1,0:T(8,128)} %fusion.1), channel_id=1, source_target_pairs={{0,4},{4,0},{1,5},{5,1},{2,6},{6,2},{3,7},{7,3},{8,12},{12,8},{9,1... | collective-permute-start | bytes 884744 | tf_op jit(solution)/shard_map/ppermute | solution.py:87
  67.6 34.7 %copy-start = (bf16[96,768]{1,0:T(8,128)(2,1)}, bf16[96,768]{1,0:T(8,128)(2,1)S(1)}, u32[]{:S(2)}) copy-start(bf16[96,768]{1,0:T(8,128)(2,1)S(1)} %multiply_convert_fusion) | copy-start | bytes 442372
  85.5 6.0 %collective-permute-start.1 = (f32[16,768]{1,0:T(8,128)S(1)}, f32[16,768]{1,0:T(8,128)S(1)}, u32[]{:S(2)}, u32[]{:S(2)}) collective-permute-start(f32[16,768]{1,0:T(8,128)S(1)} %reduce_sum.38), channel_id=1, source_target_pairs={{0,4},{4,0},{1,5},{5,1},{2,6},{6,2},{3,7},{7,3},{8,12},{12,8},{9,1... | collective-permute-start | bytes 147464 | tf_op jit(solution)/shard_map/ppermute | solution.py:101

commit v27 on v17

--- a/solution.py
+++ b/solution.py
@@ -72,16 +72,17 @@
     got_first = lax.all_to_all(
         send_first.reshape(group, capacity, wide), near, split_axis=0, concat_axis=0, tiled=True
     ).reshape(group * capacity, wide)
-    got_second = lax.all_to_all(
-        send_second.reshape(group, capacity, width), near, split_axis=0, concat_axis=0, tiled=True
-    ).reshape(group * capacity, width)
     first_slot = got_first[:, width].astype(jnp.int32) - 1
     second_slot = got_first[:, width + 1].astype(jnp.int32) - 1
 
     label_ids = jnp.arange(owned, dtype=jnp.int32)
     first_hot = (label_ids[:, None] == first_slot[None, :]).astype(bf16)
     mirror_part = jnp.dot(first_hot, got_first, preferred_element_type=f32)[:, :width]
+    send_second, mirror_part = lax.optimization_barrier((send_second, mirror_part))
     mirrored = lax.ppermute(mirror_part, "zh", [(0, 1), (1, 0)])
+    got_second = lax.all_to_all(
+        send_second.reshape(group, capacity, width), near, split_axis=0, concat_axis=0, tiled=True
+    ).reshape(group * capacity, width)
     second_hot = (label_ids[:, None] == second_slot[None, :]).astype(bf16)
     own_part = jnp.dot(second_hot, got_second, preferred_element_type=f32)
     label_sums = own_part + mirrored

time: 104 us -> 105 us (level)
  waiting for transfers between devices: 50.3 us -> 51.8 us
    ppermute x1, waiting for transfers between devices: 0.01 us -> 22.4 us  [local(): mirrored = lax.ppermute(mirror_part, 'zh', [(0, 1), (1, 0)])]
    all_to_all x1, waiting for transfers between devices: 22.5 us -> 1.53 us  [local(): lax.all_to_all(send_second.reshape(group, capacity, width), near, split_a...]
  transfers between devices with their start and end apart: 4 -> 4, of which waited for: 3 -> 4; matrix products, arithmetic and copies ran while one was open for 3% -> 2% of each run, Pallas kernels for 0% -> 0%
where the time goes in v27:
time: 105 us
  waiting for transfers between devices  51.8 us (49%)
  blocking collectives  28.2 us (27%)
  starting transfers between devices  13.1 us (12%)
  matrix products  8.07 us (8%)
  other arithmetic  1.67 us (2%)
  local copies, waits for them, and re-layouts  1.08 us (1%)
    ppermute x1, waiting for transfers between devices, local(): mirrored = lax.ppermute(mirror_part, 'zh', [(0, 1), (1, 0)])  22.4 us
    all_to_all x1, waiting for transfers between devices, local(): lax.all_to_all(send_first.reshape(group, capacity, wide), near, split_axi...  22.2 us
    all_to_all x1, blocking collectives, local(): lax.all_to_all(partial_sums.reshape(group, share, width), near, split_axi...  17.6 us
    all_to_all x1, blocking collectives, local(): lax.all_to_all(jnp.broadcast_to(own[None], (group, share, width)), near,...  10.5 us
    all_to_all x1, starting transfers between devices, local(): lax.all_to_all(send_first.reshape(group, capacity, wide), near, split_axi...  6.32 us
    ppermute x1, waiting for transfers between devices, local(): sums = half_sums + lax.ppermute(half_sums, 'zh', [(0, 1), (1, 0)])  5.64 us
    all_to_all x1, starting transfers between devices, local(): lax.all_to_all(send_second.reshape(group, capacity, width), near, split_a...  3.72 us
    ppermute x1, starting transfers between devices, local(): mirrored = lax.ppermute(mirror_part, 'zh', [(0, 1), (1, 0)])  2.65 us
  transfers between devices with their start and end apart: 4, of which 4 were waited for; matrix products, arithmetic and copies ran while one was open for 2% of the time, Pallas kernels for 0%

profile of v27, /device:TPU:0, one launch (start us, length us, event | category | flops | bytes accessed | tf_op | source)
XLA Modules:
  0.0 104.6 jit_solution(17713512101640520800)
XLA Ops:
  0.6 0.0 copy-start.1
  0.7 1.2 %fusion.5 = f32[1024]{0:T(1024)S(1)} fusion(s32[1024]{0:T(1024)} %bitcast.19, s32[32]{0:T(128)S(1)} %fusion.24), kind=kOutput, calls=%fused_computation.10 | convolution fusion | flops 68353024 | bytes 8320 | tf_op jit(solution)/shard_map/dot_general | solution.py:41
  1.9 0.7 add_convert_fusion.1
  2.7 0.9 convolution_convert_fusion.1
  3.6 0.1 slice_convert_fusion
  3.7 0.1 slice.43
  3.7 0.1 slice.46
  3.8 0.1 slice.48
  3.9 0.0 copy-done.1
  3.9 2.2 %add_convert_fusion = bf16[1024,896]{1,0:T(8,128)(2,1)} fusion(f32[1024]{0:T(1024)S(1)} %slice.48, f32[1024]{0:T(1024)S(1)} %slice.46, pred[896]{0:T(1024)(128)(4,1)S(1)} %get-tuple-element.23, pred[896]{0:T(1024)(128)(4,1)S(1)} %get-tuple-element.24, s32[1024]{0:T(1024)S(1)} %slice.43, bf16[128,768]{1,0:T(8,128)(2,1)S(1)} %copy-done.1), kind=kOutput, calls=%fused_computation.2 | convolution fusion | flops 238682112 | bytes 2045696 | tf_op jit(solution)/shard_map/dot_general | solution.py:68
  6.1 6.3 %all-to-all-start = ((bf16[16,64,896]{2,1,0:T(8,128)(2,1)}), bf16[16,64,896]{2,1,0:T(8,128)(2,1)S(1)}, u32[]{:S(2)}, u32[]{:S(2)}) async-start(bf16[16,64,896]{2,1,0:T(8,128)(2,1)} %bitcast.18), calls=%async_computation | async-start | bytes 3670016 | tf_op jit(solution)/shard_map/all_to_all | solution.py:72
  12.4 0.1 slice.51
  12.4 1.8 %convolution_convert_fusion = bf16[1024,768]{1,0:T(8,128)(2,1)} fusion(bf16[128,768]{1,0:T(8,128)(2,1)S(1)} %copy-done.1, s32[1024]{0:T(1024)S(1)} %slice.51), kind=kOutput, calls=%fused_computation.3 | convolution fusion | flops 202244096 | bytes 1773568 | tf_op jit(solution)/shard_map/dot_general | solution.py:70
  14.2 22.2 %all-to-all-done = bf16[16,64,896]{2,1,0:T(8,128)(2,1)S(1)} async-done(((bf16[16,64,896]{2,1,0:T(8,128)(2,1)}), bf16[16,64,896]{2,1,0:T(8,128)(2,1)S(1)}, u32[]{:S(2)}, u32[]{:S(2)}) %all-to-all-start) | async-done | bytes 1835040 | tf_op jit(solution)/shard_map/all_to_all | solution.py:72
  36.4 0.4 add_reduce_fusion.1
  36.8 0.4 fusion.1
  37.2 3.7 %all-to-all-start.1 = ((bf16[16,64,768]{2,1,0:T(8,128)(2,1)}), bf16[16,64,768]{2,1,0:T(8,128)(2,1)S(1)}, u32[]{:S(2)}, u32[]{:S(2)}) async-start(bf16[16,64,768]{2,1,0:T(8,128)(2,1)} %bitcast.3), calls=%async_computation.1 | async-start | bytes 3145728 | tf_op jit(solution)/shard_map/all_to_all | solution.py:83
  41.0 0.0 copy-start.2
  41.0 2.7 %collective-permute-start = (f32[96,768]{1,0:T(8,128)S(1)}, f32[96,768]{1,0:T(8,128)S(1)}, u32[]{:S(2)}, u32[]{:S(2)}) collective-permute-start(f32[96,768]{1,0:T(8,128)S(1)} %fusion.1), channel_id=1, source_target_pairs={{0,4},{4,0},{1,5},{5,1},{2,6},{6,2},{3,7},{7,3},{8,12},{12,8},{9,1... | collective-permute-start | bytes 884744 | tf_op jit(solution)/shard_map/ppermute | solution.py:82
  43.6 22.4 %collective-permute-done = f32[96,768]{1,0:T(8,128)S(1)} collective-permute-done((f32[96,768]{1,0:T(8,128)S(1)}, f32[96,768]{1,0:T(8,128)S(1)}, u32[]{:S(2)}, u32[]{:S(2)}) %collective-permute-start) | collective-permute-done | bytes 294944 | tf_op jit(solution)/shard_map/ppermute | solution.py:82
  66.1 1.5 %all-to-all-done.1 = bf16[16,64,768]{2,1,0:T(8,128)(2,1)S(1)} async-done(((bf16[16,64,768]{2,1,0:T(8,128)(2,1)}), bf16[16,64,768]{2,1,0:T(8,128)(2,1)S(1)}, u32[]{:S(2)}, u32[]{:S(2)}) %all-to-all-start.1) | async-done | bytes 1572896 | tf_op jit(solution)/shard_map/all_to_all | solution.py:83
  67.6 0.5 multiply_reduce_fusion
  68.1 0.1 multiply_convert_fusion
  68.2 0.0 copy-done.2
  68.2 0.0 copy-start
  68.2 0.2 fusion.16
  68.5 17.6 %all_to_all.20 = f32[16,16,768]{2,1,0:T(8,128)S(1)} all-to-all(f32[16,16,768]{2,1,0:T(8,128)S(1)} %bitcast.15), channel_id=1, replica_groups=mesh['y'=2,'core'=2,'zh'=2,'zl'=2,'x'=2] {'y','core','x','zl'}, dimensions={0} | all-to-all | bytes 1572864 | tf_op jit(solution)/shard_map/all_to_all | solution.py:95
  86.2 0.4 collective-permute-start.1
  86.5 5.6 %collective-permute-done.1 = f32[16,768]{1,0:T(8,128)S(1)} collective-permute-done((f32[16,768]{1,0:T(8,128)S(1)}, f32[16,768]{1,0:T(8,128)S(1)}, u32[]{:S(2)}, u32[]{:S(2)}) %collective-permute-start.1) | collective-permute-done | bytes 49184 | tf_op jit(solution)/shard_map/ppermute | solution.py:99
  92.2 0.1 multiply_reduce_fusion.1
  92.3 0.1 multiply_convert_fusion.1
  92.4 10.5 %all_to_all.21 = bf16[16,16,768]{2,1,0:T(8,128)(2,1)S(1)} all-to-all(bf16[16,16,768]{2,1,0:T(8,128)(2,1)S(1)} %broadcast_in_dim.76), channel_id=1, replica_groups=mesh['y'=2,'core'=2,'zh'=2,'zl'=2,'x'=2] {'y','core','x','zl'}, dimensions={0} | all-to-all | bytes 786432 | tf_op jit(solution)/shard_map/all_to_all | solution.py:101
  103.0 0.0 copy-done
  103.0 0.9 fusion.4
  103.9 0.7 copy.10
  (10 shorter events, 0.2 us)
Async XLA Ops:
  0.6 3.3 %copy-start.1 = (bf16[128,768]{1,0:T(8,128)(2,1)S(1)}, bf16[128,768]{1,0:T(8,128)(2,1)}, u32[]{:S(2)}) copy-start(bf16[128,768]{1,0:T(8,128)(2,1)} %param.5) | copy-start | bytes 589828
  6.1 30.3 %all-to-all-start = ((bf16[16,64,896]{2,1,0:T(8,128)(2,1)}), bf16[16,64,896]{2,1,0:T(8,128)(2,1)S(1)}, u32[]{:S(2)}, u32[]{:S(2)}) async-start(bf16[16,64,896]{2,1,0:T(8,128)(2,1)} %bitcast.18), calls=%async_computation | async-start | bytes 3670016 | tf_op jit(solution)/shard_map/all_to_all | solution.py:72
  37.2 30.4 %all-to-all-start.1 = ((bf16[16,64,768]{2,1,0:T(8,128)(2,1)}), bf16[16,64,768]{2,1,0:T(8,128)(2,1)S(1)}, u32[]{:S(2)}, u32[]{:S(2)}) async-start(bf16[16,64,768]{2,1,0:T(8,128)(2,1)} %bitcast.3), calls=%async_computation.1 | async-start | bytes 3145728 | tf_op jit(solution)/shard_map/all_to_all | solution.py:83
  41.0 27.2 %copy-start.2 = (s32[96]{0:T(128)S(1)}, s32[96]{0:T(128)}, u32[]{:S(2)}) copy-start(s32[96]{0:T(128)} %param.9) | copy-start | bytes 1156
  41.0 25.1 %collective-permute-start = (f32[96,768]{1,0:T(8,128)S(1)}, f32[96,768]{1,0:T(8,128)S(1)}, u32[]{:S(2)}, u32[]{:S(2)}) collective-permute-start(f32[96,768]{1,0:T(8,128)S(1)} %fusion.1), channel_id=1, source_target_pairs={{0,4},{4,0},{1,5},{5,1},{2,6},{6,2},{3,7},{7,3},{8,12},{12,8},{9,1... | collective-permute-start | bytes 884744 | tf_op jit(solution)/shard_map/ppermute | solution.py:82
  68.2 34.8 %copy-start = (bf16[96,768]{1,0:T(8,128)(2,1)}, bf16[96,768]{1,0:T(8,128)(2,1)S(1)}, u32[]{:S(2)}) copy-start(bf16[96,768]{1,0:T(8,128)(2,1)S(1)} %multiply_convert_fusion) | copy-start | bytes 442372
  86.2 6.0 %collective-permute-start.1 = (f32[16,768]{1,0:T(8,128)S(1)}, f32[16,768]{1,0:T(8,128)S(1)}, u32[]{:S(2)}, u32[]{:S(2)}) collective-permute-start(f32[16,768]{1,0:T(8,128)S(1)} %reduce_sum.38), channel_id=1, source_target_pairs={{0,4},{4,0},{1,5},{5,1},{2,6},{6,2},{3,7},{7,3},{8,12},{12,8},{9,1... | collective-permute-start | bytes 147464 | tf_op jit(solution)/shard_map/ppermute | solution.py:99
